TPU v7x, 256 devices: a whole 4x4x8 slice. The times are simulated.
256 devices in a mesh: seq: 64 (over z_hi, y, x, core), tp: 4 (over z_lo).
Axes of the slice: x: 4, y: 4, z: 8 (z_hi: 2, z_lo: 4; z = z_hi * 4 + z_lo), core: 2. Of those that a mesh axis runs over, the one named last changes fastest.
Arguments:
- residual: bfloat16 [32768, 2048], P('seq', 'tp'), may hold values from -6 to 6
- norm_gain: float32 [2048], replicated, may hold values from 0.3 to 3
- query_weight: bfloat16 [2048, 1024], P(None, 'tp'), as said below
- key_weight: bfloat16 [2048, 1024], P(None, 'tp'), as said below
- value_weight: bfloat16 [2048, 1024], P(None, 'tp'), may hold values from -0.375 to 0.375
- out_weight: bfloat16 [1024, 2048], P('tp'), may hold values from -0.1875 to 0.1875
- segment_start: int32 [32768], P('seq'), may hold values from 0 to 32640, as said below
- token_valid: int32 [32768], P('seq'), may hold values from 0 to 1, as said below
- page_slot: int32 [256], P('seq'), may hold values from 4 to 511, as said below
Outputs:
- hidden: bfloat16 [32768, 2048], P('seq', 'tp')
- cache: bfloat16 [512, 128, 2048], P('seq', None, 'tp')
Inputs may be any that keep to these rules, and one draw needn't show every extreme that they name: `segment_start`: prompts start at multiples of 128 and are contiguous; each holds at most 8192 tokens and one holds exactly 8192. `token_valid`: zeros form a tail of the last page of a prompt; the first token of every prompt is 1. No two pages share a cache page; page_slot // 8 is the device that holds the page's tokens, or the next device when that one holds tokens of the same prompt. `query_weight`: independent entries whose scale falls as the inverse square root of 2048. `key_weight`: independent entries whose scale falls as the inverse square root of 2048.
All inputs are finite; a program needn't handle non-finite values.
Results may differ from a plain program's by a relative error of at most 0.02.
The roundings to bfloat16 on the way count: a program that leaves them out, or rounds other values in their place, can miss the bound.
Values may be sent and summed in bfloat16 or wider, within the bound.
No kernel may reach another device: no remote copies, remote signals or barrier semaphores. Data moves between devices by JAX's collectives and lax.ppermute only.
A program may use at most 128 MiB of HBM per device.

v0:
```python
import jax
import jax.numpy as jnp
from jax import lax
from jax.experimental import pallas as pl
from jax.experimental.pallas import tpu as pltpu
from jax.sharding import PartitionSpec as P

HD = 64
PAGE = 128
SPAN = 16


THETA = 130000.0
EPS = 1e-05
SCALE = HD ** (-0.5)
FAR = 1 << 30


def _step_kernel(step_ref, meta_ref, valid_ref, seg_ref, q_ref, kv_a_ref, kv_b_ref, s_ref, out_ref):
    rows, width = out_ref.shape
    keys = kv_a_ref.shape[0]
    step = step_ref[0]
    qstart = meta_ref[0]
    check_valid = jnp.where(step == 0, meta_ref[1], 0)
    seg_last = meta_ref[2]
    kstart = qstart - step * keys
    seg_first = seg_ref[0, 0]
    none_allowed = kstart + keys - 1 < seg_first
    all_allowed = (seg_last <= kstart) & (kstart + keys - 1 <= qstart) & (check_valid == 0)
    first_half = pl.program_id(0) < 2

    def update(allowed):
        q = q_ref[...]
        kv = jnp.where(first_half, kv_a_ref[...], kv_b_ref[...])
        scores = lax.dot_general(
            q, kv[:, :HD], (((1,), (1,)), ((), ())), preferred_element_type=jnp.float32
        ) * SCALE
        state = s_ref[...]
        m_old = state[:, 0:1]
        l_old = state[:, 1:2]
        if allowed is None:
            block_max = jnp.max(scores, axis=1, keepdims=True)
        else:
            block_max = jnp.max(jnp.where(allowed, scores, -1e30), axis=1, keepdims=True)
        m_new = jnp.maximum(m_old, block_max)
        weights = jnp.exp(scores - m_new)
        if allowed is not None:
            weights = jnp.where(allowed, weights, 0.0)
        shrink = jnp.exp(m_old - m_new)
        l_new = l_old * shrink + jnp.sum(weights, axis=1, keepdims=True)
        pv = jnp.dot(weights.astype(jnp.bfloat16), kv, preferred_element_type=jnp.float32)
        lane = lax.broadcasted_iota(jnp.int32, (rows, width), 1)
        acc = state * shrink + pv
        out_ref[...] = jnp.where(
            lane >= HD, acc, jnp.where(lane == 0, m_new, jnp.where(lane == 1, l_new, 0.0))
        )

    @pl.when(none_allowed)
    def _():
        out_ref[...] = s_ref[...]

    @pl.when(all_allowed & jnp.logical_not(none_allowed))
    def _():
        update(None)

    @pl.when(jnp.logical_not(all_allowed) & jnp.logical_not(none_allowed))
    def _():
        kpos = kstart + lax.broadcasted_iota(jnp.int32, (1, keys), 1)
        kpos = jnp.where((valid_ref[...] > 0) | (check_valid == 0), kpos, FAR)
        tpos = qstart + lax.broadcasted_iota(jnp.int32, (rows, 1), 0)
        update((kpos >= seg_ref[...]) & (kpos <= tpos))


def attend_step(step, meta, valid_row, seg_col, q_hm, kv_a, kv_b, state):
    heads, rows, _ = q_hm.shape
    part = kv_a.shape[0]
    keys = kv_a.shape[1]
    width = kv_a.shape[2]
    grid_spec = pltpu.PrefetchScalarGridSpec(
        num_scalar_prefetch=2,
        grid=(heads,),
        in_specs=[
            pl.BlockSpec((1, keys), lambda h, s, m: (0, 0)),
            pl.BlockSpec((rows, 1), lambda h, s, m: (0, 0)),
            pl.BlockSpec((None, rows, HD), lambda h, s, m: (h, 0, 0)),
            pl.BlockSpec((None, keys, width), lambda h, s, m: (h % part, 0, 0)),
            pl.BlockSpec((None, keys, width), lambda h, s, m: (h % part, 0, 0)),
            pl.BlockSpec((None, rows, width), lambda h, s, m: (h, 0, 0)),
        ],
        out_specs=pl.BlockSpec((None, rows, width), lambda h, s, m: (h, 0, 0)),
    )
    flops = heads * rows * keys * (2 * HD + 2 * width)
    return pl.pallas_call(
        _step_kernel,
        grid_spec=grid_spec,
        out_shape=jax.ShapeDtypeStruct(state.shape, jnp.float32),
        input_output_aliases={7: 0},
        cost_estimate=pl.CostEstimate(
            flops=flops,
            transcendentals=heads * rows * keys,
            bytes_accessed=q_hm.size * 2 + 2 * (kv_a.size + kv_b.size) * 2 + state.size * 8,
        ),
    )(step, meta, valid_row, seg_col, q_hm, kv_a, kv_b, state)


def passed_along(x, axis, by):
    count = lax.axis_size(axis)
    pairs = [(i, i + by) for i in range(count) if 0 <= i + by < count]
    return lax.ppermute(x, axis, pairs)


def rotate(inputs, positions):
    half_dim = inputs.shape[-1] // 2
    frequency = THETA ** (-2.0 * jnp.arange(half_dim, dtype=jnp.float32) / inputs.shape[-1])
    angles = positions.astype(jnp.float32)[:, None] * frequency[None, :]
    cosine = jnp.cos(angles)[:, None, :]
    sine_part = jnp.sin(angles)[:, None, :]
    front_half = inputs[..., :half_dim]
    back_half = inputs[..., half_dim:]
    return jnp.concatenate(
        [front_half * cosine - back_half * sine_part, back_half * cosine + front_half * sine_part],
        axis=-1,
    )


def body(
    residual,
    norm_gain,
    query_weight,
    key_weight,
    value_weight,
    out_weight,
    segment_start,
    token_valid,
    page_slot,
):
    row_count = residual.shape[0]
    local_heads = query_weight.shape[1] // HD
    seq_rank = lax.axis_index("seq")
    seq_count = lax.axis_size("seq")
    reach_dev = min(SPAN, seq_count // 2)
    half = seq_count // 2
    chain = [(i, i + 1) for i in range(seq_count - 1)]
    inner = [p for p in chain if p != (half - 1, half)]
    first_block = segment_start[0] // row_count
    cross_here = jnp.clip(seq_rank - first_block, 0, reach_dev).astype(jnp.int32)
    told = jnp.broadcast_to(jnp.where(seq_rank == half, cross_here, 0), (seq_count,))
    cross_steps = jnp.sum(lax.all_to_all(told, "seq", 0, 0, tiled=True))
    cross_steps = jnp.maximum(cross_steps, 1)
    gathered = lax.all_gather(residual, "tp", axis=1, tiled=True)
    widened = gathered.astype(jnp.float32)
    mean_sq = jnp.mean(widened * widened, axis=1, keepdims=True)
    normed = (widened * lax.rsqrt(mean_sq + EPS) * norm_gain[None, :]).astype(jnp.bfloat16)
    seq_rank = lax.axis_index("seq")
    first_row = seq_rank * row_count
    places = first_row + jnp.arange(row_count, dtype=jnp.int32)
    offsets = places - segment_start
    queries = jnp.dot(normed, query_weight, preferred_element_type=jnp.float32).reshape(
        row_count, local_heads, HD
    )
    queries = rotate(queries, offsets).astype(jnp.bfloat16)
    key_rot = jnp.dot(normed, key_weight, preferred_element_type=jnp.float32).reshape(
        row_count, local_heads, HD
    )
    key_rot = rotate(key_rot, offsets).astype(jnp.bfloat16)
    values = (
        jnp.dot(normed, value_weight, preferred_element_type=jnp.float32)
        .reshape(row_count, local_heads, HD)
        .astype(jnp.bfloat16)
    )
    packed = jnp.concatenate([key_rot[:, :, None, :], values[:, :, None, :]], axis=2).reshape(
        row_count, local_heads * 2 * HD
    )
    packed = jnp.where(token_valid[:, None] > 0, packed, jnp.zeros_like(packed))

    out_cols = lax.all_to_all(out_weight, "tp", 1, 0, tiled=True)
    prev_slot = passed_along(page_slot, "seq", 1)

    q_hm = jnp.transpose(queries, (1, 0, 2))
    kv_hm = jnp.transpose(packed.reshape(row_count, local_heads, 2 * HD), (1, 0, 2))
    seg_col = segment_start[:, None]
    valid_row = token_valid[None, :]
    seg_last = segment_start[row_count - 1]

    meta = jnp.stack([first_row, 1, seg_last]).astype(jnp.int32)
    split = local_heads // 2

    def absorb(state, incoming, step):
        step_arr = jnp.asarray(step, jnp.int32).reshape(1)
        return attend_step(step_arr, meta, valid_row, seg_col, q_hm, incoming[0], incoming[1], state)

    lane = jnp.arange(2 * HD, dtype=jnp.int32)
    initial = jnp.broadcast_to(
        jnp.where(lane == 0, -1e30, 0.0).astype(jnp.float32), (local_heads, row_count, 2 * HD)
    )

    own = (kv_hm[:split], kv_hm[split:])
    prev_block = tuple(lax.ppermute(part, "seq", chain) for part in own)
    carried = absorb(initial, own, 0)

    def step_with(pairs):
        def advance(step_index, carry_in):
            held, state = carry_in
            sent = tuple(lax.ppermute(part, "seq", pairs) for part in held)
            state = absorb(state, held, step_index)
            return (sent, state)

        return advance

    held, carried = lax.fori_loop(1, cross_steps, step_with(chain), (prev_block, carried))
    held, carried = lax.fori_loop(cross_steps, reach_dev, step_with(inner), (held, carried))
    carried = absorb(carried, held, reach_dev)
    attended = (
        jnp.transpose(carried[:, :, HD:] / carried[:, :, 1:2], (1, 0, 2))
        .astype(jnp.bfloat16)
        .reshape(row_count, local_heads * HD)
    )

    tiles = page_slot.shape[0]
    slot_count = 2 * tiles
    base_slot = seq_rank * slot_count
    has_prev = seq_rank > 0
    cand_slot = jnp.concatenate([page_slot, jnp.where(has_prev, prev_slot, -1)]) - base_slot
    cand_pages = jnp.concatenate(
        [packed.reshape(tiles, PAGE, -1), jnp.transpose(jnp.concatenate(prev_block, axis=0), (1, 0, 2)).reshape(tiles, PAGE, -1)],
        axis=0,
    )
    match = cand_slot[None, :] == jnp.arange(slot_count, dtype=jnp.int32)[:, None]
    pick = jnp.argmax(match.astype(jnp.int32), axis=1)
    found = jnp.any(match, axis=1)
    cache_pages = jnp.where(found[:, None, None], cand_pages[pick], jnp.zeros_like(cand_pages[:1]))

    attended_all = lax.all_gather(attended, "tp", axis=1, tiled=True)
    projected = jnp.dot(attended_all, out_cols, preferred_element_type=jnp.float32)
    hidden = (residual.astype(jnp.float32) + projected).astype(jnp.bfloat16)
    return (hidden, cache_pages)


def solution(mesh):
    return jax.shard_map(
        body,
        mesh=mesh,
        in_specs=(
            P("seq", "tp"),
            P(),
            P(None, "tp"),
            P(None, "tp"),
            P(None, "tp"),
            P("tp", None),
            P("seq"),
            P("seq"),
            P("seq"),
        ),
        out_specs=(P("seq", "tp"), P("seq", None, "tp")),
        check_vma=False,
    )
```

profile of v0, /device:TPU:24, one launch (start us, length us, event | category | flops | bytes accessed | tf_op | source)
XLA Modules:
  0.0 385.9 jit_solution(15553166374796864255)
XLA Ops:
  7.9 1.9 collective-permute-start.6
  14.4 15.3 %all-to-all-start = ((s32[64,1,1]{2,1,0:T(1,128)}), s32[64,1,1]{2,1,0:T(1,128)S(1)}, u32[]{:S(2)}, u32[]{:S(2)}) async-start(s32[64,1,1]{2,1,0:T(1,128)} %broadcast_in_dim.79), calls=%async_computation | async-start | bytes 65536 | tf_op jit(solution)/shard_map/all_to_all | solution.py:148
  30.6 2.3 copy.77
  35.5 27.8 %all-gather.3.cloned.1.call-done = bf16[512,2048]{1,0:T(8,128)(2,1)} async-done(((bf16[512,512]{1,0:T(8,128)(2,1)}), bf16[512,2048]{1,0:T(8,128)(2,1)}) %all-gather.3.cloned.1.call-update) | async-done | bytes 2097168 | tf_op jit(solution)/shard_map/all_gather | solution.py:150
  63.2 2.2 fusion
  67.1 2.0 copy.69
  69.1 2.2 fusion.10
  75.5 2.3 copy.85
  77.8 2.3 copy.87
  80.0 3.3 fusion.5
  85.4 2.0 collective-permute-start.5
  87.4 3.5 collective-permute-start.4
  90.9 4.3 %all-to-all-start.1 = ((bf16[256,4,512]{0,2,1:T(8,128)(2,1)}), bf16[256,4,512]{0,2,1:T(8,128)(2,1)}, u32[]{:S(2)}, u32[]{:S(2)}) async-start(bf16[256,4,512]{0,2,1:T(8,128)(2,1)} %bitcast.16), calls=%async_computation.1 | async-start | bytes 2097152 | tf_op jit(solution)/shard_map/all_to_all | solution.py:176
  97.0 9.3 %shard_map.104 = f32[4,512,128]{2,1,0:T(8,128)S(1)} custom-call(s32[1]{0:T(128)} %constant.69.clone.1.step_ref, s32[3]{0:T(128)S(1)} %pad_add_fusion.meta_ref, s32[1,512]{1,0:T(1,128)S(1)} %bitcast.42, s32[512,1]{1,0:T(8,128)S(1)} %copy.75.seg_ref, bf16[4,512,64]{2,1,0:T(8,128)(2,1)S(1)} %maximum_bitcast_fusion.q_ref, ...), custom_call_target="tpu_custom_call", output_to_operand_aliasing={{}: (7, {})} | custom-call | flops 402653184 | bytes 3407872 | tf_op jit(solution)/shard_map/pallas_call | solution.py:93
  108.2 223.2 %while.29 = (s32[]{:T(128)}, bf16[2,512,128]{2,1,0:T(8,128)(2,1)S(1)}, bf16[2,512,128]{2,1,0:T(8,128)(2,1)S(1)}, f32[4,512,128]{2,1,0:T(8,128)S(1)}, s32[3]{0:T(...) while((s32[]{:T(128)}, ...), condition=%wide.region_5.6_spmd, body=%wide.region_4.5_spmd.sunk | while | flops 402653184 | bytes 6553781 | solution.py:211
  111.5 3.5 collective-permute-start.3
  115.0 8.9 %body.5 = f32[4,512,128]{2,1,0:T(8,128)S(1)} custom-call(s32[1]{0:T(128)} %bitcast.36.step_ref, s32[3]{0:T(128)S(1)} %get-tuple-element.379.meta_ref, s32[1,512]{1,0:T(1,128)S(1)} %get-tuple-element.380.valid_ref, s32[512,1]{1,0:T(8,128)S(1)} %get-tuple-element.381.seg_ref, ...), custom_call_target="tpu_custom_call", output_to_operand_aliasing={{}: (7, {})} | custom-call | flops 402653184 | bytes 3407872 | tf_op jit(solution)/shard_map/while/body/pallas_call | solution.py:93
  124.6 1.9 collective-permute-start.2
  127.3 3.2 collective-permute-start.3
  130.5 8.9 %body.5 = f32[4,512,128]{2,1,0:T(8,128)S(1)} custom-call(s32[1]{0:T(128)} %bitcast.36.step_ref, s32[3]{0:T(128)S(1)} %get-tuple-element.379.meta_ref, s32[1,512]{1,0:T(1,128)S(1)} %get-tuple-element.380.valid_ref, s32[512,1]{1,0:T(8,128)S(1)} %get-tuple-element.381.seg_ref, ...), custom_call_target="tpu_custom_call", output_to_operand_aliasing={{}: (7, {})} | custom-call | flops 402653184 | bytes 3407872 | tf_op jit(solution)/shard_map/while/body/pallas_call | solution.py:93
  140.1 1.9 collective-permute-start.2
  142.7 6.4 %collective-permute-start.3 = (bf16[2,512,128]{2,1,0:T(8,128)(2,1)}, bf16[2,512,128]{2,1,0:T(8,128)(2,1)S(1)}, u32[]{:S(2)}, u32[]{:S(2)}) collective-permute-start(bf16[2,512,128]{2,1,0:T(8,128)(2,1)} %copy.110.kv_b_ref), channel_id=1, source_target_pairs={{0,4},{4,8},{8,12},{12,16},{16,20},{20,24},{24,28},{28,32},{32,36}... | collective-permute-start | bytes 786440 | tf_op jit(solution)/shard_map/while/body/ppermute | solution.py:204
  149.1 8.9 %body.5 = f32[4,512,128]{2,1,0:T(8,128)S(1)} custom-call(s32[1]{0:T(128)} %bitcast.36.step_ref, s32[3]{0:T(128)S(1)} %get-tuple-element.379.meta_ref, s32[1,512]{1,0:T(1,128)S(1)} %get-tuple-element.380.valid_ref, s32[512,1]{1,0:T(8,128)S(1)} %get-tuple-element.381.seg_ref, ...), custom_call_target="tpu_custom_call", output_to_operand_aliasing={{}: (7, {})} | custom-call | flops 402653184 | bytes 3407872 | tf_op jit(solution)/shard_map/while/body/pallas_call | solution.py:93
  158.7 1.9 collective-permute-start.2
  161.4 2.3 collective-permute-start.3
  163.7 8.9 %body.5 = f32[4,512,128]{2,1,0:T(8,128)S(1)} custom-call(s32[1]{0:T(128)} %bitcast.36.step_ref, s32[3]{0:T(128)S(1)} %get-tuple-element.379.meta_ref, s32[1,512]{1,0:T(1,128)S(1)} %get-tuple-element.380.valid_ref, s32[512,1]{1,0:T(8,128)S(1)} %get-tuple-element.381.seg_ref, ...), custom_call_target="tpu_custom_call", output_to_operand_aliasing={{}: (7, {})} | custom-call | flops 402653184 | bytes 3407872 | tf_op jit(solution)/shard_map/while/body/pallas_call | solution.py:93
  173.3 1.9 collective-permute-start.2
  176.0 2.3 collective-permute-start.3
  178.3 8.9 %body.5 = f32[4,512,128]{2,1,0:T(8,128)S(1)} custom-call(s32[1]{0:T(128)} %bitcast.36.step_ref, s32[3]{0:T(128)S(1)} %get-tuple-element.379.meta_ref, s32[1,512]{1,0:T(1,128)S(1)} %get-tuple-element.380.valid_ref, s32[512,1]{1,0:T(8,128)S(1)} %get-tuple-element.381.seg_ref, ...), custom_call_target="tpu_custom_call", output_to_operand_aliasing={{}: (7, {})} | custom-call | flops 402653184 | bytes 3407872 | tf_op jit(solution)/shard_map/while/body/pallas_call | solution.py:93
  188.0 1.9 collective-permute-start.2
  190.6 2.3 collective-permute-start.3
  192.9 8.9 %body.5 = f32[4,512,128]{2,1,0:T(8,128)S(1)} custom-call(s32[1]{0:T(128)} %bitcast.36.step_ref, s32[3]{0:T(128)S(1)} %get-tuple-element.379.meta_ref, s32[1,512]{1,0:T(1,128)S(1)} %get-tuple-element.380.valid_ref, s32[512,1]{1,0:T(8,128)S(1)} %get-tuple-element.381.seg_ref, ...), custom_call_target="tpu_custom_call", output_to_operand_aliasing={{}: (7, {})} | custom-call | flops 402653184 | bytes 3407872 | tf_op jit(solution)/shard_map/while/body/pallas_call | solution.py:93
  202.6 1.9 collective-permute-start.2
  205.2 2.3 collective-permute-start.3
  207.6 8.9 %body.5 = f32[4,512,128]{2,1,0:T(8,128)S(1)} custom-call(s32[1]{0:T(128)} %bitcast.36.step_ref, s32[3]{0:T(128)S(1)} %get-tuple-element.379.meta_ref, s32[1,512]{1,0:T(1,128)S(1)} %get-tuple-element.380.valid_ref, s32[512,1]{1,0:T(8,128)S(1)} %get-tuple-element.381.seg_ref, ...), custom_call_target="tpu_custom_call", output_to_operand_aliasing={{}: (7, {})} | custom-call | flops 402653184 | bytes 3407872 | tf_op jit(solution)/shard_map/while/body/pallas_call | solution.py:93
  217.2 1.9 collective-permute-start.2
  219.8 2.3 collective-permute-start.3
  222.2 8.9 %body.5 = f32[4,512,128]{2,1,0:T(8,128)S(1)} custom-call(s32[1]{0:T(128)} %bitcast.36.step_ref, s32[3]{0:T(128)S(1)} %get-tuple-element.379.meta_ref, s32[1,512]{1,0:T(1,128)S(1)} %get-tuple-element.380.valid_ref, s32[512,1]{1,0:T(8,128)S(1)} %get-tuple-element.381.seg_ref, ...), custom_call_target="tpu_custom_call", output_to_operand_aliasing={{}: (7, {})} | custom-call | flops 402653184 | bytes 3407872 | tf_op jit(solution)/shard_map/while/body/pallas_call | solution.py:93
  231.8 1.9 collective-permute-start.2
  234.4 2.3 collective-permute-start.3
  236.8 8.9 %body.5 = f32[4,512,128]{2,1,0:T(8,128)S(1)} custom-call(s32[1]{0:T(128)} %bitcast.36.step_ref, s32[3]{0:T(128)S(1)} %get-tuple-element.379.meta_ref, s32[1,512]{1,0:T(1,128)S(1)} %get-tuple-element.380.valid_ref, s32[512,1]{1,0:T(8,128)S(1)} %get-tuple-element.381.seg_ref, ...), custom_call_target="tpu_custom_call", output_to_operand_aliasing={{}: (7, {})} | custom-call | flops 402653184 | bytes 3407872 | tf_op jit(solution)/shard_map/while/body/pallas_call | solution.py:93
  246.4 1.9 collective-permute-start.2
  249.0 2.3 collective-permute-start.3
  251.4 8.9 %body.5 = f32[4,512,128]{2,1,0:T(8,128)S(1)} custom-call(s32[1]{0:T(128)} %bitcast.36.step_ref, s32[3]{0:T(128)S(1)} %get-tuple-element.379.meta_ref, s32[1,512]{1,0:T(1,128)S(1)} %get-tuple-element.380.valid_ref, s32[512,1]{1,0:T(8,128)S(1)} %get-tuple-element.381.seg_ref, ...), custom_call_target="tpu_custom_call", output_to_operand_aliasing={{}: (7, {})} | custom-call | flops 402653184 | bytes 3407872 | tf_op jit(solution)/shard_map/while/body/pallas_call | solution.py:93
  261.0 1.9 collective-permute-start.2
  263.6 2.3 collective-permute-start.3
  266.0 8.9 %body.5 = f32[4,512,128]{2,1,0:T(8,128)S(1)} custom-call(s32[1]{0:T(128)} %bitcast.36.step_ref, s32[3]{0:T(128)S(1)} %get-tuple-element.379.meta_ref, s32[1,512]{1,0:T(1,128)S(1)} %get-tuple-element.380.valid_ref, s32[512,1]{1,0:T(8,128)S(1)} %get-tuple-element.381.seg_ref, ...), custom_call_target="tpu_custom_call", output_to_operand_aliasing={{}: (7, {})} | custom-call | flops 402653184 | bytes 3407872 | tf_op jit(solution)/shard_map/while/body/pallas_call | solution.py:93
  278.3 2.3 collective-permute-start.3
  280.6 9.3 %body.5 = f32[4,512,128]{2,1,0:T(8,128)S(1)} custom-call(s32[1]{0:T(128)} %bitcast.36.step_ref, s32[3]{0:T(128)S(1)} %get-tuple-element.379.meta_ref, s32[1,512]{1,0:T(1,128)S(1)} %get-tuple-element.380.valid_ref, s32[512,1]{1,0:T(8,128)S(1)} %get-tuple-element.381.seg_ref, ...), custom_call_target="tpu_custom_call", output_to_operand_aliasing={{}: (7, {})} | custom-call | flops 402653184 | bytes 3407872 | tf_op jit(solution)/shard_map/while/body/pallas_call | solution.py:93
  293.3 1.9 collective-permute-start.3
  295.2 2.8 body.5
  298.1 2.6 collective-permute-done.2
  300.7 2.8 collective-permute-done.3
  304.2 3.0 collective-permute-start.2
  307.9 1.9 collective-permute-start.3
  309.8 2.8 body.5
  314.2 3.7 collective-permute-done.3
  321.2 3.6 collective-permute-start.3
  324.9 2.8 body.5
  328.6 2.8 collective-permute-done.3
  334.4 1.9 copy.76
  337.2 2.3 copy.78
  346.7 29.5 %all-gather.5.cloned.1.call-done = bf16[512,1024]{0,1:T(8,128)(2,1)} async-done(((bf16[512,256]{0,1:T(8,128)(2,1)}), bf16[512,1024]{0,1:T(8,128)(2,1)}) %all-gather.5.cloned.1.call-update) | async-done | bytes 1048592 | tf_op jit(solution)/shard_map/all_gather | solution.py:233
  376.2 2.9 fusion.3
  (141 shorter events, 59.3 us)
Async XLA Ops:
  7.2 58.3 %copy-start = (bf16[2048,256]{1,0:T(8,128)(2,1)S(1)}, bf16[2048,256]{1,0:T(8,128)(2,1)}, u32[]{:S(2)}) copy-start(bf16[2048,256]{1,0:T(8,128)(2,1)} %param.17) | copy-start | bytes 3145732
  7.2 26.5 %copy-start.9 = (s32[512]{0:T(512)S(1)}, s32[512]{0:T(512)}, u32[]{:S(2)}) copy-start(s32[512]{0:T(512)} %param.19) | copy-start | bytes 6148
  7.2 26.4 %copy-start.8 = (s32[512]{0:T(512)S(1)}, s32[512]{0:T(512)}, u32[]{:S(2)}) copy-start(s32[512]{0:T(512)} %param.20) | copy-start | bytes 6148
  7.2 56.0 %all-gather.3.cloned.1.call-start = ((), (), s32[]{:S(2)}) async-start(), calls=%async_computation.2 | async-start | bytes 2621440 | tf_op jit(solution)/shard_map/all_gather | solution.py:150
  7.9 82.9 %collective-permute-start.6 = (s32[4]{0:T(128)}, s32[4]{0:T(128)S(1)}, u32[]{:S(2)}, u32[]{:S(2)}) collective-permute-start(s32[4]{0:T(128)} %param.21), channel_id=1, source_target_pairs={{0,4},{4,8},{8,12},{12,16},{16,20},{20,24},{24,28},{28,32},{32,36}... | collective-permute-start | bytes 56 | tf_op jit(solution)/shard_map/ppermute | solution.py:109
  14.4 76.5 %all-to-all-start = ((s32[64,1,1]{2,1,0:T(1,128)}), s32[64,1,1]{2,1,0:T(1,128)S(1)}, u32[]{:S(2)}, u32[]{:S(2)}) async-start(s32[64,1,1]{2,1,0:T(1,128)} %broadcast_in_dim.79), calls=%async_computation | async-start | bytes 65536 | tf_op jit(solution)/shard_map/all_to_all | solution.py:148
  30.6 34.9 %copy-start.12 = (f32[2048]{0:T(1024)S(1)}, f32[2048]{0:T(1024)}, u32[]{:S(2)}) copy-start(f32[2048]{0:T(1024)} %param.14) | copy-start | bytes 24580
  63.2 2.3 copy-start.4
  69.1 3.1 copy-start.11
  80.0 3.3 copy-start.3
  83.7 1.6 copy-start.1
  84.5 12.1 %copy-start.5 = (bf16[512,4,32]{2,0,1:T(8,128)(2,1)S(1)}, bf16[512,4,32]{2,0,1:T(8,128)(2,1)}, u32[]{:S(2)}) copy-start(bf16[512,4,32]{2,0,1:T(8,128)(2,1)} %get-tuple-element.212) | copy-start | bytes 393220
  85.4 11.2 %copy-start.6 = (bf16[512,4,32]{2,0,1:T(8,128)(2,1)S(1)}, bf16[512,4,32]{2,0,1:T(8,128)(2,1)}, u32[]{:S(2)}) copy-start(bf16[512,4,32]{2,0,1:T(8,128)(2,1)} %get-tuple-element.213) | copy-start | bytes 393220
  85.4 20.9 %collective-permute-start.5 = (bf16[2,512,128]{2,1,0:T(8,128)(2,1)}, bf16[2,512,128]{2,1,0:T(8,128)(2,1)}, u32[]{:S(2)}, u32[]{:S(2)}) collective-permute-start(bf16[2,512,128]{2,1,0:T(8,128)(2,1)} %get-tuple-element.210.kv_b_ref), channel_id=1, source_target_pairs={{0,4},{4,8},{8,12},{12,16},{16,20},{20,24},{24,28},{28,32},{32,36}... | collective-permute-start | bytes 786440 | tf_op jit(solution)/shard_map/ppermute | solution.py:198
  87.4 19.8 %collective-permute-start.4 = (bf16[2,512,128]{2,1,0:T(8,128)(2,1)}, bf16[2,512,128]{2,1,0:T(8,128)(2,1)}, u32[]{:S(2)}, u32[]{:S(2)}) collective-permute-start(bf16[2,512,128]{2,1,0:T(8,128)(2,1)} %get-tuple-element.211.kv_a_ref), channel_id=1, source_target_pairs={{0,4},{4,8},{8,12},{12,16},{16,20},{20,24},{24,28},{28,32},{32,36}... | collective-permute-start | bytes 786440 | tf_op jit(solution)/shard_map/ppermute | solution.py:198
  90.9 246.3 %all-to-all-start.1 = ((bf16[256,4,512]{0,2,1:T(8,128)(2,1)}), bf16[256,4,512]{0,2,1:T(8,128)(2,1)}, u32[]{:S(2)}, u32[]{:S(2)}) async-start(bf16[256,4,512]{0,2,1:T(8,128)(2,1)} %bitcast.16), calls=%async_computation.1 | async-start | bytes 2097152 | tf_op jit(solution)/shard_map/all_to_all | solution.py:176
  95.2 281.0 %all-gather.5.cloned.1.call-start = ((), (), s32[]{:S(2)}) async-start(), calls=%async_computation.3 | async-start | bytes 1310720 | tf_op jit(solution)/shard_map/all_gather | solution.py:233
  108.9 15.0 %collective-permute-start.2 = (bf16[2,512,128]{2,1,0:T(8,128)(2,1)}, bf16[2,512,128]{2,1,0:T(8,128)(2,1)S(1)}, u32[]{:S(2)}, u32[]{:S(2)}) collective-permute-start(bf16[2,512,128]{2,1,0:T(8,128)(2,1)} %copy.109.kv_a_ref), channel_id=1, source_target_pairs={{0,4},{4,8},{8,12},{12,16},{16,20},{20,24},{24,28},{28,32},{32,36}... | collective-permute-start | bytes 786440 | tf_op jit(solution)/shard_map/while/body/ppermute | solution.py:204
  111.5 12.4 %collective-permute-start.3 = (bf16[2,512,128]{2,1,0:T(8,128)(2,1)}, bf16[2,512,128]{2,1,0:T(8,128)(2,1)S(1)}, u32[]{:S(2)}, u32[]{:S(2)}) collective-permute-start(bf16[2,512,128]{2,1,0:T(8,128)(2,1)} %copy.110.kv_b_ref), channel_id=1, source_target_pairs={{0,4},{4,8},{8,12},{12,16},{16,20},{20,24},{24,28},{28,32},{32,36}... | collective-permute-start | bytes 786440 | tf_op jit(solution)/shard_map/while/body/ppermute | solution.py:204
  124.6 14.7 %collective-permute-start.2 = (bf16[2,512,128]{2,1,0:T(8,128)(2,1)}, bf16[2,512,128]{2,1,0:T(8,128)(2,1)S(1)}, u32[]{:S(2)}, u32[]{:S(2)}) collective-permute-start(bf16[2,512,128]{2,1,0:T(8,128)(2,1)} %copy.109.kv_a_ref), channel_id=1, source_target_pairs={{0,4},{4,8},{8,12},{12,16},{16,20},{20,24},{24,28},{28,32},{32,36}... | collective-permute-start | bytes 786440 | tf_op jit(solution)/shard_map/while/body/ppermute | solution.py:204
  127.3 12.1 %collective-permute-start.3 = (bf16[2,512,128]{2,1,0:T(8,128)(2,1)}, bf16[2,512,128]{2,1,0:T(8,128)(2,1)S(1)}, u32[]{:S(2)}, u32[]{:S(2)}) collective-permute-start(bf16[2,512,128]{2,1,0:T(8,128)(2,1)} %copy.110.kv_b_ref), channel_id=1, source_target_pairs={{0,4},{4,8},{8,12},{12,16},{16,20},{20,24},{24,28},{28,32},{32,36}... | collective-permute-start | bytes 786440 | tf_op jit(solution)/shard_map/while/body/ppermute | solution.py:204
  140.1 17.9 %collective-permute-start.2 = (bf16[2,512,128]{2,1,0:T(8,128)(2,1)}, bf16[2,512,128]{2,1,0:T(8,128)(2,1)S(1)}, u32[]{:S(2)}, u32[]{:S(2)}) collective-permute-start(bf16[2,512,128]{2,1,0:T(8,128)(2,1)} %copy.109.kv_a_ref), channel_id=1, source_target_pairs={{0,4},{4,8},{8,12},{12,16},{16,20},{20,24},{24,28},{28,32},{32,36}... | collective-permute-start | bytes 786440 | tf_op jit(solution)/shard_map/while/body/ppermute | solution.py:204
  142.7 15.3 %collective-permute-start.3 = (bf16[2,512,128]{2,1,0:T(8,128)(2,1)}, bf16[2,512,128]{2,1,0:T(8,128)(2,1)S(1)}, u32[]{:S(2)}, u32[]{:S(2)}) collective-permute-start(bf16[2,512,128]{2,1,0:T(8,128)(2,1)} %copy.110.kv_b_ref), channel_id=1, source_target_pairs={{0,4},{4,8},{8,12},{12,16},{16,20},{20,24},{24,28},{28,32},{32,36}... | collective-permute-start | bytes 786440 | tf_op jit(solution)/shard_map/while/body/ppermute | solution.py:204
  158.7 13.9 %collective-permute-start.2 = (bf16[2,512,128]{2,1,0:T(8,128)(2,1)}, bf16[2,512,128]{2,1,0:T(8,128)(2,1)S(1)}, u32[]{:S(2)}, u32[]{:S(2)}) collective-permute-start(bf16[2,512,128]{2,1,0:T(8,128)(2,1)} %copy.109.kv_a_ref), channel_id=1, source_target_pairs={{0,4},{4,8},{8,12},{12,16},{16,20},{20,24},{24,28},{28,32},{32,36}... | collective-permute-start | bytes 786440 | tf_op jit(solution)/shard_map/while/body/ppermute | solution.py:204
  161.4 11.2 %collective-permute-start.3 = (bf16[2,512,128]{2,1,0:T(8,128)(2,1)}, bf16[2,512,128]{2,1,0:T(8,128)(2,1)S(1)}, u32[]{:S(2)}, u32[]{:S(2)}) collective-permute-start(bf16[2,512,128]{2,1,0:T(8,128)(2,1)} %copy.110.kv_b_ref), channel_id=1, source_target_pairs={{0,4},{4,8},{8,12},{12,16},{16,20},{20,24},{24,28},{28,32},{32,36}... | collective-permute-start | bytes 786440 | tf_op jit(solution)/shard_map/while/body/ppermute | solution.py:204
  173.3 13.9 %collective-permute-start.2 = (bf16[2,512,128]{2,1,0:T(8,128)(2,1)}, bf16[2,512,128]{2,1,0:T(8,128)(2,1)S(1)}, u32[]{:S(2)}, u32[]{:S(2)}) collective-permute-start(bf16[2,512,128]{2,1,0:T(8,128)(2,1)} %copy.109.kv_a_ref), channel_id=1, source_target_pairs={{0,4},{4,8},{8,12},{12,16},{16,20},{20,24},{24,28},{28,32},{32,36}... | collective-permute-start | bytes 786440 | tf_op jit(solution)/shard_map/while/body/ppermute | solution.py:204
  176.0 11.2 %collective-permute-start.3 = (bf16[2,512,128]{2,1,0:T(8,128)(2,1)}, bf16[2,512,128]{2,1,0:T(8,128)(2,1)S(1)}, u32[]{:S(2)}, u32[]{:S(2)}) collective-permute-start(bf16[2,512,128]{2,1,0:T(8,128)(2,1)} %copy.110.kv_b_ref), channel_id=1, source_target_pairs={{0,4},{4,8},{8,12},{12,16},{16,20},{20,24},{24,28},{28,32},{32,36}... | collective-permute-start | bytes 786440 | tf_op jit(solution)/shard_map/while/body/ppermute | solution.py:204
  188.0 13.9 %collective-permute-start.2 = (bf16[2,512,128]{2,1,0:T(8,128)(2,1)}, bf16[2,512,128]{2,1,0:T(8,128)(2,1)S(1)}, u32[]{:S(2)}, u32[]{:S(2)}) collective-permute-start(bf16[2,512,128]{2,1,0:T(8,128)(2,1)} %copy.109.kv_a_ref), channel_id=1, source_target_pairs={{0,4},{4,8},{8,12},{12,16},{16,20},{20,24},{24,28},{28,32},{32,36}... | collective-permute-start | bytes 786440 | tf_op jit(solution)/shard_map/while/body/ppermute | solution.py:204
  190.6 11.2 %collective-permute-start.3 = (bf16[2,512,128]{2,1,0:T(8,128)(2,1)}, bf16[2,512,128]{2,1,0:T(8,128)(2,1)S(1)}, u32[]{:S(2)}, u32[]{:S(2)}) collective-permute-start(bf16[2,512,128]{2,1,0:T(8,128)(2,1)} %copy.110.kv_b_ref), channel_id=1, source_target_pairs={{0,4},{4,8},{8,12},{12,16},{16,20},{20,24},{24,28},{28,32},{32,36}... | collective-permute-start | bytes 786440 | tf_op jit(solution)/shard_map/while/body/ppermute | solution.py:204
  202.6 13.9 %collective-permute-start.2 = (bf16[2,512,128]{2,1,0:T(8,128)(2,1)}, bf16[2,512,128]{2,1,0:T(8,128)(2,1)S(1)}, u32[]{:S(2)}, u32[]{:S(2)}) collective-permute-start(bf16[2,512,128]{2,1,0:T(8,128)(2,1)} %copy.109.kv_a_ref), channel_id=1, source_target_pairs={{0,4},{4,8},{8,12},{12,16},{16,20},{20,24},{24,28},{28,32},{32,36}... | collective-permute-start | bytes 786440 | tf_op jit(solution)/shard_map/while/body/ppermute | solution.py:204
  205.2 11.2 %collective-permute-start.3 = (bf16[2,512,128]{2,1,0:T(8,128)(2,1)}, bf16[2,512,128]{2,1,0:T(8,128)(2,1)S(1)}, u32[]{:S(2)}, u32[]{:S(2)}) collective-permute-start(bf16[2,512,128]{2,1,0:T(8,128)(2,1)} %copy.110.kv_b_ref), channel_id=1, source_target_pairs={{0,4},{4,8},{8,12},{12,16},{16,20},{20,24},{24,28},{28,32},{32,36}... | collective-permute-start | bytes 786440 | tf_op jit(solution)/shard_map/while/body/ppermute | solution.py:204
  217.2 13.9 %collective-permute-start.2 = (bf16[2,512,128]{2,1,0:T(8,128)(2,1)}, bf16[2,512,128]{2,1,0:T(8,128)(2,1)S(1)}, u32[]{:S(2)}, u32[]{:S(2)}) collective-permute-start(bf16[2,512,128]{2,1,0:T(8,128)(2,1)} %copy.109.kv_a_ref), channel_id=1, source_target_pairs={{0,4},{4,8},{8,12},{12,16},{16,20},{20,24},{24,28},{28,32},{32,36}... | collective-permute-start | bytes 786440 | tf_op jit(solution)/shard_map/while/body/ppermute | solution.py:204
  219.8 11.2 %collective-permute-start.3 = (bf16[2,512,128]{2,1,0:T(8,128)(2,1)}, bf16[2,512,128]{2,1,0:T(8,128)(2,1)S(1)}, u32[]{:S(2)}, u32[]{:S(2)}) collective-permute-start(bf16[2,512,128]{2,1,0:T(8,128)(2,1)} %copy.110.kv_b_ref), channel_id=1, source_target_pairs={{0,4},{4,8},{8,12},{12,16},{16,20},{20,24},{24,28},{28,32},{32,36}... | collective-permute-start | bytes 786440 | tf_op jit(solution)/shard_map/while/body/ppermute | solution.py:204
  231.8 13.9 %collective-permute-start.2 = (bf16[2,512,128]{2,1,0:T(8,128)(2,1)}, bf16[2,512,128]{2,1,0:T(8,128)(2,1)S(1)}, u32[]{:S(2)}, u32[]{:S(2)}) collective-permute-start(bf16[2,512,128]{2,1,0:T(8,128)(2,1)} %copy.109.kv_a_ref), channel_id=1, source_target_pairs={{0,4},{4,8},{8,12},{12,16},{16,20},{20,24},{24,28},{28,32},{32,36}... | collective-permute-start | bytes 786440 | tf_op jit(solution)/shard_map/while/body/ppermute | solution.py:204
  234.4 11.2 %collective-permute-start.3 = (bf16[2,512,128]{2,1,0:T(8,128)(2,1)}, bf16[2,512,128]{2,1,0:T(8,128)(2,1)S(1)}, u32[]{:S(2)}, u32[]{:S(2)}) collective-permute-start(bf16[2,512,128]{2,1,0:T(8,128)(2,1)} %copy.110.kv_b_ref), channel_id=1, source_target_pairs={{0,4},{4,8},{8,12},{12,16},{16,20},{20,24},{24,28},{28,32},{32,36}... | collective-permute-start | bytes 786440 | tf_op jit(solution)/shard_map/while/body/ppermute | solution.py:204
  246.4 13.9 %collective-permute-start.2 = (bf16[2,512,128]{2,1,0:T(8,128)(2,1)}, bf16[2,512,128]{2,1,0:T(8,128)(2,1)S(1)}, u32[]{:S(2)}, u32[]{:S(2)}) collective-permute-start(bf16[2,512,128]{2,1,0:T(8,128)(2,1)} %copy.109.kv_a_ref), channel_id=1, source_target_pairs={{0,4},{4,8},{8,12},{12,16},{16,20},{20,24},{24,28},{28,32},{32,36}... | collective-permute-start | bytes 786440 | tf_op jit(solution)/shard_map/while/body/ppermute | solution.py:204
  249.0 11.2 %collective-permute-start.3 = (bf16[2,512,128]{2,1,0:T(8,128)(2,1)}, bf16[2,512,128]{2,1,0:T(8,128)(2,1)S(1)}, u32[]{:S(2)}, u32[]{:S(2)}) collective-permute-start(bf16[2,512,128]{2,1,0:T(8,128)(2,1)} %copy.110.kv_b_ref), channel_id=1, source_target_pairs={{0,4},{4,8},{8,12},{12,16},{16,20},{20,24},{24,28},{28,32},{32,36}... | collective-permute-start | bytes 786440 | tf_op jit(solution)/shard_map/while/body/ppermute | solution.py:204
  261.0 13.9 %collective-permute-start.2 = (bf16[2,512,128]{2,1,0:T(8,128)(2,1)}, bf16[2,512,128]{2,1,0:T(8,128)(2,1)S(1)}, u32[]{:S(2)}, u32[]{:S(2)}) collective-permute-start(bf16[2,512,128]{2,1,0:T(8,128)(2,1)} %copy.109.kv_a_ref), channel_id=1, source_target_pairs={{0,4},{4,8},{8,12},{12,16},{16,20},{20,24},{24,28},{28,32},{32,36}... | collective-permute-start | bytes 786440 | tf_op jit(solution)/shard_map/while/body/ppermute | solution.py:204
  263.6 11.2 %collective-permute-start.3 = (bf16[2,512,128]{2,1,0:T(8,128)(2,1)}, bf16[2,512,128]{2,1,0:T(8,128)(2,1)S(1)}, u32[]{:S(2)}, u32[]{:S(2)}) collective-permute-start(bf16[2,512,128]{2,1,0:T(8,128)(2,1)} %copy.110.kv_b_ref), channel_id=1, source_target_pairs={{0,4},{4,8},{8,12},{12,16},{16,20},{20,24},{24,28},{28,32},{32,36}... | collective-permute-start | bytes 786440 | tf_op jit(solution)/shard_map/while/body/ppermute | solution.py:204
  275.6 14.3 %collective-permute-start.2 = (bf16[2,512,128]{2,1,0:T(8,128)(2,1)}, bf16[2,512,128]{2,1,0:T(8,128)(2,1)S(1)}, u32[]{:S(2)}, u32[]{:S(2)}) collective-permute-start(bf16[2,512,128]{2,1,0:T(8,128)(2,1)} %copy.109.kv_a_ref), channel_id=1, source_target_pairs={{0,4},{4,8},{8,12},{12,16},{16,20},{20,24},{24,28},{28,32},{32,36}... | collective-permute-start | bytes 786440 | tf_op jit(solution)/shard_map/while/body/ppermute | solution.py:204
  278.3 11.7 %collective-permute-start.3 = (bf16[2,512,128]{2,1,0:T(8,128)(2,1)}, bf16[2,512,128]{2,1,0:T(8,128)(2,1)S(1)}, u32[]{:S(2)}, u32[]{:S(2)}) collective-permute-start(bf16[2,512,128]{2,1,0:T(8,128)(2,1)} %copy.110.kv_b_ref), channel_id=1, source_target_pairs={{0,4},{4,8},{8,12},{12,16},{16,20},{20,24},{24,28},{28,32},{32,36}... | collective-permute-start | bytes 786440 | tf_op jit(solution)/shard_map/while/body/ppermute | solution.py:204
  290.7 10.0 %collective-permute-start.2 = (bf16[2,512,128]{2,1,0:T(8,128)(2,1)}, bf16[2,512,128]{2,1,0:T(8,128)(2,1)S(1)}, u32[]{:S(2)}, u32[]{:S(2)}) collective-permute-start(bf16[2,512,128]{2,1,0:T(8,128)(2,1)} %copy.109.kv_a_ref), channel_id=1, source_target_pairs={{0,4},{4,8},{8,12},{12,16},{16,20},{20,24},{24,28},{28,32},{32,36}... | collective-permute-start | bytes 786440 | tf_op jit(solution)/shard_map/while/body/ppermute | solution.py:204
  293.3 10.2 %collective-permute-start.3 = (bf16[2,512,128]{2,1,0:T(8,128)(2,1)}, bf16[2,512,128]{2,1,0:T(8,128)(2,1)S(1)}, u32[]{:S(2)}, u32[]{:S(2)}) collective-permute-start(bf16[2,512,128]{2,1,0:T(8,128)(2,1)} %copy.110.kv_b_ref), channel_id=1, source_target_pairs={{0,4},{4,8},{8,12},{12,16},{16,20},{20,24},{24,28},{28,32},{32,36}... | collective-permute-start | bytes 786440 | tf_op jit(solution)/shard_map/while/body/ppermute | solution.py:204
  304.2 10.0 %collective-permute-start.2 = (bf16[2,512,128]{2,1,0:T(8,128)(2,1)}, bf16[2,512,128]{2,1,0:T(8,128)(2,1)S(1)}, u32[]{:S(2)}, u32[]{:S(2)}) collective-permute-start(bf16[2,512,128]{2,1,0:T(8,128)(2,1)} %copy.109.kv_a_ref), channel_id=1, source_target_pairs={{0,4},{4,8},{8,12},{12,16},{16,20},{20,24},{24,28},{28,32},{32,36}... | collective-permute-start | bytes 786440 | tf_op jit(solution)/shard_map/while/body/ppermute | solution.py:204
  307.9 10.0 %collective-permute-start.3 = (bf16[2,512,128]{2,1,0:T(8,128)(2,1)}, bf16[2,512,128]{2,1,0:T(8,128)(2,1)S(1)}, u32[]{:S(2)}, u32[]{:S(2)}) collective-permute-start(bf16[2,512,128]{2,1,0:T(8,128)(2,1)} %copy.110.kv_b_ref), channel_id=1, source_target_pairs={{0,4},{4,8},{8,12},{12,16},{16,20},{20,24},{24,28},{28,32},{32,36}... | collective-permute-start | bytes 786440 | tf_op jit(solution)/shard_map/while/body/ppermute | solution.py:204
  318.6 10.0 %collective-permute-start.2 = (bf16[2,512,128]{2,1,0:T(8,128)(2,1)}, bf16[2,512,128]{2,1,0:T(8,128)(2,1)S(1)}, u32[]{:S(2)}, u32[]{:S(2)}) collective-permute-start(bf16[2,512,128]{2,1,0:T(8,128)(2,1)} %copy.109.kv_a_ref), channel_id=1, source_target_pairs={{0,4},{4,8},{8,12},{12,16},{16,20},{20,24},{24,28},{28,32},{32,36}... | collective-permute-start | bytes 786440 | tf_op jit(solution)/shard_map/while/body/ppermute | solution.py:204
  321.2 10.2 %collective-permute-start.3 = (bf16[2,512,128]{2,1,0:T(8,128)(2,1)}, bf16[2,512,128]{2,1,0:T(8,128)(2,1)S(1)}, u32[]{:S(2)}, u32[]{:S(2)}) collective-permute-start(bf16[2,512,128]{2,1,0:T(8,128)(2,1)} %copy.110.kv_b_ref), channel_id=1, source_target_pairs={{0,4},{4,8},{8,12},{12,16},{16,20},{20,24},{24,28},{28,32},{32,36}... | collective-permute-start | bytes 786440 | tf_op jit(solution)/shard_map/while/body/ppermute | solution.py:204
  332.3 4.0 %copy-start.10 = (s32[4]{0:T(128)S(1)}, s32[4]{0:T(128)}, u32[]{:S(2)}) copy-start(s32[4]{0:T(128)} %param.21) | copy-start | bytes 52
  333.0 6.5 %copy-start.2 = (bf16[512,4,2,64]{3,0,1,2:T(8,128)(2,1)S(1)}, bf16[512,4,2,64]{3,0,1,2:T(8,128)(2,1)}, u32[]{:S(2)}) copy-start(bf16[512,4,2,64]{3,0,1,2:T(8,128)(2,1)} %copy-done.1) | copy-start | bytes 1572868
  345.6 30.6 %copy-start.7 = (bf16[4,256,512]{2,1,0:T(8,128)(2,1)S(1)}, bf16[4,256,512]{2,1,0:T(8,128)(2,1)}, u32[]{:S(2)}) copy-start(bf16[4,256,512]{2,1,0:T(8,128)(2,1)} %copy.78) | copy-start | bytes 3145732
Sparse Core Ops, SparseCore 0:
  9.8 53.3 all-gather.2
  336.5 39.7 all-gather.4
where the time goes:
time: 387 us; the launch traced here: 386 us
  Pallas kernels  126 us (33%)
  starting transfers between devices  98.3 us (25%)
  waiting for transfers between devices  72.4 us (19%)
  local copies, waits for them, and re-layouts  47.3 us (12%)
  between operations  17.7 us (5%)
  other arithmetic  16.2 us (4%)
  matrix products  7.71 us (2%)
    pallas_call x17, Pallas kernels, attend_step(): pl.pallas_call(_step_kernel, grid_spec=grid_spec, out_shape=jax.ShapeDtyp...  126 us
    ppermute x30, starting transfers between devices, advance(): sent = tuple((lax.ppermute(part, 'seq', pairs) for part in held))  71.3 us
    all_gather x1, waiting for transfers between devices, body(): attended_all = lax.all_gather(attended, 'tp', axis=1, tiled=True)  29.5 us
    all_gather x1, waiting for transfers between devices, body(): gathered = lax.all_gather(residual, 'tp', axis=1, tiled=True)  27.8 us
    another operation x30, local copies, waits for them, and re-layouts  21.3 us
    all_to_all x1, starting transfers between devices, body(): cross_steps = jnp.sum(lax.all_to_all(told, 'seq', 0, 0, tiled=True))  15.3 us
    ppermute x30, waiting for transfers between devices, advance(): sent = tuple((lax.ppermute(part, 'seq', pairs) for part in held))  14.4 us
    unnamed x33, local copies, waits for them, and re-layouts  10.4 us
  transfers between devices with their start and end apart: 37, of which 8 were waited for; matrix products, arithmetic and copies ran while one was open for 18% of the time, Pallas kernels for 33%

commit v1 on v0

--- a/solution.py
+++ b/solution.py
@@ -103,6 +103,12 @@
     )(step, meta, valid_row, seg_col, q_hm, kv_a, kv_b, state)
 
 
+def tp_gather(x, count):
+    copies = jnp.broadcast_to(x[None], (count,) + x.shape)
+    got = lax.all_to_all(copies, "tp", 0, 0, tiled=True)
+    return jnp.transpose(got, (1, 0, 2)).reshape(x.shape[0], count * x.shape[1])
+
+
 def passed_along(x, axis, by):
     count = lax.axis_size(axis)
     pairs = [(i, i + by) for i in range(count) if 0 <= i + by < count]
@@ -147,7 +153,8 @@
     told = jnp.broadcast_to(jnp.where(seq_rank == half, cross_here, 0), (seq_count,))
     cross_steps = jnp.sum(lax.all_to_all(told, "seq", 0, 0, tiled=True))
     cross_steps = jnp.maximum(cross_steps, 1)
-    gathered = lax.all_gather(residual, "tp", axis=1, tiled=True)
+    tp_count = lax.axis_size("tp")
+    gathered = tp_gather(residual, tp_count)
     widened = gathered.astype(jnp.float32)
     mean_sq = jnp.mean(widened * widened, axis=1, keepdims=True)
     normed = (widened * lax.rsqrt(mean_sq + EPS) * norm_gain[None, :]).astype(jnp.bfloat16)
@@ -230,7 +237,7 @@
     found = jnp.any(match, axis=1)
     cache_pages = jnp.where(found[:, None, None], cand_pages[pick], jnp.zeros_like(cand_pages[:1]))
 
-    attended_all = lax.all_gather(attended, "tp", axis=1, tiled=True)
+    attended_all = tp_gather(attended, tp_count)
     projected = jnp.dot(attended_all, out_cols, preferred_element_type=jnp.float32)
     hidden = (residual.astype(jnp.float32) + projected).astype(jnp.bfloat16)
     return (hidden, cache_pages)

time: 387 us -> 340 us (0.88)
  Pallas kernels: 126 us -> 83.4 us
  waiting for transfers between devices: 72.4 us -> 105 us
  local copies, waits for them, and re-layouts: 47.3 us -> 22.9 us
  between operations: 17.7 us -> 4.42 us
  starting transfers between devices: 98.3 us -> 109 us
  other arithmetic: 16.2 us -> 7.95 us
    all_gather x2 -> x0, waiting for transfers between devices: 57.3 us -> none  [the longest x1 29.5 us: body(): attended_all = lax.all_gather(attended, 'tp', axis=1, tiled=True)]
    all_to_all x0 -> x2, waiting for transfers between devices: none -> 47 us  [tp_gather(): got = lax.all_to_all(copies, 'tp', 0, 0, tiled=True)]
    ppermute x30, waiting for transfers between devices: 14.4 us -> 57.8 us  [advance(): sent = tuple((lax.ppermute(part, 'seq', pairs) for part in held))]
    pallas_call x17, Pallas kernels: 126 us -> 83.4 us  [attend_step(): pl.pallas_call(_step_kernel, grid_spec=grid_spec, out_shape=jax.ShapeDtyp...]
    another operation x30, local copies, waits for them, and re-layouts: 21.3 us -> 0.56 us
    all_to_all x0 -> x2, starting transfers between devices: none -> 10.7 us  [tp_gather(): got = lax.all_to_all(copies, 'tp', 0, 0, tiled=True)]
    unnamed x33 -> x36, local copies, waits for them, and re-layouts: 10.4 us -> 8.37 us
  transfers between devices with their start and end apart: 37 -> 37, of which waited for: 8 -> 23; matrix products, arithmetic and copies ran while one was open for 18% -> 9% of each run, Pallas kernels for 33% -> 24%
where the time goes in v1:
time: 340 us; the launch traced here: 341 us
  starting transfers between devices  109 us (32%)
  waiting for transfers between devices  105 us (31%)
  Pallas kernels  83.4 us (25%)
  local copies, waits for them, and re-layouts  22.9 us (7%)
  other arithmetic  7.95 us (2%)
  matrix products  6.94 us (2%)
  between operations  4.42 us (1%)
    pallas_call x17, Pallas kernels, attend_step(): pl.pallas_call(_step_kernel, grid_spec=grid_spec, out_shape=jax.ShapeDtyp...  83.4 us
    ppermute x30, starting transfers between devices, advance(): sent = tuple((lax.ppermute(part, 'seq', pairs) for part in held))  74.1 us
    ppermute x30, waiting for transfers between devices, advance(): sent = tuple((lax.ppermute(part, 'seq', pairs) for part in held))  57.8 us
    all_to_all x2, waiting for transfers between devices, tp_gather(): got = lax.all_to_all(copies, 'tp', 0, 0, tiled=True)  47 us
    all_to_all x1, starting transfers between devices, body(): cross_steps = jnp.sum(lax.all_to_all(told, 'seq', 0, 0, tiled=True))  12.3 us
    all_to_all x2, starting transfers between devices, tp_gather(): got = lax.all_to_all(copies, 'tp', 0, 0, tiled=True)  10.7 us
    unnamed x36, local copies, waits for them, and re-layouts  8.37 us
  transfers between devices with their start and end apart: 37, of which 23 were waited for; matrix products, arithmetic and copies ran while one was open for 9% of the time, Pallas kernels for 24%

profile of v1, /device:TPU:24, one launch (start us, length us, event | category | flops | bytes accessed | tf_op | source)
XLA Modules:
  0.0 340.7 jit_solution(15844857541152778773)
XLA Ops:
  0.6 2.6 broadcast_in_dim.94
  3.2 6.0 %all-to-all-start = ((bf16[4,512,512]{2,1,0:T(8,128)(2,1)}), bf16[4,512,512]{2,1,0:T(8,128)(2,1)S(1)}, u32[]{:S(2)}, u32[]{:S(2)}) async-start(bf16[4,512,512]{2,1,0:T(8,128)(2,1)} %broadcast_in_dim.94), calls=%async_computation | async-start | bytes 4194304 | tf_op jit(solution)/shard_map/all_to_all | solution.py:108
  15.2 2.4 copy.121
  24.4 33.0 %all-to-all-done = bf16[4,512,512]{2,1,0:T(8,128)(2,1)S(1)} async-done(((bf16[4,512,512]{2,1,0:T(8,128)(2,1)}), bf16[4,512,512]{2,1,0:T(8,128)(2,1)S(1)}, u32[]{:S(2)}, u32[]{:S(2)}) %all-to-all-start) | async-done | bytes 2097184 | tf_op jit(solution)/shard_map/all_to_all | solution.py:108
  58.8 12.3 %all-to-all-start.1 = ((s32[64,1,1]{2,1,0:T(1,128)}), s32[64,1,1]{2,1,0:T(1,128)S(1)}, u32[]{:S(2)}, u32[]{:S(2)}) async-start(s32[64,1,1]{2,1,0:T(1,128)} %broadcast_in_dim.95), calls=%async_computation.1 | async-start | bytes 65536 | tf_op jit(solution)/shard_map/all_to_all | solution.py:154
  71.1 2.8 copy.115
  81.8 4.2 %all-to-all-start.3 = ((bf16[256,4,512]{2,0,1:T(8,128)(2,1)}), bf16[256,4,512]{2,0,1:T(8,128)(2,1)}, u32[]{:S(2)}, u32[]{:S(2)}) async-start(bf16[256,4,512]{2,0,1:T(8,128)(2,1)} %copy.137), calls=%async_computation.3 | async-start | bytes 2097152 | tf_op jit(solution)/shard_map/all_to_all | solution.py:183
  86.2 2.0 collective-permute-start.4
  88.3 3.6 %collective-permute-start.5 = (bf16[2,512,128]{2,1,0:T(8,128)(2,1)S(1)}, bf16[2,512,128]{2,1,0:T(8,128)(2,1)S(1)}, u32[]{:S(2)}, u32[]{:S(2)}) collective-permute-start(bf16[2,512,128]{2,1,0:T(8,128)(2,1)S(1)} %get-tuple-element.227.kv_b_ref), channel_id=1, source_target_pairs={{0,4},{4,8},{8,12},{12,16},{16,20},{20,24},{24,28},{28,32},{32,36}... | collective-permute-start | bytes 786440 | tf_op jit(solution)/shard_map/ppermute | solution.py:205
  93.7 9.3 %shard_map.104 = f32[4,512,128]{2,1,0:T(8,128)S(1)} custom-call(s32[1]{0:T(128)} %constant.69.clone.1.step_ref, s32[3]{0:T(128)S(1)} %pad_add_fusion.meta_ref, s32[1,512]{1,0:T(1,128)S(1)} %bitcast.72, s32[512,1]{1,0:T(8,128)S(1)} %copy.133.seg_ref, bf16[4,512,64]{2,1,0:T(8,128)(2,1)S(1)} %maximum_bitcast_fusion.q_ref, ...), custom_call_target="tpu_custom_call", output_to_operand_aliasing={{}: (7, {})} | custom-call | flops 402653184 | bytes 3407872 | tf_op jit(solution)/shard_map/pallas_call | solution.py:93
  103.1 14.4 %while.28 = (s32[]{:T(128)}, bf16[2,512,128]{2,1,0:T(8,128)(2,1)S(1)}, bf16[2,512,128]{2,1,0:T(8,128)(2,1)S(1)}, f32[4,512,128]{2,1,0:T(8,128)S(1)}, s32[]{:T(12...) while((s32[]{:T(128)}, ...), condition=%wide.region_3.4_spmd, body=%wide.region_2.3_spmd.sunk | while | flops 402653184 | bytes 8650997 | solution.py:217
  103.2 2.0 collective-permute-start
  105.2 3.4 collective-permute-start.1
  108.6 8.9 %body.4 = f32[4,512,128]{2,1,0:T(8,128)S(1)} custom-call(s32[1]{0:T(128)} %bitcast.61.step_ref, s32[3]{0:T(128)S(1)} %get-tuple-element.365.meta_ref, s32[1,512]{1,0:T(1,128)S(1)} %get-tuple-element.366.valid_ref, s32[512,1]{1,0:T(8,128)S(1)} %get-tuple-element.367.seg_ref, ...), custom_call_target="tpu_custom_call", output_to_operand_aliasing={{}: (7, {})} | custom-call | flops 402653184 | bytes 3407872 | tf_op jit(solution)/shard_map/while/body/pallas_call | solution.py:93
  117.6 192.6 %while.29 = (s32[]{:T(128)}, bf16[2,512,128]{2,1,0:T(8,128)(2,1)S(1)}, bf16[2,512,128]{2,1,0:T(8,128)(2,1)S(1)}, f32[4,512,128]{2,1,0:T(8,128)S(1)}, s32[3]{0:T(...) while((s32[]{:T(128)}, ...), condition=%wide.region_5.6_spmd, body=%wide.region_4.5_spmd.sunk | while | flops 402653184 | bytes 8650989 | solution.py:218
  117.6 2.0 collective-permute-start.2
  119.7 3.1 collective-permute-start.3
  122.8 8.9 %body.5 = f32[4,512,128]{2,1,0:T(8,128)S(1)} custom-call(s32[1]{0:T(128)} %bitcast.62.step_ref, s32[3]{0:T(128)S(1)} %get-tuple-element.392.meta_ref, s32[1,512]{1,0:T(1,128)S(1)} %get-tuple-element.393.valid_ref, s32[512,1]{1,0:T(8,128)S(1)} %get-tuple-element.394.seg_ref, ...), custom_call_target="tpu_custom_call", output_to_operand_aliasing={{}: (7, {})} | custom-call | flops 402653184 | bytes 3407872 | tf_op jit(solution)/shard_map/while/body/pallas_call | solution.py:93
  131.8 2.0 collective-permute-start.2
  133.8 1.9 collective-permute-start.3
  135.8 8.9 %body.5 = f32[4,512,128]{2,1,0:T(8,128)S(1)} custom-call(s32[1]{0:T(128)} %bitcast.62.step_ref, s32[3]{0:T(128)S(1)} %get-tuple-element.392.meta_ref, s32[1,512]{1,0:T(1,128)S(1)} %get-tuple-element.393.valid_ref, s32[512,1]{1,0:T(8,128)S(1)} %get-tuple-element.394.seg_ref, ...), custom_call_target="tpu_custom_call", output_to_operand_aliasing={{}: (7, {})} | custom-call | flops 402653184 | bytes 3407872 | tf_op jit(solution)/shard_map/while/body/pallas_call | solution.py:93
  144.7 4.0 %collective-permute-start.2 = (bf16[2,512,128]{2,1,0:T(8,128)(2,1)S(1)}, bf16[2,512,128]{2,1,0:T(8,128)(2,1)S(1)}, u32[]{:S(2)}, u32[]{:S(2)}) collective-permute-start(bf16[2,512,128]{2,1,0:T(8,128)(2,1)S(1)} %copy.173.kv_a_ref), channel_id=1, source_target_pairs={{0,4},{4,8},{8,12},{12,16},{16,20},{20,24},{24,28},{28,32},{32,36}... | collective-permute-start | bytes 786440 | tf_op jit(solution)/shard_map/while/body/ppermute | solution.py:211
  148.8 6.3 %collective-permute-start.3 = (bf16[2,512,128]{2,1,0:T(8,128)(2,1)S(1)}, bf16[2,512,128]{2,1,0:T(8,128)(2,1)S(1)}, u32[]{:S(2)}, u32[]{:S(2)}) collective-permute-start(bf16[2,512,128]{2,1,0:T(8,128)(2,1)S(1)} %copy.174.kv_b_ref), channel_id=1, source_target_pairs={{0,4},{4,8},{8,12},{12,16},{16,20},{20,24},{24,28},{28,32},{32,36}... | collective-permute-start | bytes 786440 | tf_op jit(solution)/shard_map/while/body/ppermute | solution.py:211
  155.1 8.9 %body.5 = f32[4,512,128]{2,1,0:T(8,128)S(1)} custom-call(s32[1]{0:T(128)} %bitcast.62.step_ref, s32[3]{0:T(128)S(1)} %get-tuple-element.392.meta_ref, s32[1,512]{1,0:T(1,128)S(1)} %get-tuple-element.393.valid_ref, s32[512,1]{1,0:T(8,128)S(1)} %get-tuple-element.394.seg_ref, ...), custom_call_target="tpu_custom_call", output_to_operand_aliasing={{}: (7, {})} | custom-call | flops 402653184 | bytes 3407872 | tf_op jit(solution)/shard_map/while/body/pallas_call | solution.py:93
  164.1 8.3 %collective-permute-start.2 = (bf16[2,512,128]{2,1,0:T(8,128)(2,1)S(1)}, bf16[2,512,128]{2,1,0:T(8,128)(2,1)S(1)}, u32[]{:S(2)}, u32[]{:S(2)}) collective-permute-start(bf16[2,512,128]{2,1,0:T(8,128)(2,1)S(1)} %copy.173.kv_a_ref), channel_id=1, source_target_pairs={{0,4},{4,8},{8,12},{12,16},{16,20},{20,24},{24,28},{28,32},{32,36}... | collective-permute-start | bytes 786440 | tf_op jit(solution)/shard_map/while/body/ppermute | solution.py:211
  174.4 9.3 %body.5 = f32[4,512,128]{2,1,0:T(8,128)S(1)} custom-call(s32[1]{0:T(128)} %bitcast.62.step_ref, s32[3]{0:T(128)S(1)} %get-tuple-element.392.meta_ref, s32[1,512]{1,0:T(1,128)S(1)} %get-tuple-element.393.valid_ref, s32[512,1]{1,0:T(8,128)S(1)} %get-tuple-element.394.seg_ref, ...), custom_call_target="tpu_custom_call", output_to_operand_aliasing={{}: (7, {})} | custom-call | flops 402653184 | bytes 3407872 | tf_op jit(solution)/shard_map/while/body/pallas_call | solution.py:93
  187.7 2.8 body.5
  190.5 3.0 collective-permute-done.2
  193.6 2.8 collective-permute-done.3
  196.4 2.2 collective-permute-start.2
  198.6 1.9 collective-permute-start.3
  200.6 2.8 body.5
  203.4 2.8 collective-permute-done.2
  206.2 2.8 collective-permute-done.3
  211.0 2.4 collective-permute-start.3
  213.4 2.8 body.5
  216.3 2.6 collective-permute-done.2
  218.9 2.8 collective-permute-done.3
  223.7 1.9 collective-permute-start.3
  225.6 2.8 body.5
  228.5 3.0 collective-permute-done.2
  231.5 2.8 collective-permute-done.3
  234.4 1.9 collective-permute-start.2
  238.3 2.8 body.5
  241.1 3.0 collective-permute-done.2
  244.2 2.8 collective-permute-done.3
  250.9 2.8 body.5
  253.8 3.0 collective-permute-done.2
  256.8 2.8 collective-permute-done.3
  263.6 2.8 body.5
  266.4 3.0 collective-permute-done.2
  269.4 2.8 collective-permute-done.3
  276.2 2.8 body.5
  279.1 3.0 collective-permute-done.2
  282.1 2.8 collective-permute-done.3
  288.8 2.8 body.5
  291.7 3.0 collective-permute-done.2
  294.7 2.8 collective-permute-done.3
  301.5 2.8 body.5
  304.3 3.0 collective-permute-done.2
  307.4 2.8 collective-permute-done.3
  313.8 4.7 %all-to-all-start.2 = ((bf16[4,512,256]{2,1,0:T(8,128)(2,1)}), bf16[4,512,256]{2,1,0:T(8,128)(2,1)}, u32[]{:S(2)}, u32[]{:S(2)}) async-start(bf16[4,512,256]{2,1,0:T(8,128)(2,1)} %broadcast_in_dim.103), calls=%async_computation.2 | async-start | bytes 2097152 | tf_op jit(solution)/shard_map/all_to_all | solution.py:108
  323.7 14.0 %all-to-all-done.2 = bf16[4,512,256]{2,1,0:T(8,128)(2,1)} async-done(((bf16[4,512,256]{2,1,0:T(8,128)(2,1)}), bf16[4,512,256]{2,1,0:T(8,128)(2,1)}, u32[]{:S(2)}, u32[]{:S(2)}) %all-to-all-start.2) | async-done | bytes 1048608 | tf_op jit(solution)/shard_map/all_to_all | solution.py:108
  337.7 3.0 fusion.4
  (205 shorter events, 60.8 us)
Async XLA Ops:
  3.2 6.1 %copy-start.18 = (s32[4]{0:T(128)S(1)}, s32[4]{0:T(128)}, u32[]{:S(2)}) copy-start(s32[4]{0:T(128)} %param.21) | copy-start | bytes 52
  3.2 8.0 %copy-start.16 = (s32[512]{0:T(512)S(1)}, s32[512]{0:T(512)}, u32[]{:S(2)}) copy-start(s32[512]{0:T(512)} %param.19) | copy-start | bytes 6148
  3.2 10.6 %copy-start.17 = (f32[2048]{0:T(1024)S(1)}, f32[2048]{0:T(1024)}, u32[]{:S(2)}) copy-start(f32[2048]{0:T(1024)} %param.14) | copy-start | bytes 24580
  3.2 10.6 %copy-start.7 = (bf16[2048,256]{1,0:T(8,128)(2,1)S(1)}, bf16[2048,256]{1,0:T(8,128)(2,1)}, u32[]{:S(2)}) copy-start(bf16[2048,256]{1,0:T(8,128)(2,1)} %param.15) | copy-start | bytes 3145732
  3.2 54.2 %all-to-all-start = ((bf16[4,512,512]{2,1,0:T(8,128)(2,1)}), bf16[4,512,512]{2,1,0:T(8,128)(2,1)S(1)}, u32[]{:S(2)}, u32[]{:S(2)}) async-start(bf16[4,512,512]{2,1,0:T(8,128)(2,1)} %broadcast_in_dim.94), calls=%async_computation | async-start | bytes 4194304 | tf_op jit(solution)/shard_map/all_to_all | solution.py:108
  9.2 82.6 %collective-permute-start.6 = (s32[4]{0:T(128)S(1)}, s32[4]{0:T(128)S(1)}, u32[]{:S(2)}, u32[]{:S(2)}) collective-permute-start(s32[4]{0:T(128)S(1)} %copy-done.18), channel_id=1, source_target_pairs={{0,4},{4,8},{8,12},{12,16},{16,20},{20,24},{24,28},{28,32},{32,36}... | collective-permute-start | bytes 56 | tf_op jit(solution)/shard_map/ppermute | solution.py:115
  19.9 3.5 %copy-start.15 = (s32[512]{0:T(512)S(1)}, s32[512]{0:T(512)}, u32[]{:S(2)}) copy-start(s32[512]{0:T(512)} %param.20) | copy-start | bytes 6148
  58.8 22.8 %all-to-all-start.1 = ((s32[64,1,1]{2,1,0:T(1,128)}), s32[64,1,1]{2,1,0:T(1,128)S(1)}, u32[]{:S(2)}, u32[]{:S(2)}) async-start(s32[64,1,1]{2,1,0:T(1,128)} %broadcast_in_dim.95), calls=%async_computation.1 | async-start | bytes 65536 | tf_op jit(solution)/shard_map/all_to_all | solution.py:154
  81.8 230.9 %all-to-all-start.3 = ((bf16[256,4,512]{2,0,1:T(8,128)(2,1)}), bf16[256,4,512]{2,0,1:T(8,128)(2,1)}, u32[]{:S(2)}, u32[]{:S(2)}) async-start(bf16[256,4,512]{2,0,1:T(8,128)(2,1)} %copy.137), calls=%async_computation.3 | async-start | bytes 2097152 | tf_op jit(solution)/shard_map/all_to_all | solution.py:183
  86.2 7.5 %copy-start.12 = (bf16[2,512,128]{2,1,0:T(8,128)(2,1)}, bf16[2,512,128]{2,1,0:T(8,128)(2,1)S(1)}, u32[]{:S(2)}) copy-start(bf16[2,512,128]{2,1,0:T(8,128)(2,1)S(1)} %get-tuple-element.227.kv_b_ref) | copy-start | bytes 786436
  86.2 7.5 %copy-start.13 = (bf16[2,512,128]{2,1,0:T(8,128)(2,1)}, bf16[2,512,128]{2,1,0:T(8,128)(2,1)S(1)}, u32[]{:S(2)}) copy-start(bf16[2,512,128]{2,1,0:T(8,128)(2,1)S(1)} %get-tuple-element.228.kv_a_ref) | copy-start | bytes 786436
  86.2 16.8 %collective-permute-start.4 = (bf16[2,512,128]{2,1,0:T(8,128)(2,1)S(1)}, bf16[2,512,128]{2,1,0:T(8,128)(2,1)S(1)}, u32[]{:S(2)}, u32[]{:S(2)}) collective-permute-start(bf16[2,512,128]{2,1,0:T(8,128)(2,1)S(1)} %get-tuple-element.228.kv_a_ref), channel_id=1, source_target_pairs={{0,4},{4,8},{8,12},{12,16},{16,20},{20,24},{24,28},{28,32},{32,36}... | collective-permute-start | bytes 786440 | tf_op jit(solution)/shard_map/ppermute | solution.py:205
  88.3 14.8 %collective-permute-start.5 = (bf16[2,512,128]{2,1,0:T(8,128)(2,1)S(1)}, bf16[2,512,128]{2,1,0:T(8,128)(2,1)S(1)}, u32[]{:S(2)}, u32[]{:S(2)}) collective-permute-start(bf16[2,512,128]{2,1,0:T(8,128)(2,1)S(1)} %get-tuple-element.227.kv_b_ref), channel_id=1, source_target_pairs={{0,4},{4,8},{8,12},{12,16},{16,20},{20,24},{24,28},{28,32},{32,36}... | collective-permute-start | bytes 786440 | tf_op jit(solution)/shard_map/ppermute | solution.py:205
  103.1 5.5 %copy-start = (bf16[2,512,128]{2,1,0:T(8,128)(2,1)}, bf16[2,512,128]{2,1,0:T(8,128)(2,1)S(1)}, u32[]{:S(2)}) copy-start(bf16[2,512,128]{2,1,0:T(8,128)(2,1)S(1)} %copy.161.kv_a_ref) | copy-start | bytes 786436 | tf_op jit(solution)/shard_map/while
  103.2 14.4 %collective-permute-start = (bf16[2,512,128]{2,1,0:T(8,128)(2,1)S(1)}, bf16[2,512,128]{2,1,0:T(8,128)(2,1)S(1)}, u32[]{:S(2)}, u32[]{:S(2)}) collective-permute-start(bf16[2,512,128]{2,1,0:T(8,128)(2,1)S(1)} %copy.161.kv_a_ref), channel_id=1, source_target_pairs={{0,4},{4,8},{8,12},{12,16},{16,20},{20,24},{24,28},{28,32},{32,36}... | collective-permute-start | bytes 786440 | tf_op jit(solution)/shard_map/while/body/ppermute | solution.py:211
  105.2 3.4 %copy-start.2 = (bf16[2,512,128]{2,1,0:T(8,128)(2,1)}, bf16[2,512,128]{2,1,0:T(8,128)(2,1)S(1)}, u32[]{:S(2)}) copy-start(bf16[2,512,128]{2,1,0:T(8,128)(2,1)S(1)} %copy.162.kv_b_ref) | copy-start | bytes 786436 | tf_op jit(solution)/shard_map/while
  105.2 12.3 %collective-permute-start.1 = (bf16[2,512,128]{2,1,0:T(8,128)(2,1)S(1)}, bf16[2,512,128]{2,1,0:T(8,128)(2,1)S(1)}, u32[]{:S(2)}, u32[]{:S(2)}) collective-permute-start(bf16[2,512,128]{2,1,0:T(8,128)(2,1)S(1)} %copy.162.kv_b_ref), channel_id=1, source_target_pairs={{0,4},{4,8},{8,12},{12,16},{16,20},{20,24},{24,28},{28,32},{32,36}... | collective-permute-start | bytes 786440 | tf_op jit(solution)/shard_map/while/body/ppermute | solution.py:211
  117.6 5.2 %copy-start.1 = (bf16[2,512,128]{2,1,0:T(8,128)(2,1)}, bf16[2,512,128]{2,1,0:T(8,128)(2,1)S(1)}, u32[]{:S(2)}) copy-start(bf16[2,512,128]{2,1,0:T(8,128)(2,1)S(1)} %copy.173.kv_a_ref) | copy-start | bytes 786436 | tf_op jit(solution)/shard_map/while
  117.6 14.1 %collective-permute-start.2 = (bf16[2,512,128]{2,1,0:T(8,128)(2,1)S(1)}, bf16[2,512,128]{2,1,0:T(8,128)(2,1)S(1)}, u32[]{:S(2)}, u32[]{:S(2)}) collective-permute-start(bf16[2,512,128]{2,1,0:T(8,128)(2,1)S(1)} %copy.173.kv_a_ref), channel_id=1, source_target_pairs={{0,4},{4,8},{8,12},{12,16},{16,20},{20,24},{24,28},{28,32},{32,36}... | collective-permute-start | bytes 786440 | tf_op jit(solution)/shard_map/while/body/ppermute | solution.py:211
  119.7 3.1 copy-start.3
  119.7 12.0 %collective-permute-start.3 = (bf16[2,512,128]{2,1,0:T(8,128)(2,1)S(1)}, bf16[2,512,128]{2,1,0:T(8,128)(2,1)S(1)}, u32[]{:S(2)}, u32[]{:S(2)}) collective-permute-start(bf16[2,512,128]{2,1,0:T(8,128)(2,1)S(1)} %copy.174.kv_b_ref), channel_id=1, source_target_pairs={{0,4},{4,8},{8,12},{12,16},{16,20},{20,24},{24,28},{28,32},{32,36}... | collective-permute-start | bytes 786440 | tf_op jit(solution)/shard_map/while/body/ppermute | solution.py:211
  131.7 4.0 %copy-start.1 = (bf16[2,512,128]{2,1,0:T(8,128)(2,1)}, bf16[2,512,128]{2,1,0:T(8,128)(2,1)S(1)}, u32[]{:S(2)}) copy-start(bf16[2,512,128]{2,1,0:T(8,128)(2,1)S(1)} %copy.173.kv_a_ref) | copy-start | bytes 786436 | tf_op jit(solution)/shard_map/while
  131.8 12.9 %collective-permute-start.2 = (bf16[2,512,128]{2,1,0:T(8,128)(2,1)S(1)}, bf16[2,512,128]{2,1,0:T(8,128)(2,1)S(1)}, u32[]{:S(2)}, u32[]{:S(2)}) collective-permute-start(bf16[2,512,128]{2,1,0:T(8,128)(2,1)S(1)} %copy.173.kv_a_ref), channel_id=1, source_target_pairs={{0,4},{4,8},{8,12},{12,16},{16,20},{20,24},{24,28},{28,32},{32,36}... | collective-permute-start | bytes 786440 | tf_op jit(solution)/shard_map/while/body/ppermute | solution.py:211
  133.8 10.8 %collective-permute-start.3 = (bf16[2,512,128]{2,1,0:T(8,128)(2,1)S(1)}, bf16[2,512,128]{2,1,0:T(8,128)(2,1)S(1)}, u32[]{:S(2)}, u32[]{:S(2)}) collective-permute-start(bf16[2,512,128]{2,1,0:T(8,128)(2,1)S(1)} %copy.174.kv_b_ref), channel_id=1, source_target_pairs={{0,4},{4,8},{8,12},{12,16},{16,20},{20,24},{24,28},{28,32},{32,36}... | collective-permute-start | bytes 786440 | tf_op jit(solution)/shard_map/while/body/ppermute | solution.py:211
  144.7 10.4 %copy-start.1 = (bf16[2,512,128]{2,1,0:T(8,128)(2,1)}, bf16[2,512,128]{2,1,0:T(8,128)(2,1)S(1)}, u32[]{:S(2)}) copy-start(bf16[2,512,128]{2,1,0:T(8,128)(2,1)S(1)} %copy.173.kv_a_ref) | copy-start | bytes 786436 | tf_op jit(solution)/shard_map/while
  144.7 19.3 %collective-permute-start.2 = (bf16[2,512,128]{2,1,0:T(8,128)(2,1)S(1)}, bf16[2,512,128]{2,1,0:T(8,128)(2,1)S(1)}, u32[]{:S(2)}, u32[]{:S(2)}) collective-permute-start(bf16[2,512,128]{2,1,0:T(8,128)(2,1)S(1)} %copy.173.kv_a_ref), channel_id=1, source_target_pairs={{0,4},{4,8},{8,12},{12,16},{16,20},{20,24},{24,28},{28,32},{32,36}... | collective-permute-start | bytes 786440 | tf_op jit(solution)/shard_map/while/body/ppermute | solution.py:211
  148.8 6.3 %copy-start.3 = (bf16[2,512,128]{2,1,0:T(8,128)(2,1)}, bf16[2,512,128]{2,1,0:T(8,128)(2,1)S(1)}, u32[]{:S(2)}) copy-start(bf16[2,512,128]{2,1,0:T(8,128)(2,1)S(1)} %copy.174.kv_b_ref) | copy-start | bytes 786436 | tf_op jit(solution)/shard_map/while
  148.8 15.2 %collective-permute-start.3 = (bf16[2,512,128]{2,1,0:T(8,128)(2,1)S(1)}, bf16[2,512,128]{2,1,0:T(8,128)(2,1)S(1)}, u32[]{:S(2)}, u32[]{:S(2)}) collective-permute-start(bf16[2,512,128]{2,1,0:T(8,128)(2,1)S(1)} %copy.174.kv_b_ref), channel_id=1, source_target_pairs={{0,4},{4,8},{8,12},{12,16},{16,20},{20,24},{24,28},{28,32},{32,36}... | collective-permute-start | bytes 786440 | tf_op jit(solution)/shard_map/while/body/ppermute | solution.py:211
  164.1 10.3 %copy-start.1 = (bf16[2,512,128]{2,1,0:T(8,128)(2,1)}, bf16[2,512,128]{2,1,0:T(8,128)(2,1)S(1)}, u32[]{:S(2)}) copy-start(bf16[2,512,128]{2,1,0:T(8,128)(2,1)S(1)} %copy.173.kv_a_ref) | copy-start | bytes 786436 | tf_op jit(solution)/shard_map/while
  164.1 19.6 %collective-permute-start.2 = (bf16[2,512,128]{2,1,0:T(8,128)(2,1)S(1)}, bf16[2,512,128]{2,1,0:T(8,128)(2,1)S(1)}, u32[]{:S(2)}, u32[]{:S(2)}) collective-permute-start(bf16[2,512,128]{2,1,0:T(8,128)(2,1)S(1)} %copy.173.kv_a_ref), channel_id=1, source_target_pairs={{0,4},{4,8},{8,12},{12,16},{16,20},{20,24},{24,28},{28,32},{32,36}... | collective-permute-start | bytes 786440 | tf_op jit(solution)/shard_map/while/body/ppermute | solution.py:211
  172.4 11.3 %collective-permute-start.3 = (bf16[2,512,128]{2,1,0:T(8,128)(2,1)S(1)}, bf16[2,512,128]{2,1,0:T(8,128)(2,1)S(1)}, u32[]{:S(2)}, u32[]{:S(2)}) collective-permute-start(bf16[2,512,128]{2,1,0:T(8,128)(2,1)S(1)} %copy.174.kv_b_ref), channel_id=1, source_target_pairs={{0,4},{4,8},{8,12},{12,16},{16,20},{20,24},{24,28},{28,32},{32,36}... | collective-permute-start | bytes 786440 | tf_op jit(solution)/shard_map/while/body/ppermute | solution.py:211
  183.8 3.9 %copy-start.1 = (bf16[2,512,128]{2,1,0:T(8,128)(2,1)}, bf16[2,512,128]{2,1,0:T(8,128)(2,1)S(1)}, u32[]{:S(2)}) copy-start(bf16[2,512,128]{2,1,0:T(8,128)(2,1)S(1)} %copy.173.kv_a_ref) | copy-start | bytes 786436 | tf_op jit(solution)/shard_map/while
  183.8 9.8 %collective-permute-start.2 = (bf16[2,512,128]{2,1,0:T(8,128)(2,1)S(1)}, bf16[2,512,128]{2,1,0:T(8,128)(2,1)S(1)}, u32[]{:S(2)}, u32[]{:S(2)}) collective-permute-start(bf16[2,512,128]{2,1,0:T(8,128)(2,1)S(1)} %copy.173.kv_a_ref), channel_id=1, source_target_pairs={{0,4},{4,8},{8,12},{12,16},{16,20},{20,24},{24,28},{28,32},{32,36}... | collective-permute-start | bytes 786440 | tf_op jit(solution)/shard_map/while/body/ppermute | solution.py:211
  185.7 10.6 %collective-permute-start.3 = (bf16[2,512,128]{2,1,0:T(8,128)(2,1)S(1)}, bf16[2,512,128]{2,1,0:T(8,128)(2,1)S(1)}, u32[]{:S(2)}, u32[]{:S(2)}) collective-permute-start(bf16[2,512,128]{2,1,0:T(8,128)(2,1)S(1)} %copy.174.kv_b_ref), channel_id=1, source_target_pairs={{0,4},{4,8},{8,12},{12,16},{16,20},{20,24},{24,28},{28,32},{32,36}... | collective-permute-start | bytes 786440 | tf_op jit(solution)/shard_map/while/body/ppermute | solution.py:211
  196.4 4.1 %copy-start.1 = (bf16[2,512,128]{2,1,0:T(8,128)(2,1)}, bf16[2,512,128]{2,1,0:T(8,128)(2,1)S(1)}, u32[]{:S(2)}) copy-start(bf16[2,512,128]{2,1,0:T(8,128)(2,1)S(1)} %copy.173.kv_a_ref) | copy-start | bytes 786436 | tf_op jit(solution)/shard_map/while
  196.4 9.8 %collective-permute-start.2 = (bf16[2,512,128]{2,1,0:T(8,128)(2,1)S(1)}, bf16[2,512,128]{2,1,0:T(8,128)(2,1)S(1)}, u32[]{:S(2)}, u32[]{:S(2)}) collective-permute-start(bf16[2,512,128]{2,1,0:T(8,128)(2,1)S(1)} %copy.173.kv_a_ref), channel_id=1, source_target_pairs={{0,4},{4,8},{8,12},{12,16},{16,20},{20,24},{24,28},{28,32},{32,36}... | collective-permute-start | bytes 786440 | tf_op jit(solution)/shard_map/while/body/ppermute | solution.py:211
  198.6 10.4 %collective-permute-start.3 = (bf16[2,512,128]{2,1,0:T(8,128)(2,1)S(1)}, bf16[2,512,128]{2,1,0:T(8,128)(2,1)S(1)}, u32[]{:S(2)}, u32[]{:S(2)}) collective-permute-start(bf16[2,512,128]{2,1,0:T(8,128)(2,1)S(1)} %copy.174.kv_b_ref), channel_id=1, source_target_pairs={{0,4},{4,8},{8,12},{12,16},{16,20},{20,24},{24,28},{28,32},{32,36}... | collective-permute-start | bytes 786440 | tf_op jit(solution)/shard_map/while/body/ppermute | solution.py:211
  209.1 4.4 %copy-start.1 = (bf16[2,512,128]{2,1,0:T(8,128)(2,1)}, bf16[2,512,128]{2,1,0:T(8,128)(2,1)S(1)}, u32[]{:S(2)}) copy-start(bf16[2,512,128]{2,1,0:T(8,128)(2,1)S(1)} %copy.173.kv_a_ref) | copy-start | bytes 786436 | tf_op jit(solution)/shard_map/while
  209.1 9.8 %collective-permute-start.2 = (bf16[2,512,128]{2,1,0:T(8,128)(2,1)S(1)}, bf16[2,512,128]{2,1,0:T(8,128)(2,1)S(1)}, u32[]{:S(2)}, u32[]{:S(2)}) collective-permute-start(bf16[2,512,128]{2,1,0:T(8,128)(2,1)S(1)} %copy.173.kv_a_ref), channel_id=1, source_target_pairs={{0,4},{4,8},{8,12},{12,16},{16,20},{20,24},{24,28},{28,32},{32,36}... | collective-permute-start | bytes 786440 | tf_op jit(solution)/shard_map/while/body/ppermute | solution.py:211
  211.0 10.6 %collective-permute-start.3 = (bf16[2,512,128]{2,1,0:T(8,128)(2,1)S(1)}, bf16[2,512,128]{2,1,0:T(8,128)(2,1)S(1)}, u32[]{:S(2)}, u32[]{:S(2)}) collective-permute-start(bf16[2,512,128]{2,1,0:T(8,128)(2,1)S(1)} %copy.174.kv_b_ref), channel_id=1, source_target_pairs={{0,4},{4,8},{8,12},{12,16},{16,20},{20,24},{24,28},{28,32},{32,36}... | collective-permute-start | bytes 786440 | tf_op jit(solution)/shard_map/while/body/ppermute | solution.py:211
  221.7 3.9 %copy-start.1 = (bf16[2,512,128]{2,1,0:T(8,128)(2,1)}, bf16[2,512,128]{2,1,0:T(8,128)(2,1)S(1)}, u32[]{:S(2)}) copy-start(bf16[2,512,128]{2,1,0:T(8,128)(2,1)S(1)} %copy.173.kv_a_ref) | copy-start | bytes 786436 | tf_op jit(solution)/shard_map/while
  221.7 9.8 %collective-permute-start.2 = (bf16[2,512,128]{2,1,0:T(8,128)(2,1)S(1)}, bf16[2,512,128]{2,1,0:T(8,128)(2,1)S(1)}, u32[]{:S(2)}, u32[]{:S(2)}) collective-permute-start(bf16[2,512,128]{2,1,0:T(8,128)(2,1)S(1)} %copy.173.kv_a_ref), channel_id=1, source_target_pairs={{0,4},{4,8},{8,12},{12,16},{16,20},{20,24},{24,28},{28,32},{32,36}... | collective-permute-start | bytes 786440 | tf_op jit(solution)/shard_map/while/body/ppermute | solution.py:211
  223.7 10.6 %collective-permute-start.3 = (bf16[2,512,128]{2,1,0:T(8,128)(2,1)S(1)}, bf16[2,512,128]{2,1,0:T(8,128)(2,1)S(1)}, u32[]{:S(2)}, u32[]{:S(2)}) collective-permute-start(bf16[2,512,128]{2,1,0:T(8,128)(2,1)S(1)} %copy.174.kv_b_ref), channel_id=1, source_target_pairs={{0,4},{4,8},{8,12},{12,16},{16,20},{20,24},{24,28},{28,32},{32,36}... | collective-permute-start | bytes 786440 | tf_op jit(solution)/shard_map/while/body/ppermute | solution.py:211
  234.3 3.9 %copy-start.1 = (bf16[2,512,128]{2,1,0:T(8,128)(2,1)}, bf16[2,512,128]{2,1,0:T(8,128)(2,1)S(1)}, u32[]{:S(2)}) copy-start(bf16[2,512,128]{2,1,0:T(8,128)(2,1)S(1)} %copy.173.kv_a_ref) | copy-start | bytes 786436 | tf_op jit(solution)/shard_map/while
  234.4 9.8 %collective-permute-start.2 = (bf16[2,512,128]{2,1,0:T(8,128)(2,1)S(1)}, bf16[2,512,128]{2,1,0:T(8,128)(2,1)S(1)}, u32[]{:S(2)}, u32[]{:S(2)}) collective-permute-start(bf16[2,512,128]{2,1,0:T(8,128)(2,1)S(1)} %copy.173.kv_a_ref), channel_id=1, source_target_pairs={{0,4},{4,8},{8,12},{12,16},{16,20},{20,24},{24,28},{28,32},{32,36}... | collective-permute-start | bytes 786440 | tf_op jit(solution)/shard_map/while/body/ppermute | solution.py:211
  236.3 10.6 %collective-permute-start.3 = (bf16[2,512,128]{2,1,0:T(8,128)(2,1)S(1)}, bf16[2,512,128]{2,1,0:T(8,128)(2,1)S(1)}, u32[]{:S(2)}, u32[]{:S(2)}) collective-permute-start(bf16[2,512,128]{2,1,0:T(8,128)(2,1)S(1)} %copy.174.kv_b_ref), channel_id=1, source_target_pairs={{0,4},{4,8},{8,12},{12,16},{16,20},{20,24},{24,28},{28,32},{32,36}... | collective-permute-start | bytes 786440 | tf_op jit(solution)/shard_map/while/body/ppermute | solution.py:211
  247.0 3.9 %copy-start.1 = (bf16[2,512,128]{2,1,0:T(8,128)(2,1)}, bf16[2,512,128]{2,1,0:T(8,128)(2,1)S(1)}, u32[]{:S(2)}) copy-start(bf16[2,512,128]{2,1,0:T(8,128)(2,1)S(1)} %copy.173.kv_a_ref) | copy-start | bytes 786436 | tf_op jit(solution)/shard_map/while
  247.0 9.8 %collective-permute-start.2 = (bf16[2,512,128]{2,1,0:T(8,128)(2,1)S(1)}, bf16[2,512,128]{2,1,0:T(8,128)(2,1)S(1)}, u32[]{:S(2)}, u32[]{:S(2)}) collective-permute-start(bf16[2,512,128]{2,1,0:T(8,128)(2,1)S(1)} %copy.173.kv_a_ref), channel_id=1, source_target_pairs={{0,4},{4,8},{8,12},{12,16},{16,20},{20,24},{24,28},{28,32},{32,36}... | collective-permute-start | bytes 786440 | tf_op jit(solution)/shard_map/while/body/ppermute | solution.py:211
  249.0 10.6 %collective-permute-start.3 = (bf16[2,512,128]{2,1,0:T(8,128)(2,1)S(1)}, bf16[2,512,128]{2,1,0:T(8,128)(2,1)S(1)}, u32[]{:S(2)}, u32[]{:S(2)}) collective-permute-start(bf16[2,512,128]{2,1,0:T(8,128)(2,1)S(1)} %copy.174.kv_b_ref), channel_id=1, source_target_pairs={{0,4},{4,8},{8,12},{12,16},{16,20},{20,24},{24,28},{28,32},{32,36}... | collective-permute-start | bytes 786440 | tf_op jit(solution)/shard_map/while/body/ppermute | solution.py:211
  259.6 3.9 %copy-start.1 = (bf16[2,512,128]{2,1,0:T(8,128)(2,1)}, bf16[2,512,128]{2,1,0:T(8,128)(2,1)S(1)}, u32[]{:S(2)}) copy-start(bf16[2,512,128]{2,1,0:T(8,128)(2,1)S(1)} %copy.173.kv_a_ref) | copy-start | bytes 786436 | tf_op jit(solution)/shard_map/while
  259.6 9.8 %collective-permute-start.2 = (bf16[2,512,128]{2,1,0:T(8,128)(2,1)S(1)}, bf16[2,512,128]{2,1,0:T(8,128)(2,1)S(1)}, u32[]{:S(2)}, u32[]{:S(2)}) collective-permute-start(bf16[2,512,128]{2,1,0:T(8,128)(2,1)S(1)} %copy.173.kv_a_ref), channel_id=1, source_target_pairs={{0,4},{4,8},{8,12},{12,16},{16,20},{20,24},{24,28},{28,32},{32,36}... | collective-permute-start | bytes 786440 | tf_op jit(solution)/shard_map/while/body/ppermute | solution.py:211
  261.6 10.6 %collective-permute-start.3 = (bf16[2,512,128]{2,1,0:T(8,128)(2,1)S(1)}, bf16[2,512,128]{2,1,0:T(8,128)(2,1)S(1)}, u32[]{:S(2)}, u32[]{:S(2)}) collective-permute-start(bf16[2,512,128]{2,1,0:T(8,128)(2,1)S(1)} %copy.174.kv_b_ref), channel_id=1, source_target_pairs={{0,4},{4,8},{8,12},{12,16},{16,20},{20,24},{24,28},{28,32},{32,36}... | collective-permute-start | bytes 786440 | tf_op jit(solution)/shard_map/while/body/ppermute | solution.py:211
  272.3 3.9 %copy-start.1 = (bf16[2,512,128]{2,1,0:T(8,128)(2,1)}, bf16[2,512,128]{2,1,0:T(8,128)(2,1)S(1)}, u32[]{:S(2)}) copy-start(bf16[2,512,128]{2,1,0:T(8,128)(2,1)S(1)} %copy.173.kv_a_ref) | copy-start | bytes 786436 | tf_op jit(solution)/shard_map/while
  272.3 9.8 %collective-permute-start.2 = (bf16[2,512,128]{2,1,0:T(8,128)(2,1)S(1)}, bf16[2,512,128]{2,1,0:T(8,128)(2,1)S(1)}, u32[]{:S(2)}, u32[]{:S(2)}) collective-permute-start(bf16[2,512,128]{2,1,0:T(8,128)(2,1)S(1)} %copy.173.kv_a_ref), channel_id=1, source_target_pairs={{0,4},{4,8},{8,12},{12,16},{16,20},{20,24},{24,28},{28,32},{32,36}... | collective-permute-start | bytes 786440 | tf_op jit(solution)/shard_map/while/body/ppermute | solution.py:211
  274.3 10.6 %collective-permute-start.3 = (bf16[2,512,128]{2,1,0:T(8,128)(2,1)S(1)}, bf16[2,512,128]{2,1,0:T(8,128)(2,1)S(1)}, u32[]{:S(2)}, u32[]{:S(2)}) collective-permute-start(bf16[2,512,128]{2,1,0:T(8,128)(2,1)S(1)} %copy.174.kv_b_ref), channel_id=1, source_target_pairs={{0,4},{4,8},{8,12},{12,16},{16,20},{20,24},{24,28},{28,32},{32,36}... | collective-permute-start | bytes 786440 | tf_op jit(solution)/shard_map/while/body/ppermute | solution.py:211
  284.9 3.9 %copy-start.1 = (bf16[2,512,128]{2,1,0:T(8,128)(2,1)}, bf16[2,512,128]{2,1,0:T(8,128)(2,1)S(1)}, u32[]{:S(2)}) copy-start(bf16[2,512,128]{2,1,0:T(8,128)(2,1)S(1)} %copy.173.kv_a_ref) | copy-start | bytes 786436 | tf_op jit(solution)/shard_map/while
  284.9 9.8 %collective-permute-start.2 = (bf16[2,512,128]{2,1,0:T(8,128)(2,1)S(1)}, bf16[2,512,128]{2,1,0:T(8,128)(2,1)S(1)}, u32[]{:S(2)}, u32[]{:S(2)}) collective-permute-start(bf16[2,512,128]{2,1,0:T(8,128)(2,1)S(1)} %copy.173.kv_a_ref), channel_id=1, source_target_pairs={{0,4},{4,8},{8,12},{12,16},{16,20},{20,24},{24,28},{28,32},{32,36}... | collective-permute-start | bytes 786440 | tf_op jit(solution)/shard_map/while/body/ppermute | solution.py:211
  286.9 10.6 %collective-permute-start.3 = (bf16[2,512,128]{2,1,0:T(8,128)(2,1)S(1)}, bf16[2,512,128]{2,1,0:T(8,128)(2,1)S(1)}, u32[]{:S(2)}, u32[]{:S(2)}) collective-permute-start(bf16[2,512,128]{2,1,0:T(8,128)(2,1)S(1)} %copy.174.kv_b_ref), channel_id=1, source_target_pairs={{0,4},{4,8},{8,12},{12,16},{16,20},{20,24},{24,28},{28,32},{32,36}... | collective-permute-start | bytes 786440 | tf_op jit(solution)/shard_map/while/body/ppermute | solution.py:211
  297.6 3.9 %copy-start.1 = (bf16[2,512,128]{2,1,0:T(8,128)(2,1)}, bf16[2,512,128]{2,1,0:T(8,128)(2,1)S(1)}, u32[]{:S(2)}) copy-start(bf16[2,512,128]{2,1,0:T(8,128)(2,1)S(1)} %copy.173.kv_a_ref) | copy-start | bytes 786436 | tf_op jit(solution)/shard_map/while
  297.6 9.8 %collective-permute-start.2 = (bf16[2,512,128]{2,1,0:T(8,128)(2,1)S(1)}, bf16[2,512,128]{2,1,0:T(8,128)(2,1)S(1)}, u32[]{:S(2)}, u32[]{:S(2)}) collective-permute-start(bf16[2,512,128]{2,1,0:T(8,128)(2,1)S(1)} %copy.173.kv_a_ref), channel_id=1, source_target_pairs={{0,4},{4,8},{8,12},{12,16},{16,20},{20,24},{24,28},{28,32},{32,36}... | collective-permute-start | bytes 786440 | tf_op jit(solution)/shard_map/while/body/ppermute | solution.py:211
  299.5 10.6 %collective-permute-start.3 = (bf16[2,512,128]{2,1,0:T(8,128)(2,1)S(1)}, bf16[2,512,128]{2,1,0:T(8,128)(2,1)S(1)}, u32[]{:S(2)}, u32[]{:S(2)}) collective-permute-start(bf16[2,512,128]{2,1,0:T(8,128)(2,1)S(1)} %copy.174.kv_b_ref), channel_id=1, source_target_pairs={{0,4},{4,8},{8,12},{12,16},{16,20},{20,24},{24,28},{28,32},{32,36}... | collective-permute-start | bytes 786440 | tf_op jit(solution)/shard_map/while/body/ppermute | solution.py:211
  312.5 6.8 %copy-start.5 = (bf16[512,4,2,64]{3,0,1,2:T(8,128)(2,1)S(1)}, bf16[512,4,2,64]{3,0,1,2:T(8,128)(2,1)}, u32[]{:S(2)}) copy-start(bf16[512,4,2,64]{3,0,1,2:T(8,128)(2,1)} %copy-done.4) | copy-start | bytes 1572868
  313.8 23.9 %all-to-all-start.2 = ((bf16[4,512,256]{2,1,0:T(8,128)(2,1)}), bf16[4,512,256]{2,1,0:T(8,128)(2,1)}, u32[]{:S(2)}, u32[]{:S(2)}) async-start(bf16[4,512,256]{2,1,0:T(8,128)(2,1)} %broadcast_in_dim.103), calls=%async_computation.2 | async-start | bytes 2097152 | tf_op jit(solution)/shard_map/all_to_all | solution.py:108
  322.0 15.7 %copy-start.14 = (bf16[512,512]{1,0:T(8,128)(2,1)S(1)}, bf16[512,512]{1,0:T(8,128)(2,1)}, u32[]{:S(2)}) copy-start(bf16[512,512]{1,0:T(8,128)(2,1)} %param.13) | copy-start | bytes 1572868
  (18 other events, 32.4 us)

commit v2 on v1

--- a/solution.py
+++ b/solution.py
@@ -16,9 +16,9 @@
 FAR = 1 << 30
 
 
-def _step_kernel(step_ref, meta_ref, valid_ref, seg_ref, q_ref, kv_a_ref, kv_b_ref, s_ref, out_ref):
+def _step_kernel(step_ref, meta_ref, valid_ref, seg_ref, q_ref, kv_ref, s_ref, out_ref):
     rows, width = out_ref.shape
-    keys = kv_a_ref.shape[0]
+    keys = kv_ref.shape[0]
     step = step_ref[0]
     qstart = meta_ref[0]
     check_valid = jnp.where(step == 0, meta_ref[1], 0)
@@ -27,11 +27,10 @@
     seg_first = seg_ref[0, 0]
     none_allowed = kstart + keys - 1 < seg_first
     all_allowed = (seg_last <= kstart) & (kstart + keys - 1 <= qstart) & (check_valid == 0)
-    first_half = pl.program_id(0) < 2
 
     def update(allowed):
         q = q_ref[...]
-        kv = jnp.where(first_half, kv_a_ref[...], kv_b_ref[...])
+        kv = kv_ref[...]
         scores = lax.dot_general(
             q, kv[:, :HD], (((1,), (1,)), ((), ())), preferred_element_type=jnp.float32
         ) * SCALE
@@ -71,11 +70,10 @@
         update((kpos >= seg_ref[...]) & (kpos <= tpos))
 
 
-def attend_step(step, meta, valid_row, seg_col, q_hm, kv_a, kv_b, state):
+def attend_step(step, meta, valid_row, seg_col, q_hm, kv_hm, state):
     heads, rows, _ = q_hm.shape
-    part = kv_a.shape[0]
-    keys = kv_a.shape[1]
-    width = kv_a.shape[2]
+    keys = kv_hm.shape[1]
+    width = kv_hm.shape[2]
     grid_spec = pltpu.PrefetchScalarGridSpec(
         num_scalar_prefetch=2,
         grid=(heads,),
@@ -83,8 +81,7 @@
             pl.BlockSpec((1, keys), lambda h, s, m: (0, 0)),
             pl.BlockSpec((rows, 1), lambda h, s, m: (0, 0)),
             pl.BlockSpec((None, rows, HD), lambda h, s, m: (h, 0, 0)),
-            pl.BlockSpec((None, keys, width), lambda h, s, m: (h % part, 0, 0)),
-            pl.BlockSpec((None, keys, width), lambda h, s, m: (h % part, 0, 0)),
+            pl.BlockSpec((None, keys, width), lambda h, s, m: (h, 0, 0)),
             pl.BlockSpec((None, rows, width), lambda h, s, m: (h, 0, 0)),
         ],
         out_specs=pl.BlockSpec((None, rows, width), lambda h, s, m: (h, 0, 0)),
@@ -94,13 +91,13 @@
         _step_kernel,
         grid_spec=grid_spec,
         out_shape=jax.ShapeDtypeStruct(state.shape, jnp.float32),
-        input_output_aliases={7: 0},
+        input_output_aliases={6: 0},
         cost_estimate=pl.CostEstimate(
             flops=flops,
             transcendentals=heads * rows * keys,
-            bytes_accessed=q_hm.size * 2 + 2 * (kv_a.size + kv_b.size) * 2 + state.size * 8,
+            bytes_accessed=q_hm.size * 2 + kv_hm.size * 2 + state.size * 8,
         ),
-    )(step, meta, valid_row, seg_col, q_hm, kv_a, kv_b, state)
+    )(step, meta, valid_row, seg_col, q_hm, kv_hm, state)
 
 
 def tp_gather(x, count):
@@ -190,25 +187,23 @@
     seg_last = segment_start[row_count - 1]
 
     meta = jnp.stack([first_row, 1, seg_last]).astype(jnp.int32)
-    split = local_heads // 2
 
     def absorb(state, incoming, step):
         step_arr = jnp.asarray(step, jnp.int32).reshape(1)
-        return attend_step(step_arr, meta, valid_row, seg_col, q_hm, incoming[0], incoming[1], state)
+        return attend_step(step_arr, meta, valid_row, seg_col, q_hm, incoming, state)
 
     lane = jnp.arange(2 * HD, dtype=jnp.int32)
     initial = jnp.broadcast_to(
         jnp.where(lane == 0, -1e30, 0.0).astype(jnp.float32), (local_heads, row_count, 2 * HD)
     )
 
-    own = (kv_hm[:split], kv_hm[split:])
-    prev_block = tuple(lax.ppermute(part, "seq", chain) for part in own)
-    carried = absorb(initial, own, 0)
+    prev_block = lax.ppermute(kv_hm, "seq", chain)
+    carried = absorb(initial, kv_hm, 0)
 
     def step_with(pairs):
         def advance(step_index, carry_in):
             held, state = carry_in
-            sent = tuple(lax.ppermute(part, "seq", pairs) for part in held)
+            sent = lax.ppermute(held, "seq", pairs)
             state = absorb(state, held, step_index)
             return (sent, state)
 
@@ -229,7 +224,7 @@
     has_prev = seq_rank > 0
     cand_slot = jnp.concatenate([page_slot, jnp.where(has_prev, prev_slot, -1)]) - base_slot
     cand_pages = jnp.concatenate(
-        [packed.reshape(tiles, PAGE, -1), jnp.transpose(jnp.concatenate(prev_block, axis=0), (1, 0, 2)).reshape(tiles, PAGE, -1)],
+        [packed.reshape(tiles, PAGE, -1), jnp.transpose(prev_block, (1, 0, 2)).reshape(tiles, PAGE, -1)],
         axis=0,
     )
     match = cand_slot[None, :] == jnp.arange(slot_count, dtype=jnp.int32)[:, None]

time: 340 us -> 328 us (0.965)
  waiting for transfers between devices: 105 us -> 148 us
  starting transfers between devices: 109 us -> 66.6 us
  Pallas kernels: 83.4 us -> 68.5 us
    ppermute x32 -> x16, starting transfers between devices: 79.7 us -> 37.2 us  [the longest x15 34.9 us: advance(): sent = lax.ppermute(held, 'seq', pairs)]
    ppermute x32 -> x16, waiting for transfers between devices: 57.8 us -> 95.4 us  [the longest x15 95.4 us: advance(): sent = lax.ppermute(held, 'seq', pairs)]
    pallas_call x17, Pallas kernels: 83.4 us -> 68.5 us  [attend_step(): pl.pallas_call(_step_kernel, grid_spec=grid_spec, out_shape=jax.ShapeDtyp...]
    all_to_all x2, waiting for transfers between devices: 47 us -> 52.5 us  [tp_gather(): got = lax.all_to_all(copies, 'tp', 0, 0, tiled=True)]
    unnamed x36 -> x33, local copies, waits for them, and re-layouts: 8.37 us -> 8.34 us
  transfers between devices with their start and end apart: 37 -> 21, of which waited for: 23 -> 18; matrix products, arithmetic and copies ran while one was open for 9% -> 9% of each run, Pallas kernels for 24% -> 21%
where the time goes in v2:
time: 328 us; the launch traced here: 325 us
  waiting for transfers between devices  148 us (45%)
  Pallas kernels  68.5 us (21%)
  starting transfers between devices  66.6 us (20%)
  local copies, waits for them, and re-layouts  22.7 us (7%)
  other arithmetic  7.86 us (2%)
  matrix products  6.94 us (2%)
  between operations  4.2 us (1%)
    ppermute x15, waiting for transfers between devices, advance(): sent = lax.ppermute(held, 'seq', pairs)  95.4 us
    pallas_call x17, Pallas kernels, attend_step(): pl.pallas_call(_step_kernel, grid_spec=grid_spec, out_shape=jax.ShapeDtyp...  68.5 us
    all_to_all x2, waiting for transfers between devices, tp_gather(): got = lax.all_to_all(copies, 'tp', 0, 0, tiled=True)  52.5 us
    ppermute x15, starting transfers between devices, advance(): sent = lax.ppermute(held, 'seq', pairs)  34.9 us
    all_to_all x1, starting transfers between devices, body(): cross_steps = jnp.sum(lax.all_to_all(told, 'seq', 0, 0, tiled=True))  12.3 us
    all_to_all x2, starting transfers between devices, tp_gather(): got = lax.all_to_all(copies, 'tp', 0, 0, tiled=True)  11 us
    unnamed x33, local copies, waits for them, and re-layouts  8.34 us
  transfers between devices with their start and end apart: 21, of which 18 were waited for; matrix products, arithmetic and copies ran while one was open for 9% of the time, Pallas kernels for 21%

profile of v2, /device:TPU:24, one launch (start us, length us, event | category | flops | bytes accessed | tf_op | source)
XLA Modules:
  0.0 325.5 jit_solution(14004393899256166098)
XLA Ops:
  0.6 2.5 broadcast_in_dim.94
  3.2 6.0 %all-to-all-start = ((bf16[4,512,512]{2,1,0:T(8,128)(2,1)}), bf16[4,512,512]{2,1,0:T(8,128)(2,1)S(1)}, u32[]{:S(2)}, u32[]{:S(2)}) async-start(bf16[4,512,512]{2,1,0:T(8,128)(2,1)} %broadcast_in_dim.94), calls=%async_computation | async-start | bytes 4194304 | tf_op jit(solution)/shard_map/all_to_all | solution.py:105
  9.2 1.9 collective-permute-start.3
  14.4 1.4 copy.116
  15.9 2.3 copy.121
  18.2 1.4 copy.125
  19.6 1.5 copy.136
  21.1 1.3 copy.137
  23.5 33.9 %all-to-all-done = bf16[4,512,512]{2,1,0:T(8,128)(2,1)S(1)} async-done(((bf16[4,512,512]{2,1,0:T(8,128)(2,1)}), bf16[4,512,512]{2,1,0:T(8,128)(2,1)S(1)}, u32[]{:S(2)}, u32[]{:S(2)}) %all-to-all-start) | async-done | bytes 2097184 | tf_op jit(solution)/shard_map/all_to_all | solution.py:105
  58.8 12.3 %all-to-all-start.1 = ((s32[64,1,1]{2,1,0:T(1,128)}), s32[64,1,1]{2,1,0:T(1,128)S(1)}, u32[]{:S(2)}, u32[]{:S(2)}) async-start(s32[64,1,1]{2,1,0:T(1,128)} %broadcast_in_dim.95), calls=%async_computation.1 | async-start | bytes 65536 | tf_op jit(solution)/shard_map/all_to_all | solution.py:151
  71.1 2.8 copy.115
  78.3 1.3 fusion.5
  81.8 4.3 %all-to-all-start.3 = ((bf16[256,4,512]{2,0,1:T(8,128)(2,1)}), bf16[256,4,512]{2,0,1:T(8,128)(2,1)}, u32[]{:S(2)}, u32[]{:S(2)}) async-start(bf16[256,4,512]{2,0,1:T(8,128)(2,1)} %copy.137), calls=%async_computation.3 | async-start | bytes 2097152 | tf_op jit(solution)/shard_map/all_to_all | solution.py:180
  86.2 2.2 collective-permute-start.2
  91.0 9.2 %shard_map.104 = f32[4,512,128]{2,1,0:T(8,128)S(1)} custom-call(s32[1]{0:T(128)} %constant.69.clone.1.step_ref, s32[3]{0:T(128)S(1)} %pad_add_fusion.meta_ref, s32[1,512]{1,0:T(1,128)S(1)} %bitcast.72, s32[512,1]{1,0:T(8,128)S(1)} %copy.133.seg_ref, bf16[4,512,64]{2,1,0:T(8,128)(2,1)S(1)} %maximum_bitcast_fusion.q_ref, ...), custom_call_target="tpu_custom_call", output_to_operand_aliasing={{}: (6, {})} | custom-call | flops 402653184 | bytes 2883584 | tf_op jit(solution)/shard_map/pallas_call | solution.py:90
  100.2 50.7 %while.24 = (s32[]{:T(128)}, bf16[4,512,128]{2,1,0:T(8,128)(2,1)S(1)}, f32[4,512,128]{2,1,0:T(8,128)S(1)}, s32[]{:T(128)}, s32[3]{0:T(128)S(1)}, /*index=5*/s32[...) while((s32[]{:T(128)}, bf16[4,512,128]{2,1,0:T(8,128)(2,1)S(1)}, ...), condition=%wide.region_3.4_spmd, body=%wide.region_2.3_spmd.sunk | while | flops 402653184 | bytes 8126633 | solution.py:212
  100.3 3.4 %collective-permute-start = (bf16[4,512,128]{2,1,0:T(8,128)(2,1)S(1)}, bf16[4,512,128]{2,1,0:T(8,128)(2,1)S(1)}, u32[]{:S(2)}, u32[]{:S(2)}) collective-permute-start(bf16[4,512,128]{2,1,0:T(8,128)(2,1)S(1)} %copy.160.kv_ref), channel_id=1, source_target_pairs={{0,4},{4,8},{8,12},{12,16},{16,20},{20,24},{24,28},{28,32},{32,36}... | collective-permute-start | bytes 1572872 | tf_op jit(solution)/shard_map/while/body/ppermute | solution.py:206
  103.7 8.8 %body.4 = f32[4,512,128]{2,1,0:T(8,128)S(1)} custom-call(s32[1]{0:T(128)} %bitcast.60.step_ref, s32[3]{0:T(128)S(1)} %get-tuple-element.320.meta_ref, s32[1,512]{1,0:T(1,128)S(1)} %get-tuple-element.321.valid_ref, s32[512,1]{1,0:T(8,128)S(1)} %get-tuple-element.322.seg_ref, ...), custom_call_target="tpu_custom_call", output_to_operand_aliasing={{}: (6, {})} | custom-call | flops 402653184 | bytes 2883584 | tf_op jit(solution)/shard_map/while/body/pallas_call | solution.py:90
  113.0 1.9 collective-permute-start
  114.9 8.8 %body.4 = f32[4,512,128]{2,1,0:T(8,128)S(1)} custom-call(s32[1]{0:T(128)} %bitcast.60.step_ref, s32[3]{0:T(128)S(1)} %get-tuple-element.320.meta_ref, s32[1,512]{1,0:T(1,128)S(1)} %get-tuple-element.321.valid_ref, s32[512,1]{1,0:T(8,128)S(1)} %get-tuple-element.322.seg_ref, ...), custom_call_target="tpu_custom_call", output_to_operand_aliasing={{}: (6, {})} | custom-call | flops 402653184 | bytes 2883584 | tf_op jit(solution)/shard_map/while/body/pallas_call | solution.py:90
  123.7 1.9 collective-permute-done
  125.6 1.9 collective-permute-start
  127.6 9.2 %body.4 = f32[4,512,128]{2,1,0:T(8,128)S(1)} custom-call(s32[1]{0:T(128)} %bitcast.60.step_ref, s32[3]{0:T(128)S(1)} %get-tuple-element.320.meta_ref, s32[1,512]{1,0:T(1,128)S(1)} %get-tuple-element.321.valid_ref, s32[512,1]{1,0:T(8,128)S(1)} %get-tuple-element.322.seg_ref, ...), custom_call_target="tpu_custom_call", output_to_operand_aliasing={{}: (6, {})} | custom-call | flops 402653184 | bytes 2883584 | tf_op jit(solution)/shard_map/while/body/pallas_call | solution.py:90
  136.8 1.5 collective-permute-done
  138.3 1.9 collective-permute-start
  140.2 2.6 body.4
  142.9 8.0 %collective-permute-done = bf16[4,512,128]{2,1,0:T(8,128)(2,1)S(1)} collective-permute-done((bf16[4,512,128]{2,1,0:T(8,128)(2,1)S(1)}, bf16[4,512,128]{2,1,0:T(8,128)(2,1)S(1)}, u32[]{:S(2)}, u32[]{:S(2)}) %collective-permute-start) | collective-permute-done | bytes 524320 | tf_op jit(solution)/shard_map/while/body/ppermute | solution.py:206
  150.9 139.3 %while.25 = (s32[]{:T(128)}, bf16[4,512,128]{2,1,0:T(8,128)(2,1)S(1)}, f32[4,512,128]{2,1,0:T(8,128)S(1)}, s32[3]{0:T(128)S(1)}, s32[1,512]{1,0:T(1,128)S(1)}, /...) while((s32[]{:T(128)}, bf16[4,512,128]{2,1,0:T(8,128)(2,1)S(1)}, ...), condition=%wide.region_5.6_spmd, body=%wide.region_4.5_spmd.sunk | while | flops 402653184 | bytes 8126625 | solution.py:213
  150.9 1.9 collective-permute-start.1
  152.9 2.6 body.5
  155.5 8.0 %collective-permute-done.1 = bf16[4,512,128]{2,1,0:T(8,128)(2,1)S(1)} collective-permute-done((bf16[4,512,128]{2,1,0:T(8,128)(2,1)S(1)}, bf16[4,512,128]{2,1,0:T(8,128)(2,1)S(1)}, u32[]{:S(2)}, u32[]{:S(2)}) %collective-permute-start.1) | collective-permute-done | bytes 524320 | tf_op jit(solution)/shard_map/while/body/ppermute | solution.py:206
  163.6 1.9 collective-permute-start.1
  165.5 2.6 body.5
  168.2 8.0 %collective-permute-done.1 = bf16[4,512,128]{2,1,0:T(8,128)(2,1)S(1)} collective-permute-done((bf16[4,512,128]{2,1,0:T(8,128)(2,1)S(1)}, bf16[4,512,128]{2,1,0:T(8,128)(2,1)S(1)}, u32[]{:S(2)}, u32[]{:S(2)}) %collective-permute-start.1) | collective-permute-done | bytes 524320 | tf_op jit(solution)/shard_map/while/body/ppermute | solution.py:206
  176.3 1.9 collective-permute-start.1
  178.2 2.6 body.5
  180.8 8.0 %collective-permute-done.1 = bf16[4,512,128]{2,1,0:T(8,128)(2,1)S(1)} collective-permute-done((bf16[4,512,128]{2,1,0:T(8,128)(2,1)S(1)}, bf16[4,512,128]{2,1,0:T(8,128)(2,1)S(1)}, u32[]{:S(2)}, u32[]{:S(2)}) %collective-permute-start.1) | collective-permute-done | bytes 524320 | tf_op jit(solution)/shard_map/while/body/ppermute | solution.py:206
  188.9 1.9 collective-permute-start.1
  190.9 2.6 body.5
  193.5 8.0 %collective-permute-done.1 = bf16[4,512,128]{2,1,0:T(8,128)(2,1)S(1)} collective-permute-done((bf16[4,512,128]{2,1,0:T(8,128)(2,1)S(1)}, bf16[4,512,128]{2,1,0:T(8,128)(2,1)S(1)}, u32[]{:S(2)}, u32[]{:S(2)}) %collective-permute-start.1) | collective-permute-done | bytes 524320 | tf_op jit(solution)/shard_map/while/body/ppermute | solution.py:206
  201.6 1.9 collective-permute-start.1
  203.5 2.6 body.5
  206.2 8.0 %collective-permute-done.1 = bf16[4,512,128]{2,1,0:T(8,128)(2,1)S(1)} collective-permute-done((bf16[4,512,128]{2,1,0:T(8,128)(2,1)S(1)}, bf16[4,512,128]{2,1,0:T(8,128)(2,1)S(1)}, u32[]{:S(2)}, u32[]{:S(2)}) %collective-permute-start.1) | collective-permute-done | bytes 524320 | tf_op jit(solution)/shard_map/while/body/ppermute | solution.py:206
  214.2 1.9 collective-permute-start.1
  216.2 2.6 body.5
  218.8 8.0 %collective-permute-done.1 = bf16[4,512,128]{2,1,0:T(8,128)(2,1)S(1)} collective-permute-done((bf16[4,512,128]{2,1,0:T(8,128)(2,1)S(1)}, bf16[4,512,128]{2,1,0:T(8,128)(2,1)S(1)}, u32[]{:S(2)}, u32[]{:S(2)}) %collective-permute-start.1) | collective-permute-done | bytes 524320 | tf_op jit(solution)/shard_map/while/body/ppermute | solution.py:206
  226.9 5.3 %collective-permute-start.1 = (bf16[4,512,128]{2,1,0:T(8,128)(2,1)S(1)}, bf16[4,512,128]{2,1,0:T(8,128)(2,1)S(1)}, u32[]{:S(2)}, u32[]{:S(2)}) collective-permute-start(bf16[4,512,128]{2,1,0:T(8,128)(2,1)S(1)} %copy.169.kv_ref), channel_id=1, source_target_pairs={{0,4},{4,8},{8,12},{12,16},{16,20},{20,24},{24,28},{28,32},{32,36}... | collective-permute-start | bytes 1572872 | tf_op jit(solution)/shard_map/while/body/ppermute | solution.py:206
  232.2 2.6 body.5
  234.9 4.6 %collective-permute-done.1 = bf16[4,512,128]{2,1,0:T(8,128)(2,1)S(1)} collective-permute-done((bf16[4,512,128]{2,1,0:T(8,128)(2,1)S(1)}, bf16[4,512,128]{2,1,0:T(8,128)(2,1)S(1)}, u32[]{:S(2)}, u32[]{:S(2)}) %collective-permute-start.1) | collective-permute-done | bytes 524320 | tf_op jit(solution)/shard_map/while/body/ppermute | solution.py:206
  239.6 3.2 collective-permute-start.1
  242.8 2.6 body.5
  245.4 6.7 %collective-permute-done.1 = bf16[4,512,128]{2,1,0:T(8,128)(2,1)S(1)} collective-permute-done((bf16[4,512,128]{2,1,0:T(8,128)(2,1)S(1)}, bf16[4,512,128]{2,1,0:T(8,128)(2,1)S(1)}, u32[]{:S(2)}, u32[]{:S(2)}) %collective-permute-start.1) | collective-permute-done | bytes 524320 | tf_op jit(solution)/shard_map/while/body/ppermute | solution.py:206
  252.2 1.9 collective-permute-start.1
  254.2 2.6 body.5
  256.8 8.0 %collective-permute-done.1 = bf16[4,512,128]{2,1,0:T(8,128)(2,1)S(1)} collective-permute-done((bf16[4,512,128]{2,1,0:T(8,128)(2,1)S(1)}, bf16[4,512,128]{2,1,0:T(8,128)(2,1)S(1)}, u32[]{:S(2)}, u32[]{:S(2)}) %collective-permute-start.1) | collective-permute-done | bytes 524320 | tf_op jit(solution)/shard_map/while/body/ppermute | solution.py:206
  264.9 1.9 collective-permute-start.1
  266.8 2.6 body.5
  269.5 8.0 %collective-permute-done.1 = bf16[4,512,128]{2,1,0:T(8,128)(2,1)S(1)} collective-permute-done((bf16[4,512,128]{2,1,0:T(8,128)(2,1)S(1)}, bf16[4,512,128]{2,1,0:T(8,128)(2,1)S(1)}, u32[]{:S(2)}, u32[]{:S(2)}) %collective-permute-start.1) | collective-permute-done | bytes 524320 | tf_op jit(solution)/shard_map/while/body/ppermute | solution.py:206
  277.5 1.9 collective-permute-start.1
  279.5 2.6 body.5
  282.1 8.0 %collective-permute-done.1 = bf16[4,512,128]{2,1,0:T(8,128)(2,1)S(1)} collective-permute-done((bf16[4,512,128]{2,1,0:T(8,128)(2,1)S(1)}, bf16[4,512,128]{2,1,0:T(8,128)(2,1)S(1)}, u32[]{:S(2)}, u32[]{:S(2)}) %collective-permute-start.1) | collective-permute-done | bytes 524320 | tf_op jit(solution)/shard_map/while/body/ppermute | solution.py:206
  293.7 4.9 %all-to-all-start.2 = ((bf16[4,512,256]{2,1,0:T(8,128)(2,1)}), bf16[4,512,256]{2,1,0:T(8,128)(2,1)}, u32[]{:S(2)}, u32[]{:S(2)}) async-start(bf16[4,512,256]{2,1,0:T(8,128)(2,1)} %broadcast_in_dim.103), calls=%async_computation.2 | async-start | bytes 2097152 | tf_op jit(solution)/shard_map/all_to_all | solution.py:105
  303.8 18.6 %all-to-all-done.2 = bf16[4,512,256]{2,1,0:T(8,128)(2,1)} async-done(((bf16[4,512,256]{2,1,0:T(8,128)(2,1)}), bf16[4,512,256]{2,1,0:T(8,128)(2,1)}, u32[]{:S(2)}, u32[]{:S(2)}) %all-to-all-start.2) | async-done | bytes 1048608 | tf_op jit(solution)/shard_map/all_to_all | solution.py:105
  322.4 3.0 fusion.4
  (123 shorter events, 21.3 us)
Async XLA Ops:
  3.2 6.1 %copy-start.15 = (s32[4]{0:T(128)S(1)}, s32[4]{0:T(128)}, u32[]{:S(2)}) copy-start(s32[4]{0:T(128)} %param.21) | copy-start | bytes 52
  3.2 8.0 %copy-start.13 = (s32[512]{0:T(512)S(1)}, s32[512]{0:T(512)}, u32[]{:S(2)}) copy-start(s32[512]{0:T(512)} %param.19) | copy-start | bytes 6148
  3.2 11.2 %copy-start.14 = (f32[2048]{0:T(1024)S(1)}, f32[2048]{0:T(1024)}, u32[]{:S(2)}) copy-start(f32[2048]{0:T(1024)} %param.14) | copy-start | bytes 24580
  3.2 11.3 %copy-start.6 = (bf16[2048,256]{1,0:T(8,128)(2,1)S(1)}, bf16[2048,256]{1,0:T(8,128)(2,1)}, u32[]{:S(2)}) copy-start(bf16[2048,256]{1,0:T(8,128)(2,1)} %param.15) | copy-start | bytes 3145732
  3.2 54.2 %all-to-all-start = ((bf16[4,512,512]{2,1,0:T(8,128)(2,1)}), bf16[4,512,512]{2,1,0:T(8,128)(2,1)S(1)}, u32[]{:S(2)}, u32[]{:S(2)}) async-start(bf16[4,512,512]{2,1,0:T(8,128)(2,1)} %broadcast_in_dim.94), calls=%async_computation | async-start | bytes 4194304 | tf_op jit(solution)/shard_map/all_to_all | solution.py:105
  9.2 289.4 %collective-permute-start.3 = (s32[4]{0:T(128)S(1)}, s32[4]{0:T(128)S(1)}, u32[]{:S(2)}, u32[]{:S(2)}) collective-permute-start(s32[4]{0:T(128)S(1)} %copy-done.15), channel_id=1, source_target_pairs={{0,4},{4,8},{8,12},{12,16},{16,20},{20,24},{24,28},{28,32},{32,36}... | collective-permute-start | bytes 56 | tf_op jit(solution)/shard_map/ppermute | solution.py:112
  15.9 2.3 copy-start.7
  19.6 2.8 copy-start.12
  57.4 1.3 copy-start.4
  58.8 22.8 %all-to-all-start.1 = ((s32[64,1,1]{2,1,0:T(1,128)}), s32[64,1,1]{2,1,0:T(1,128)S(1)}, u32[]{:S(2)}, u32[]{:S(2)}) async-start(s32[64,1,1]{2,1,0:T(1,128)} %broadcast_in_dim.95), calls=%async_computation.1 | async-start | bytes 65536 | tf_op jit(solution)/shard_map/all_to_all | solution.py:151
  74.4 1.2 copy-start.10
  75.7 1.3 copy-start.9
  77.0 1.3 copy-start.8
  80.8 1.0 copy-start.2
  81.8 210.9 %all-to-all-start.3 = ((bf16[256,4,512]{2,0,1:T(8,128)(2,1)}), bf16[256,4,512]{2,0,1:T(8,128)(2,1)}, u32[]{:S(2)}, u32[]{:S(2)}) async-start(bf16[256,4,512]{2,0,1:T(8,128)(2,1)} %copy.137), calls=%async_computation.3 | async-start | bytes 2097152 | tf_op jit(solution)/shard_map/all_to_all | solution.py:180
  86.2 4.8 %copy-start.5 = (bf16[4,512,128]{2,1,0:T(8,128)(2,1)}, bf16[4,512,128]{2,1,0:T(8,128)(2,1)S(1)}, u32[]{:S(2)}) copy-start(bf16[4,512,128]{2,1,0:T(8,128)(2,1)S(1)} %select_bitcast_fusion.kv_ref) | copy-start | bytes 1572868
  86.2 14.0 %collective-permute-start.2 = (bf16[4,512,128]{2,1,0:T(8,128)(2,1)S(1)}, bf16[4,512,128]{2,1,0:T(8,128)(2,1)S(1)}, u32[]{:S(2)}, u32[]{:S(2)}) collective-permute-start(bf16[4,512,128]{2,1,0:T(8,128)(2,1)S(1)} %select_bitcast_fusion.kv_ref), channel_id=1, source_target_pairs={{0,4},{4,8},{8,12},{12,16},{16,20},{20,24},{24,28},{28,32},{32,36}... | collective-permute-start | bytes 1572872 | tf_op jit(solution)/shard_map/ppermute | solution.py:200
  100.3 3.4 %copy-start = (bf16[4,512,128]{2,1,0:T(8,128)(2,1)}, bf16[4,512,128]{2,1,0:T(8,128)(2,1)S(1)}, u32[]{:S(2)}) copy-start(bf16[4,512,128]{2,1,0:T(8,128)(2,1)S(1)} %copy.160.kv_ref) | copy-start | bytes 1572868 | tf_op jit(solution)/shard_map/while
  100.3 12.6 %collective-permute-start = (bf16[4,512,128]{2,1,0:T(8,128)(2,1)S(1)}, bf16[4,512,128]{2,1,0:T(8,128)(2,1)S(1)}, u32[]{:S(2)}, u32[]{:S(2)}) collective-permute-start(bf16[4,512,128]{2,1,0:T(8,128)(2,1)S(1)} %copy.160.kv_ref), channel_id=1, source_target_pairs={{0,4},{4,8},{8,12},{12,16},{16,20},{20,24},{24,28},{28,32},{32,36}... | collective-permute-start | bytes 1572872 | tf_op jit(solution)/shard_map/while/body/ppermute | solution.py:206
  112.9 1.9 copy-start
  113.0 12.6 %collective-permute-start = (bf16[4,512,128]{2,1,0:T(8,128)(2,1)S(1)}, bf16[4,512,128]{2,1,0:T(8,128)(2,1)S(1)}, u32[]{:S(2)}, u32[]{:S(2)}) collective-permute-start(bf16[4,512,128]{2,1,0:T(8,128)(2,1)S(1)} %copy.160.kv_ref), channel_id=1, source_target_pairs={{0,4},{4,8},{8,12},{12,16},{16,20},{20,24},{24,28},{28,32},{32,36}... | collective-permute-start | bytes 1572872 | tf_op jit(solution)/shard_map/while/body/ppermute | solution.py:206
  125.6 1.9 copy-start
  125.6 12.6 %collective-permute-start = (bf16[4,512,128]{2,1,0:T(8,128)(2,1)S(1)}, bf16[4,512,128]{2,1,0:T(8,128)(2,1)S(1)}, u32[]{:S(2)}, u32[]{:S(2)}) collective-permute-start(bf16[4,512,128]{2,1,0:T(8,128)(2,1)S(1)} %copy.160.kv_ref), channel_id=1, source_target_pairs={{0,4},{4,8},{8,12},{12,16},{16,20},{20,24},{24,28},{28,32},{32,36}... | collective-permute-start | bytes 1572872 | tf_op jit(solution)/shard_map/while/body/ppermute | solution.py:206
  138.3 1.9 copy-start
  138.3 12.6 %collective-permute-start = (bf16[4,512,128]{2,1,0:T(8,128)(2,1)S(1)}, bf16[4,512,128]{2,1,0:T(8,128)(2,1)S(1)}, u32[]{:S(2)}, u32[]{:S(2)}) collective-permute-start(bf16[4,512,128]{2,1,0:T(8,128)(2,1)S(1)} %copy.160.kv_ref), channel_id=1, source_target_pairs={{0,4},{4,8},{8,12},{12,16},{16,20},{20,24},{24,28},{28,32},{32,36}... | collective-permute-start | bytes 1572872 | tf_op jit(solution)/shard_map/while/body/ppermute | solution.py:206
  150.9 1.9 copy-start.1
  150.9 12.6 %collective-permute-start.1 = (bf16[4,512,128]{2,1,0:T(8,128)(2,1)S(1)}, bf16[4,512,128]{2,1,0:T(8,128)(2,1)S(1)}, u32[]{:S(2)}, u32[]{:S(2)}) collective-permute-start(bf16[4,512,128]{2,1,0:T(8,128)(2,1)S(1)} %copy.169.kv_ref), channel_id=1, source_target_pairs={{0,4},{4,8},{8,12},{12,16},{16,20},{20,24},{24,28},{28,32},{32,36}... | collective-permute-start | bytes 1572872 | tf_op jit(solution)/shard_map/while/body/ppermute | solution.py:206
  163.6 1.9 copy-start.1
  163.6 12.6 %collective-permute-start.1 = (bf16[4,512,128]{2,1,0:T(8,128)(2,1)S(1)}, bf16[4,512,128]{2,1,0:T(8,128)(2,1)S(1)}, u32[]{:S(2)}, u32[]{:S(2)}) collective-permute-start(bf16[4,512,128]{2,1,0:T(8,128)(2,1)S(1)} %copy.169.kv_ref), channel_id=1, source_target_pairs={{0,4},{4,8},{8,12},{12,16},{16,20},{20,24},{24,28},{28,32},{32,36}... | collective-permute-start | bytes 1572872 | tf_op jit(solution)/shard_map/while/body/ppermute | solution.py:206
  176.2 1.9 copy-start.1
  176.3 12.6 %collective-permute-start.1 = (bf16[4,512,128]{2,1,0:T(8,128)(2,1)S(1)}, bf16[4,512,128]{2,1,0:T(8,128)(2,1)S(1)}, u32[]{:S(2)}, u32[]{:S(2)}) collective-permute-start(bf16[4,512,128]{2,1,0:T(8,128)(2,1)S(1)} %copy.169.kv_ref), channel_id=1, source_target_pairs={{0,4},{4,8},{8,12},{12,16},{16,20},{20,24},{24,28},{28,32},{32,36}... | collective-permute-start | bytes 1572872 | tf_op jit(solution)/shard_map/while/body/ppermute | solution.py:206
  188.9 1.9 copy-start.1
  188.9 12.6 %collective-permute-start.1 = (bf16[4,512,128]{2,1,0:T(8,128)(2,1)S(1)}, bf16[4,512,128]{2,1,0:T(8,128)(2,1)S(1)}, u32[]{:S(2)}, u32[]{:S(2)}) collective-permute-start(bf16[4,512,128]{2,1,0:T(8,128)(2,1)S(1)} %copy.169.kv_ref), channel_id=1, source_target_pairs={{0,4},{4,8},{8,12},{12,16},{16,20},{20,24},{24,28},{28,32},{32,36}... | collective-permute-start | bytes 1572872 | tf_op jit(solution)/shard_map/while/body/ppermute | solution.py:206
  201.6 1.9 copy-start.1
  201.6 12.6 %collective-permute-start.1 = (bf16[4,512,128]{2,1,0:T(8,128)(2,1)S(1)}, bf16[4,512,128]{2,1,0:T(8,128)(2,1)S(1)}, u32[]{:S(2)}, u32[]{:S(2)}) collective-permute-start(bf16[4,512,128]{2,1,0:T(8,128)(2,1)S(1)} %copy.169.kv_ref), channel_id=1, source_target_pairs={{0,4},{4,8},{8,12},{12,16},{16,20},{20,24},{24,28},{28,32},{32,36}... | collective-permute-start | bytes 1572872 | tf_op jit(solution)/shard_map/while/body/ppermute | solution.py:206
  214.2 1.9 copy-start.1
  214.2 12.6 %collective-permute-start.1 = (bf16[4,512,128]{2,1,0:T(8,128)(2,1)S(1)}, bf16[4,512,128]{2,1,0:T(8,128)(2,1)S(1)}, u32[]{:S(2)}, u32[]{:S(2)}) collective-permute-start(bf16[4,512,128]{2,1,0:T(8,128)(2,1)S(1)} %copy.169.kv_ref), channel_id=1, source_target_pairs={{0,4},{4,8},{8,12},{12,16},{16,20},{20,24},{24,28},{28,32},{32,36}... | collective-permute-start | bytes 1572872 | tf_op jit(solution)/shard_map/while/body/ppermute | solution.py:206
  226.9 5.3 %copy-start.1 = (bf16[4,512,128]{2,1,0:T(8,128)(2,1)}, bf16[4,512,128]{2,1,0:T(8,128)(2,1)S(1)}, u32[]{:S(2)}) copy-start(bf16[4,512,128]{2,1,0:T(8,128)(2,1)S(1)} %copy.169.kv_ref) | copy-start | bytes 1572868 | tf_op jit(solution)/shard_map/while
  226.9 12.6 %collective-permute-start.1 = (bf16[4,512,128]{2,1,0:T(8,128)(2,1)S(1)}, bf16[4,512,128]{2,1,0:T(8,128)(2,1)S(1)}, u32[]{:S(2)}, u32[]{:S(2)}) collective-permute-start(bf16[4,512,128]{2,1,0:T(8,128)(2,1)S(1)} %copy.169.kv_ref), channel_id=1, source_target_pairs={{0,4},{4,8},{8,12},{12,16},{16,20},{20,24},{24,28},{28,32},{32,36}... | collective-permute-start | bytes 1572872 | tf_op jit(solution)/shard_map/while/body/ppermute | solution.py:206
  239.6 3.2 copy-start.1
  239.6 12.6 %collective-permute-start.1 = (bf16[4,512,128]{2,1,0:T(8,128)(2,1)S(1)}, bf16[4,512,128]{2,1,0:T(8,128)(2,1)S(1)}, u32[]{:S(2)}, u32[]{:S(2)}) collective-permute-start(bf16[4,512,128]{2,1,0:T(8,128)(2,1)S(1)} %copy.169.kv_ref), channel_id=1, source_target_pairs={{0,4},{4,8},{8,12},{12,16},{16,20},{20,24},{24,28},{28,32},{32,36}... | collective-permute-start | bytes 1572872 | tf_op jit(solution)/shard_map/while/body/ppermute | solution.py:206
  252.2 1.9 copy-start.1
  252.2 12.6 %collective-permute-start.1 = (bf16[4,512,128]{2,1,0:T(8,128)(2,1)S(1)}, bf16[4,512,128]{2,1,0:T(8,128)(2,1)S(1)}, u32[]{:S(2)}, u32[]{:S(2)}) collective-permute-start(bf16[4,512,128]{2,1,0:T(8,128)(2,1)S(1)} %copy.169.kv_ref), channel_id=1, source_target_pairs={{0,4},{4,8},{8,12},{12,16},{16,20},{20,24},{24,28},{28,32},{32,36}... | collective-permute-start | bytes 1572872 | tf_op jit(solution)/shard_map/while/body/ppermute | solution.py:206
  264.9 1.9 copy-start.1
  264.9 12.6 %collective-permute-start.1 = (bf16[4,512,128]{2,1,0:T(8,128)(2,1)S(1)}, bf16[4,512,128]{2,1,0:T(8,128)(2,1)S(1)}, u32[]{:S(2)}, u32[]{:S(2)}) collective-permute-start(bf16[4,512,128]{2,1,0:T(8,128)(2,1)S(1)} %copy.169.kv_ref), channel_id=1, source_target_pairs={{0,4},{4,8},{8,12},{12,16},{16,20},{20,24},{24,28},{28,32},{32,36}... | collective-permute-start | bytes 1572872 | tf_op jit(solution)/shard_map/while/body/ppermute | solution.py:206
  277.5 1.9 copy-start.1
  277.5 12.6 %collective-permute-start.1 = (bf16[4,512,128]{2,1,0:T(8,128)(2,1)S(1)}, bf16[4,512,128]{2,1,0:T(8,128)(2,1)S(1)}, u32[]{:S(2)}, u32[]{:S(2)}) collective-permute-start(bf16[4,512,128]{2,1,0:T(8,128)(2,1)S(1)} %copy.169.kv_ref), channel_id=1, source_target_pairs={{0,4},{4,8},{8,12},{12,16},{16,20},{20,24},{24,28},{28,32},{32,36}... | collective-permute-start | bytes 1572872 | tf_op jit(solution)/shard_map/while/body/ppermute | solution.py:206
  292.5 7.0 %copy-start.3 = (bf16[512,4,2,64]{3,0,1,2:T(8,128)(2,1)S(1)}, bf16[512,4,2,64]{3,0,1,2:T(8,128)(2,1)}, u32[]{:S(2)}) copy-start(bf16[512,4,2,64]{3,0,1,2:T(8,128)(2,1)} %copy-done.2) | copy-start | bytes 1572868
  293.7 28.7 %all-to-all-start.2 = ((bf16[4,512,256]{2,1,0:T(8,128)(2,1)}), bf16[4,512,256]{2,1,0:T(8,128)(2,1)}, u32[]{:S(2)}, u32[]{:S(2)}) async-start(bf16[4,512,256]{2,1,0:T(8,128)(2,1)} %broadcast_in_dim.103), calls=%async_computation.2 | async-start | bytes 2097152 | tf_op jit(solution)/shard_map/all_to_all | solution.py:105
  302.1 20.3 %copy-start.11 = (bf16[512,512]{1,0:T(8,128)(2,1)S(1)}, bf16[512,512]{1,0:T(8,128)(2,1)}, u32[]{:S(2)}) copy-start(bf16[512,512]{1,0:T(8,128)(2,1)} %param.13) | copy-start | bytes 1572868

commit v3 on v2

--- a/solution.py
+++ b/solution.py
@@ -101,9 +101,13 @@
 
 
 def tp_gather(x, count):
-    copies = jnp.broadcast_to(x[None], (count,) + x.shape)
-    got = lax.all_to_all(copies, "tp", 0, 0, tiled=True)
-    return jnp.transpose(got, (1, 0, 2)).reshape(x.shape[0], count * x.shape[1])
+    rank = lax.axis_index("tp")
+    by_distance = [x] + [
+        lax.ppermute(x, "tp", [(i, (i + s) % count) for i in range(count)]) for s in range(1, count)
+    ]
+    stacked = jnp.stack(by_distance)
+    ordered = jnp.take(stacked, (rank - jnp.arange(count)) % count, axis=0)
+    return jnp.transpose(ordered, (1, 0, 2)).reshape(x.shape[0], count * x.shape[1])
 
 
 def passed_along(x, axis, by):

time: 328 us -> 312 us (0.951)
  waiting for transfers between devices: 148 us -> 27.6 us
  Pallas kernels: 68.5 us -> 155 us
  other arithmetic: 7.86 us -> 19.3 us
  starting transfers between devices: 66.6 us -> 73.4 us
    pallas_call x17, Pallas kernels: 68.5 us -> 155 us  [attend_step(): pl.pallas_call(_step_kernel, grid_spec=grid_spec, out_shape=jax.ShapeDtyp...]
    ppermute x15, waiting for transfers between devices: 95.4 us -> 20.8 us  [advance(): sent = lax.ppermute(held, 'seq', pairs)]
    all_to_all x2 -> x0, waiting for transfers between devices: 52.5 us -> none  [tp_gather(): got = lax.all_to_all(copies, 'tp', 0, 0, tiled=True)]
    ppermute x0 -> x6, starting transfers between devices: none -> 12.2 us  [tp_gather(): lax.ppermute(x, 'tp', [(i, (i + s) % count) for i in range(count)])]
    all_to_all x2 -> x0, starting transfers between devices: 11 us -> none  [tp_gather(): got = lax.all_to_all(copies, 'tp', 0, 0, tiled=True)]
    all_to_all x1, starting transfers between devices: 4.26 us -> 13.8 us  [body(): out_cols = lax.all_to_all(out_weight, 'tp', 1, 0, tiled=True)]
    ppermute x0 -> x6, waiting for transfers between devices: none -> 6.76 us  [tp_gather(): lax.ppermute(x, 'tp', [(i, (i + s) % count) for i in range(count)])]
    ppermute x15, starting transfers between devices: 34.9 us -> 30.1 us  [advance(): sent = lax.ppermute(held, 'seq', pairs)]
  transfers between devices with their start and end apart: 21 -> 25, of which waited for: 18 -> 17; matrix products, arithmetic and copies ran while one was open for 9% -> 15% of each run, Pallas kernels for 21% -> 50%
where the time goes in v3:
time: 312 us
  Pallas kernels  155 us (50%)
  starting transfers between devices  73.4 us (24%)
  waiting for transfers between devices  27.6 us (9%)
  local copies, waits for them, and re-layouts  24.3 us (8%)
  other arithmetic  19.3 us (6%)
  matrix products  6.75 us (2%)
  between operations  4.24 us (1%)
    pallas_call x17, Pallas kernels, attend_step(): pl.pallas_call(_step_kernel, grid_spec=grid_spec, out_shape=jax.ShapeDtyp...  155 us
    ppermute x15, starting transfers between devices, advance(): sent = lax.ppermute(held, 'seq', pairs)  30.1 us
    ppermute x15, waiting for transfers between devices, advance(): sent = lax.ppermute(held, 'seq', pairs)  20.8 us
    all_to_all x1, starting transfers between devices, body(): out_cols = lax.all_to_all(out_weight, 'tp', 1, 0, tiled=True)  13.8 us
    all_to_all x1, starting transfers between devices, body(): cross_steps = jnp.sum(lax.all_to_all(told, 'seq', 0, 0, tiled=True))  13.5 us
    ppermute x6, starting transfers between devices, tp_gather(): lax.ppermute(x, 'tp', [(i, (i + s) % count) for i in range(count)])  12.2 us
    ppermute x6, waiting for transfers between devices, tp_gather(): lax.ppermute(x, 'tp', [(i, (i + s) % count) for i in range(count)])  6.76 us
  transfers between devices with their start and end apart: 25, of which 17 were waited for; matrix products, arithmetic and copies ran while one was open for 15% of the time, Pallas kernels for 50%

profile of v3, /device:TPU:24, one launch (start us, length us, event | category | flops | bytes accessed | tf_op | source)
XLA Modules:
  0.0 311.8 jit_solution(7720440419810554332)
XLA Ops:
  0.6 2.0 collective-permute-start.2
  2.6 3.3 %collective-permute-start.3 = (bf16[512,512]{1,0:T(8,128)(2,1)}, bf16[512,512]{1,0:T(8,128)(2,1)}, u32[]{:S(2)}, u32[]{:S(2)}) collective-permute-start(bf16[512,512]{1,0:T(8,128)(2,1)} %param.13), channel_id=1, source_target_pairs={{0,2},{1,3},{2,0},{3,1},{4,6},{5,7},{6,4},{7,5},{8,10},{9,11},{10,... | collective-permute-start | bytes 1572872 | tf_op jit(solution)/shard_map/ppermute | solution.py:106
  6.9 1.9 collective-permute-start.9
  13.4 13.5 %all-to-all-start = ((s32[64,1,1]{2,1,0:T(1,128)}), s32[64,1,1]{2,1,0:T(1,128)S(1)}, u32[]{:S(2)}, u32[]{:S(2)}) async-start(s32[64,1,1]{2,1,0:T(1,128)} %broadcast_in_dim.104), calls=%async_computation | async-start | bytes 65536 | tf_op jit(solution)/shard_map/all_to_all | solution.py:155
  29.1 2.4 copy.101
  36.3 1.8 multiply_cosine_fusion
  40.8 2.9 pad_maximum_fusion
  43.7 2.3 gather_fusion
  46.7 2.0 fusion.3
  48.7 2.9 copy.100
  55.6 1.7 fusion.12
  59.3 1.9 collective-permute-start.5
  61.4 13.8 %all-to-all-start.1 = ((bf16[256,4,512]{2,0,1:T(8,128)(2,1)}), bf16[256,4,512]{2,0,1:T(8,128)(2,1)}, u32[]{:S(2)}, u32[]{:S(2)}) async-start(bf16[256,4,512]{2,0,1:T(8,128)(2,1)} %copy.122), calls=%async_computation.1 | async-start | bytes 2097152 | tf_op jit(solution)/shard_map/all_to_all | solution.py:184
  77.9 9.2 %shard_map.104 = f32[4,512,128]{2,1,0:T(8,128)S(1)} custom-call(s32[1]{0:T(128)} %constant.116.clone.1.step_ref, s32[3]{0:T(128)S(1)} %pad_add_fusion.meta_ref, s32[1,512]{1,0:T(1,128)S(1)} %bitcast.86, s32[512,1]{1,0:T(8,128)S(1)} %copy.118.seg_ref, bf16[4,512,64]{2,1,0:T(8,128)(2,1)S(1)} %maximum_bitcast_fusion.q_ref, ...), custom_call_target="tpu_custom_call", output_to_operand_aliasing={{}: (6, {})} | custom-call | flops 402653184 | bytes 2883584 | tf_op jit(solution)/shard_map/pallas_call | solution.py:90
  87.1 2.0 copy.137
  89.2 3.2 %reshape.273 = bf16[4,128,512]{2,1,0:T(8,128)(2,1)S(1)} reshape(bf16[512,4,2,64]{3,2,1,0:T(2,128)(2,1)} %copy.137) | data formatting | bytes 1048576 | tf_op jit(solution)/shard_map/reshape | solution.py:179
  93.3 190.2 %while.25 = (s32[]{:T(128)}, bf16[4,512,128]{2,1,0:T(8,128)(2,1)S(1)}, f32[4,512,128]{2,1,0:T(8,128)S(1)}, s32[3]{0:T(128)S(1)}, s32[1,512]{1,0:T(1,128)S(1)}, /...) while((s32[]{:T(128)}, bf16[4,512,128]{2,1,0:T(8,128)(2,1)S(1)}, ...), condition=%wide.region_5.6_spmd, body=%wide.region_4.5_spmd.sunk | while | flops 402653184 | bytes 8126625 | solution.py:217
  93.7 3.2 %collective-permute-start.1 = (bf16[4,512,128]{2,1,0:T(8,128)(2,1)S(1)}, bf16[4,512,128]{2,1,0:T(8,128)(2,1)S(1)}, u32[]{:S(2)}, u32[]{:S(2)}) collective-permute-start(bf16[4,512,128]{2,1,0:T(8,128)(2,1)S(1)} %copy.156.kv_ref), channel_id=1, source_target_pairs={{0,4},{4,8},{8,12},{12,16},{16,20},{20,24},{24,28},{28,32},{32,36}... | collective-permute-start | bytes 1572872 | tf_op jit(solution)/shard_map/while/body/ppermute | solution.py:210
  96.9 9.2 %body.5 = f32[4,512,128]{2,1,0:T(8,128)S(1)} custom-call(s32[1]{0:T(128)} %bitcast.71.step_ref, s32[3]{0:T(128)S(1)} %get-tuple-element.329.meta_ref, s32[1,512]{1,0:T(1,128)S(1)} %get-tuple-element.330.valid_ref, s32[512,1]{1,0:T(8,128)S(1)} %get-tuple-element.331.seg_ref, ...), custom_call_target="tpu_custom_call", output_to_operand_aliasing={{}: (6, {})} | custom-call | flops 402653184 | bytes 2883584 | tf_op jit(solution)/shard_map/while/body/pallas_call | solution.py:90
  106.3 1.9 collective-permute-start.1
  108.3 9.2 %body.5 = f32[4,512,128]{2,1,0:T(8,128)S(1)} custom-call(s32[1]{0:T(128)} %bitcast.71.step_ref, s32[3]{0:T(128)S(1)} %get-tuple-element.329.meta_ref, s32[1,512]{1,0:T(1,128)S(1)} %get-tuple-element.330.valid_ref, s32[512,1]{1,0:T(8,128)S(1)} %get-tuple-element.331.seg_ref, ...), custom_call_target="tpu_custom_call", output_to_operand_aliasing={{}: (6, {})} | custom-call | flops 402653184 | bytes 2883584 | tf_op jit(solution)/shard_map/while/body/pallas_call | solution.py:90
  117.5 1.5 collective-permute-done.1
  119.0 1.9 collective-permute-start.1
  120.9 9.2 %body.5 = f32[4,512,128]{2,1,0:T(8,128)S(1)} custom-call(s32[1]{0:T(128)} %bitcast.71.step_ref, s32[3]{0:T(128)S(1)} %get-tuple-element.329.meta_ref, s32[1,512]{1,0:T(1,128)S(1)} %get-tuple-element.330.valid_ref, s32[512,1]{1,0:T(8,128)S(1)} %get-tuple-element.331.seg_ref, ...), custom_call_target="tpu_custom_call", output_to_operand_aliasing={{}: (6, {})} | custom-call | flops 402653184 | bytes 2883584 | tf_op jit(solution)/shard_map/while/body/pallas_call | solution.py:90
  130.1 1.5 collective-permute-done.1
  131.7 1.9 collective-permute-start.1
  133.6 9.2 %body.5 = f32[4,512,128]{2,1,0:T(8,128)S(1)} custom-call(s32[1]{0:T(128)} %bitcast.71.step_ref, s32[3]{0:T(128)S(1)} %get-tuple-element.329.meta_ref, s32[1,512]{1,0:T(1,128)S(1)} %get-tuple-element.330.valid_ref, s32[512,1]{1,0:T(8,128)S(1)} %get-tuple-element.331.seg_ref, ...), custom_call_target="tpu_custom_call", output_to_operand_aliasing={{}: (6, {})} | custom-call | flops 402653184 | bytes 2883584 | tf_op jit(solution)/shard_map/while/body/pallas_call | solution.py:90
  144.3 1.9 collective-permute-start.1
  146.3 9.2 %body.5 = f32[4,512,128]{2,1,0:T(8,128)S(1)} custom-call(s32[1]{0:T(128)} %bitcast.71.step_ref, s32[3]{0:T(128)S(1)} %get-tuple-element.329.meta_ref, s32[1,512]{1,0:T(1,128)S(1)} %get-tuple-element.330.valid_ref, s32[512,1]{1,0:T(8,128)S(1)} %get-tuple-element.331.seg_ref, ...), custom_call_target="tpu_custom_call", output_to_operand_aliasing={{}: (6, {})} | custom-call | flops 402653184 | bytes 2883584 | tf_op jit(solution)/shard_map/while/body/pallas_call | solution.py:90
  155.5 1.5 collective-permute-done.1
  157.0 1.9 collective-permute-start.1
  158.9 9.2 %body.5 = f32[4,512,128]{2,1,0:T(8,128)S(1)} custom-call(s32[1]{0:T(128)} %bitcast.71.step_ref, s32[3]{0:T(128)S(1)} %get-tuple-element.329.meta_ref, s32[1,512]{1,0:T(1,128)S(1)} %get-tuple-element.330.valid_ref, s32[512,1]{1,0:T(8,128)S(1)} %get-tuple-element.331.seg_ref, ...), custom_call_target="tpu_custom_call", output_to_operand_aliasing={{}: (6, {})} | custom-call | flops 402653184 | bytes 2883584 | tf_op jit(solution)/shard_map/while/body/pallas_call | solution.py:90
  168.1 1.5 collective-permute-done.1
  169.6 1.9 collective-permute-start.1
  171.6 9.2 %body.5 = f32[4,512,128]{2,1,0:T(8,128)S(1)} custom-call(s32[1]{0:T(128)} %bitcast.71.step_ref, s32[3]{0:T(128)S(1)} %get-tuple-element.329.meta_ref, s32[1,512]{1,0:T(1,128)S(1)} %get-tuple-element.330.valid_ref, s32[512,1]{1,0:T(8,128)S(1)} %get-tuple-element.331.seg_ref, ...), custom_call_target="tpu_custom_call", output_to_operand_aliasing={{}: (6, {})} | custom-call | flops 402653184 | bytes 2883584 | tf_op jit(solution)/shard_map/while/body/pallas_call | solution.py:90
  180.8 1.5 collective-permute-done.1
  182.3 1.9 collective-permute-start.1
  184.2 9.2 %body.5 = f32[4,512,128]{2,1,0:T(8,128)S(1)} custom-call(s32[1]{0:T(128)} %bitcast.71.step_ref, s32[3]{0:T(128)S(1)} %get-tuple-element.329.meta_ref, s32[1,512]{1,0:T(1,128)S(1)} %get-tuple-element.330.valid_ref, s32[512,1]{1,0:T(8,128)S(1)} %get-tuple-element.331.seg_ref, ...), custom_call_target="tpu_custom_call", output_to_operand_aliasing={{}: (6, {})} | custom-call | flops 402653184 | bytes 2883584 | tf_op jit(solution)/shard_map/while/body/pallas_call | solution.py:90
  193.4 1.5 collective-permute-done.1
  195.0 1.9 collective-permute-start.1
  196.9 9.2 %body.5 = f32[4,512,128]{2,1,0:T(8,128)S(1)} custom-call(s32[1]{0:T(128)} %bitcast.71.step_ref, s32[3]{0:T(128)S(1)} %get-tuple-element.329.meta_ref, s32[1,512]{1,0:T(1,128)S(1)} %get-tuple-element.330.valid_ref, s32[512,1]{1,0:T(8,128)S(1)} %get-tuple-element.331.seg_ref, ...), custom_call_target="tpu_custom_call", output_to_operand_aliasing={{}: (6, {})} | custom-call | flops 402653184 | bytes 2883584 | tf_op jit(solution)/shard_map/while/body/pallas_call | solution.py:90
  206.1 1.5 collective-permute-done.1
  207.6 1.9 collective-permute-start.1
  209.6 9.2 %body.5 = f32[4,512,128]{2,1,0:T(8,128)S(1)} custom-call(s32[1]{0:T(128)} %bitcast.71.step_ref, s32[3]{0:T(128)S(1)} %get-tuple-element.329.meta_ref, s32[1,512]{1,0:T(1,128)S(1)} %get-tuple-element.330.valid_ref, s32[512,1]{1,0:T(8,128)S(1)} %get-tuple-element.331.seg_ref, ...), custom_call_target="tpu_custom_call", output_to_operand_aliasing={{}: (6, {})} | custom-call | flops 402653184 | bytes 2883584 | tf_op jit(solution)/shard_map/while/body/pallas_call | solution.py:90
  218.8 1.5 collective-permute-done.1
  220.3 1.9 collective-permute-start.1
  222.2 9.2 %body.5 = f32[4,512,128]{2,1,0:T(8,128)S(1)} custom-call(s32[1]{0:T(128)} %bitcast.71.step_ref, s32[3]{0:T(128)S(1)} %get-tuple-element.329.meta_ref, s32[1,512]{1,0:T(1,128)S(1)} %get-tuple-element.330.valid_ref, s32[512,1]{1,0:T(8,128)S(1)} %get-tuple-element.331.seg_ref, ...), custom_call_target="tpu_custom_call", output_to_operand_aliasing={{}: (6, {})} | custom-call | flops 402653184 | bytes 2883584 | tf_op jit(solution)/shard_map/while/body/pallas_call | solution.py:90
  232.9 1.9 collective-permute-start.1
  234.9 9.2 %body.5 = f32[4,512,128]{2,1,0:T(8,128)S(1)} custom-call(s32[1]{0:T(128)} %bitcast.71.step_ref, s32[3]{0:T(128)S(1)} %get-tuple-element.329.meta_ref, s32[1,512]{1,0:T(1,128)S(1)} %get-tuple-element.330.valid_ref, s32[512,1]{1,0:T(8,128)S(1)} %get-tuple-element.331.seg_ref, ...), custom_call_target="tpu_custom_call", output_to_operand_aliasing={{}: (6, {})} | custom-call | flops 402653184 | bytes 2883584 | tf_op jit(solution)/shard_map/while/body/pallas_call | solution.py:90
  244.1 1.5 collective-permute-done.1
  245.6 1.9 collective-permute-start.1
  247.5 9.2 %body.5 = f32[4,512,128]{2,1,0:T(8,128)S(1)} custom-call(s32[1]{0:T(128)} %bitcast.71.step_ref, s32[3]{0:T(128)S(1)} %get-tuple-element.329.meta_ref, s32[1,512]{1,0:T(1,128)S(1)} %get-tuple-element.330.valid_ref, s32[512,1]{1,0:T(8,128)S(1)} %get-tuple-element.331.seg_ref, ...), custom_call_target="tpu_custom_call", output_to_operand_aliasing={{}: (6, {})} | custom-call | flops 402653184 | bytes 2883584 | tf_op jit(solution)/shard_map/while/body/pallas_call | solution.py:90
  256.7 1.5 collective-permute-done.1
  258.3 1.9 collective-permute-start.1
  260.2 9.2 %body.5 = f32[4,512,128]{2,1,0:T(8,128)S(1)} custom-call(s32[1]{0:T(128)} %bitcast.71.step_ref, s32[3]{0:T(128)S(1)} %get-tuple-element.329.meta_ref, s32[1,512]{1,0:T(1,128)S(1)} %get-tuple-element.330.valid_ref, s32[512,1]{1,0:T(8,128)S(1)} %get-tuple-element.331.seg_ref, ...), custom_call_target="tpu_custom_call", output_to_operand_aliasing={{}: (6, {})} | custom-call | flops 402653184 | bytes 2883584 | tf_op jit(solution)/shard_map/while/body/pallas_call | solution.py:90
  269.4 1.5 collective-permute-done.1
  270.9 1.9 collective-permute-start.1
  272.9 9.2 %body.5 = f32[4,512,128]{2,1,0:T(8,128)S(1)} custom-call(s32[1]{0:T(128)} %bitcast.71.step_ref, s32[3]{0:T(128)S(1)} %get-tuple-element.329.meta_ref, s32[1,512]{1,0:T(1,128)S(1)} %get-tuple-element.330.valid_ref, s32[512,1]{1,0:T(8,128)S(1)} %get-tuple-element.331.seg_ref, ...), custom_call_target="tpu_custom_call", output_to_operand_aliasing={{}: (6, {})} | custom-call | flops 402653184 | bytes 2883584 | tf_op jit(solution)/shard_map/while/body/pallas_call | solution.py:90
  282.1 1.5 collective-permute-done.1
  283.5 8.3 %shard_map.105 = f32[4,512,128]{2,1,0:T(8,128)S(1)} custom-call(s32[1]{0:T(128)} %constant.64.clone.1.step_ref, s32[3]{0:T(128)S(1)} %get-tuple-element.355, s32[1,512]{1,0:T(1,128)S(1)} %get-tuple-element.350, s32[512,1]{1,0:T(8,128)S(1)} %get-tuple-element.341, bf16[4,512,64]{2,1,0:T(8,128)(2,1)S(1)} %get-tuple-element.335, ...), custom_call_target="tpu_custom_call", output_to_operand_aliasing={{}: (6, {})} | custom-call | flops 402653184 | bytes 2883584 | tf_op jit(solution)/shard_map/pallas_call | solution.py:90
  293.3 2.7 collective-permute-start.6
  296.0 1.7 collective-permute-start.7
  301.7 5.5 %collective-permute-done.7 = bf16[512,256]{0,1:T(8,128)(2,1)S(1)} collective-permute-done((bf16[512,256]{0,1:T(8,128)(2,1)S(1)}, bf16[512,256]{0,1:T(8,128)(2,1)S(1)}, u32[]{:S(2)}, u32[]{:S(2)}) %collective-permute-start.7) | collective-permute-done | bytes 262176 | tf_op jit(solution)/shard_map/ppermute | solution.py:106
  308.9 2.8 fusion.5
  (137 shorter events, 33.3 us)
Async XLA Ops:
  0.6 30.8 %copy-start.4 = (bf16[2048,256]{1,0:T(8,128)(2,1)S(1)}, bf16[2048,256]{1,0:T(8,128)(2,1)}, u32[]{:S(2)}) copy-start(bf16[2048,256]{1,0:T(8,128)(2,1)} %param.16) | copy-start | bytes 3145732
  0.6 38.9 %collective-permute-start.2 = (bf16[512,512]{1,0:T(8,128)(2,1)}, bf16[512,512]{1,0:T(8,128)(2,1)}, u32[]{:S(2)}, u32[]{:S(2)}) collective-permute-start(bf16[512,512]{1,0:T(8,128)(2,1)} %param.13), channel_id=1, source_target_pairs={{0,1},{1,2},{2,3},{3,0},{4,5},{5,6},{6,7},{7,4},{8,9},{9,10},{10,1... | collective-permute-start | bytes 1572872 | tf_op jit(solution)/shard_map/ppermute | solution.py:106
  2.6 38.1 %collective-permute-start.3 = (bf16[512,512]{1,0:T(8,128)(2,1)}, bf16[512,512]{1,0:T(8,128)(2,1)}, u32[]{:S(2)}, u32[]{:S(2)}) collective-permute-start(bf16[512,512]{1,0:T(8,128)(2,1)} %param.13), channel_id=1, source_target_pairs={{0,2},{1,3},{2,0},{3,1},{4,6},{5,7},{6,4},{7,5},{8,10},{9,11},{10,... | collective-permute-start | bytes 1572872 | tf_op jit(solution)/shard_map/ppermute | solution.py:106
  5.9 34.9 %collective-permute-start.4 = (bf16[512,512]{1,0:T(8,128)(2,1)}, bf16[512,512]{1,0:T(8,128)(2,1)}, u32[]{:S(2)}, u32[]{:S(2)}) collective-permute-start(bf16[512,512]{1,0:T(8,128)(2,1)} %param.13), channel_id=1, source_target_pairs={{0,3},{1,0},{2,1},{3,2},{4,7},{5,4},{6,5},{7,6},{8,11},{9,8},{10,9... | collective-permute-start | bytes 1572872 | tf_op jit(solution)/shard_map/ppermute | solution.py:106
  6.9 31.8 %collective-permute-start.9 = (s32[4]{0:T(128)}, s32[4]{0:T(128)S(1)}, u32[]{:S(2)}, u32[]{:S(2)}) collective-permute-start(s32[4]{0:T(128)} %param.21), channel_id=1, source_target_pairs={{0,4},{4,8},{8,12},{12,16},{16,20},{20,24},{24,28},{28,32},{32,36}... | collective-permute-start | bytes 56 | tf_op jit(solution)/shard_map/ppermute | solution.py:116
  13.4 47.9 %all-to-all-start = ((s32[64,1,1]{2,1,0:T(1,128)}), s32[64,1,1]{2,1,0:T(1,128)S(1)}, u32[]{:S(2)}, u32[]{:S(2)}) async-start(s32[64,1,1]{2,1,0:T(1,128)} %broadcast_in_dim.104), calls=%async_computation | async-start | bytes 65536 | tf_op jit(solution)/shard_map/all_to_all | solution.py:155
  29.1 3.8 %copy-start.15 = (s32[512]{0:T(512)S(1)}, s32[512]{0:T(512)}, u32[]{:S(2)}) copy-start(s32[512]{0:T(512)} %param.19) | copy-start | bytes 6148
  29.1 3.8 %copy-start.5 = (bf16[2048,256]{1,0:T(8,128)(2,1)S(1)}, bf16[2048,256]{1,0:T(8,128)(2,1)}, u32[]{:S(2)}) copy-start(bf16[2048,256]{1,0:T(8,128)(2,1)} %param.17) | copy-start | bytes 3145732
  31.4 3.0 copy-start.6
  34.4 4.3 %copy-start.16 = (s32[4]{0:T(128)S(1)}, s32[4]{0:T(128)}, u32[]{:S(2)}) copy-start(s32[4]{0:T(128)} %param.21) | copy-start | bytes 52
  34.5 6.3 %copy-start.12 = (bf16[512,512]{1,0:T(8,128)(2,1)S(1)}, bf16[512,512]{1,0:T(8,128)(2,1)}, u32[]{:S(2)}) copy-start(bf16[512,512]{1,0:T(8,128)(2,1)} %param.13) | copy-start | bytes 1572868
  48.7 2.9 copy-start.8
  51.6 1.3 copy-start.7
  52.9 1.3 copy-start.9
  54.3 1.3 copy-start.10
  54.3 1.3 copy-start.11
  58.3 18.1 %copy-start.3 = (bf16[512,4,32]{2,0,1:T(8,128)(2,1)S(1)}, bf16[512,4,32]{2,0,1:T(8,128)(2,1)}, u32[]{:S(2)}) copy-start(bf16[512,4,32]{2,0,1:T(8,128)(2,1)} %get-tuple-element.184) | copy-start | bytes 393220
  59.3 34.0 %collective-permute-start.5 = (bf16[4,512,128]{2,1,0:T(8,128)(2,1)}, bf16[4,512,128]{2,1,0:T(8,128)(2,1)S(1)}, u32[]{:S(2)}, u32[]{:S(2)}) collective-permute-start(bf16[4,512,128]{2,1,0:T(8,128)(2,1)} %select_bitcast_fusion.kv_ref), channel_id=1, source_target_pairs={{0,4},{4,8},{8,12},{12,16},{16,20},{20,24},{24,28},{28,32},{32,36}... | collective-permute-start | bytes 1572872 | tf_op jit(solution)/shard_map/ppermute | solution.py:204
  61.4 16.5 %copy-start.14 = (s32[512]{0:T(512)S(1)}, s32[512]{0:T(512)}, u32[]{:S(2)}) copy-start(s32[512]{0:T(512)} %param.20) | copy-start | bytes 6148
  61.4 247.5 %all-to-all-start.1 = ((bf16[256,4,512]{2,0,1:T(8,128)(2,1)}), bf16[256,4,512]{2,0,1:T(8,128)(2,1)}, u32[]{:S(2)}, u32[]{:S(2)}) async-start(bf16[256,4,512]{2,0,1:T(8,128)(2,1)} %copy.122), calls=%async_computation.1 | async-start | bytes 2097152 | tf_op jit(solution)/shard_map/all_to_all | solution.py:184
  93.7 3.2 %copy-start.1 = (bf16[4,512,128]{2,1,0:T(8,128)(2,1)}, bf16[4,512,128]{2,1,0:T(8,128)(2,1)S(1)}, u32[]{:S(2)}) copy-start(bf16[4,512,128]{2,1,0:T(8,128)(2,1)S(1)} %copy.156.kv_ref) | copy-start | bytes 1572868 | tf_op jit(solution)/shard_map/while
  93.7 12.6 %collective-permute-start.1 = (bf16[4,512,128]{2,1,0:T(8,128)(2,1)S(1)}, bf16[4,512,128]{2,1,0:T(8,128)(2,1)S(1)}, u32[]{:S(2)}, u32[]{:S(2)}) collective-permute-start(bf16[4,512,128]{2,1,0:T(8,128)(2,1)S(1)} %copy.156.kv_ref), channel_id=1, source_target_pairs={{0,4},{4,8},{8,12},{12,16},{16,20},{20,24},{24,28},{28,32},{32,36}... | collective-permute-start | bytes 1572872 | tf_op jit(solution)/shard_map/while/body/ppermute | solution.py:210
  106.3 1.9 copy-start.1
  106.3 12.6 %collective-permute-start.1 = (bf16[4,512,128]{2,1,0:T(8,128)(2,1)S(1)}, bf16[4,512,128]{2,1,0:T(8,128)(2,1)S(1)}, u32[]{:S(2)}, u32[]{:S(2)}) collective-permute-start(bf16[4,512,128]{2,1,0:T(8,128)(2,1)S(1)} %copy.156.kv_ref), channel_id=1, source_target_pairs={{0,4},{4,8},{8,12},{12,16},{16,20},{20,24},{24,28},{28,32},{32,36}... | collective-permute-start | bytes 1572872 | tf_op jit(solution)/shard_map/while/body/ppermute | solution.py:210
  119.0 1.9 copy-start.1
  119.0 12.6 %collective-permute-start.1 = (bf16[4,512,128]{2,1,0:T(8,128)(2,1)S(1)}, bf16[4,512,128]{2,1,0:T(8,128)(2,1)S(1)}, u32[]{:S(2)}, u32[]{:S(2)}) collective-permute-start(bf16[4,512,128]{2,1,0:T(8,128)(2,1)S(1)} %copy.156.kv_ref), channel_id=1, source_target_pairs={{0,4},{4,8},{8,12},{12,16},{16,20},{20,24},{24,28},{28,32},{32,36}... | collective-permute-start | bytes 1572872 | tf_op jit(solution)/shard_map/while/body/ppermute | solution.py:210
  131.7 1.9 copy-start.1
  131.7 12.6 %collective-permute-start.1 = (bf16[4,512,128]{2,1,0:T(8,128)(2,1)S(1)}, bf16[4,512,128]{2,1,0:T(8,128)(2,1)S(1)}, u32[]{:S(2)}, u32[]{:S(2)}) collective-permute-start(bf16[4,512,128]{2,1,0:T(8,128)(2,1)S(1)} %copy.156.kv_ref), channel_id=1, source_target_pairs={{0,4},{4,8},{8,12},{12,16},{16,20},{20,24},{24,28},{28,32},{32,36}... | collective-permute-start | bytes 1572872 | tf_op jit(solution)/shard_map/while/body/ppermute | solution.py:210
  144.3 1.9 copy-start.1
  144.3 12.6 %collective-permute-start.1 = (bf16[4,512,128]{2,1,0:T(8,128)(2,1)S(1)}, bf16[4,512,128]{2,1,0:T(8,128)(2,1)S(1)}, u32[]{:S(2)}, u32[]{:S(2)}) collective-permute-start(bf16[4,512,128]{2,1,0:T(8,128)(2,1)S(1)} %copy.156.kv_ref), channel_id=1, source_target_pairs={{0,4},{4,8},{8,12},{12,16},{16,20},{20,24},{24,28},{28,32},{32,36}... | collective-permute-start | bytes 1572872 | tf_op jit(solution)/shard_map/while/body/ppermute | solution.py:210
  157.0 1.9 copy-start.1
  157.0 12.6 %collective-permute-start.1 = (bf16[4,512,128]{2,1,0:T(8,128)(2,1)S(1)}, bf16[4,512,128]{2,1,0:T(8,128)(2,1)S(1)}, u32[]{:S(2)}, u32[]{:S(2)}) collective-permute-start(bf16[4,512,128]{2,1,0:T(8,128)(2,1)S(1)} %copy.156.kv_ref), channel_id=1, source_target_pairs={{0,4},{4,8},{8,12},{12,16},{16,20},{20,24},{24,28},{28,32},{32,36}... | collective-permute-start | bytes 1572872 | tf_op jit(solution)/shard_map/while/body/ppermute | solution.py:210
  169.6 1.9 copy-start.1
  169.6 12.6 %collective-permute-start.1 = (bf16[4,512,128]{2,1,0:T(8,128)(2,1)S(1)}, bf16[4,512,128]{2,1,0:T(8,128)(2,1)S(1)}, u32[]{:S(2)}, u32[]{:S(2)}) collective-permute-start(bf16[4,512,128]{2,1,0:T(8,128)(2,1)S(1)} %copy.156.kv_ref), channel_id=1, source_target_pairs={{0,4},{4,8},{8,12},{12,16},{16,20},{20,24},{24,28},{28,32},{32,36}... | collective-permute-start | bytes 1572872 | tf_op jit(solution)/shard_map/while/body/ppermute | solution.py:210
  182.3 1.9 copy-start.1
  182.3 12.6 %collective-permute-start.1 = (bf16[4,512,128]{2,1,0:T(8,128)(2,1)S(1)}, bf16[4,512,128]{2,1,0:T(8,128)(2,1)S(1)}, u32[]{:S(2)}, u32[]{:S(2)}) collective-permute-start(bf16[4,512,128]{2,1,0:T(8,128)(2,1)S(1)} %copy.156.kv_ref), channel_id=1, source_target_pairs={{0,4},{4,8},{8,12},{12,16},{16,20},{20,24},{24,28},{28,32},{32,36}... | collective-permute-start | bytes 1572872 | tf_op jit(solution)/shard_map/while/body/ppermute | solution.py:210
  195.0 1.9 copy-start.1
  195.0 12.6 %collective-permute-start.1 = (bf16[4,512,128]{2,1,0:T(8,128)(2,1)S(1)}, bf16[4,512,128]{2,1,0:T(8,128)(2,1)S(1)}, u32[]{:S(2)}, u32[]{:S(2)}) collective-permute-start(bf16[4,512,128]{2,1,0:T(8,128)(2,1)S(1)} %copy.156.kv_ref), channel_id=1, source_target_pairs={{0,4},{4,8},{8,12},{12,16},{16,20},{20,24},{24,28},{28,32},{32,36}... | collective-permute-start | bytes 1572872 | tf_op jit(solution)/shard_map/while/body/ppermute | solution.py:210
  207.6 1.9 copy-start.1
  207.6 12.6 %collective-permute-start.1 = (bf16[4,512,128]{2,1,0:T(8,128)(2,1)S(1)}, bf16[4,512,128]{2,1,0:T(8,128)(2,1)S(1)}, u32[]{:S(2)}, u32[]{:S(2)}) collective-permute-start(bf16[4,512,128]{2,1,0:T(8,128)(2,1)S(1)} %copy.156.kv_ref), channel_id=1, source_target_pairs={{0,4},{4,8},{8,12},{12,16},{16,20},{20,24},{24,28},{28,32},{32,36}... | collective-permute-start | bytes 1572872 | tf_op jit(solution)/shard_map/while/body/ppermute | solution.py:210
  220.3 1.9 copy-start.1
  220.3 12.6 %collective-permute-start.1 = (bf16[4,512,128]{2,1,0:T(8,128)(2,1)S(1)}, bf16[4,512,128]{2,1,0:T(8,128)(2,1)S(1)}, u32[]{:S(2)}, u32[]{:S(2)}) collective-permute-start(bf16[4,512,128]{2,1,0:T(8,128)(2,1)S(1)} %copy.156.kv_ref), channel_id=1, source_target_pairs={{0,4},{4,8},{8,12},{12,16},{16,20},{20,24},{24,28},{28,32},{32,36}... | collective-permute-start | bytes 1572872 | tf_op jit(solution)/shard_map/while/body/ppermute | solution.py:210
  232.9 1.9 copy-start.1
  232.9 12.6 %collective-permute-start.1 = (bf16[4,512,128]{2,1,0:T(8,128)(2,1)S(1)}, bf16[4,512,128]{2,1,0:T(8,128)(2,1)S(1)}, u32[]{:S(2)}, u32[]{:S(2)}) collective-permute-start(bf16[4,512,128]{2,1,0:T(8,128)(2,1)S(1)} %copy.156.kv_ref), channel_id=1, source_target_pairs={{0,4},{4,8},{8,12},{12,16},{16,20},{20,24},{24,28},{28,32},{32,36}... | collective-permute-start | bytes 1572872 | tf_op jit(solution)/shard_map/while/body/ppermute | solution.py:210
  245.6 1.9 copy-start.1
  245.6 12.6 %collective-permute-start.1 = (bf16[4,512,128]{2,1,0:T(8,128)(2,1)S(1)}, bf16[4,512,128]{2,1,0:T(8,128)(2,1)S(1)}, u32[]{:S(2)}, u32[]{:S(2)}) collective-permute-start(bf16[4,512,128]{2,1,0:T(8,128)(2,1)S(1)} %copy.156.kv_ref), channel_id=1, source_target_pairs={{0,4},{4,8},{8,12},{12,16},{16,20},{20,24},{24,28},{28,32},{32,36}... | collective-permute-start | bytes 1572872 | tf_op jit(solution)/shard_map/while/body/ppermute | solution.py:210
  258.3 1.9 copy-start.1
  258.3 12.6 %collective-permute-start.1 = (bf16[4,512,128]{2,1,0:T(8,128)(2,1)S(1)}, bf16[4,512,128]{2,1,0:T(8,128)(2,1)S(1)}, u32[]{:S(2)}, u32[]{:S(2)}) collective-permute-start(bf16[4,512,128]{2,1,0:T(8,128)(2,1)S(1)} %copy.156.kv_ref), channel_id=1, source_target_pairs={{0,4},{4,8},{8,12},{12,16},{16,20},{20,24},{24,28},{28,32},{32,36}... | collective-permute-start | bytes 1572872 | tf_op jit(solution)/shard_map/while/body/ppermute | solution.py:210
  270.9 1.9 copy-start.1
  270.9 12.6 %collective-permute-start.1 = (bf16[4,512,128]{2,1,0:T(8,128)(2,1)S(1)}, bf16[4,512,128]{2,1,0:T(8,128)(2,1)S(1)}, u32[]{:S(2)}, u32[]{:S(2)}) collective-permute-start(bf16[4,512,128]{2,1,0:T(8,128)(2,1)S(1)} %copy.156.kv_ref), channel_id=1, source_target_pairs={{0,4},{4,8},{8,12},{12,16},{16,20},{20,24},{24,28},{28,32},{32,36}... | collective-permute-start | bytes 1572872 | tf_op jit(solution)/shard_map/while/body/ppermute | solution.py:210
  292.4 7.4 %copy-start.2 = (bf16[4,128,512]{2,1,0:T(8,128)(2,1)S(1)}, bf16[4,128,512]{2,1,0:T(8,128)(2,1)}, u32[]{:S(2)}) copy-start(bf16[4,128,512]{2,1,0:T(8,128)(2,1)} %broadcast_select_fusion.2) | copy-start | bytes 1572868
  293.3 8.4 %collective-permute-start.6 = (bf16[512,256]{0,1:T(8,128)(2,1)S(1)}, bf16[512,256]{0,1:T(8,128)(2,1)S(1)}, u32[]{:S(2)}, u32[]{:S(2)}) collective-permute-start(bf16[512,256]{0,1:T(8,128)(2,1)S(1)} %bitcast.81), channel_id=1, source_target_pairs={{0,1},{1,2},{2,3},{3,0},{4,5},{5,6},{6,7},{7,4},{8,9},{9,10},{10,1... | collective-permute-start | bytes 786440 | tf_op jit(solution)/shard_map/ppermute | solution.py:106
  296.0 11.1 %collective-permute-start.7 = (bf16[512,256]{0,1:T(8,128)(2,1)S(1)}, bf16[512,256]{0,1:T(8,128)(2,1)S(1)}, u32[]{:S(2)}, u32[]{:S(2)}) collective-permute-start(bf16[512,256]{0,1:T(8,128)(2,1)S(1)} %bitcast.82), channel_id=1, source_target_pairs={{0,2},{1,3},{2,0},{3,1},{4,6},{5,7},{6,4},{7,5},{8,10},{9,11},{10,... | collective-permute-start | bytes 786440 | tf_op jit(solution)/shard_map/ppermute | solution.py:106
  297.7 9.4 %collective-permute-start.8 = (bf16[512,256]{0,1:T(8,128)(2,1)S(1)}, bf16[512,256]{0,1:T(8,128)(2,1)}, u32[]{:S(2)}, u32[]{:S(2)}) collective-permute-start(bf16[512,256]{0,1:T(8,128)(2,1)S(1)} %bitcast.83), channel_id=1, source_target_pairs={{0,3},{1,0},{2,1},{3,2},{4,7},{5,4},{6,5},{7,6},{8,11},{9,8},{10,9... | collective-permute-start | bytes 786440 | tf_op jit(solution)/shard_map/ppermute | solution.py:106
  307.1 1.8 copy-start.13

commit v4 on v3

--- a/solution.py
+++ b/solution.py
@@ -181,7 +181,6 @@
     )
     packed = jnp.where(token_valid[:, None] > 0, packed, jnp.zeros_like(packed))
 
-    out_cols = lax.all_to_all(out_weight, "tp", 1, 0, tiled=True)
     prev_slot = passed_along(page_slot, "seq", 1)
 
     q_hm = jnp.transpose(queries, (1, 0, 2))
@@ -236,6 +235,8 @@
     found = jnp.any(match, axis=1)
     cache_pages = jnp.where(found[:, None, None], cand_pages[pick], jnp.zeros_like(cand_pages[:1]))
 
+    out_late, attended = lax.optimization_barrier((out_weight, attended))
+    out_cols = lax.all_to_all(out_late, "tp", 1, 0, tiled=True)
     attended_all = tp_gather(attended, tp_count)
     projected = jnp.dot(attended_all, out_cols, preferred_element_type=jnp.float32)
     hidden = (residual.astype(jnp.float32) + projected).astype(jnp.bfloat16)

time: 312 us -> 341 us (1.093); the launches traced: 312 us -> 335 us
  waiting for transfers between devices: 27.6 us -> 131 us
  Pallas kernels: 155 us -> 68.4 us
  starting transfers between devices: 73.4 us -> 82.6 us
    pallas_call x17, Pallas kernels: 155 us -> 68.4 us  [attend_step(): pl.pallas_call(_step_kernel, grid_spec=grid_spec, out_shape=jax.ShapeDtyp...]
    ppermute x15, waiting for transfers between devices: 20.8 us -> 92.8 us  [advance(): sent = lax.ppermute(held, 'seq', pairs)]
    ppermute x6, waiting for transfers between devices: 6.76 us -> 37.9 us  [tp_gather(): lax.ppermute(x, 'tp', [(i, (i + s) % count) for i in range(count)])]
    ppermute x15, starting transfers between devices: 30.1 us -> 37.6 us  [advance(): sent = lax.ppermute(held, 'seq', pairs)]
    reshape x3, local copies, waits for them, and re-layouts: 5.5 us -> 1.96 us  [body(): jnp.concatenate([key_rot[:, :, None, :], values[:, :, None, :]], axis=2)]
  transfers between devices with their start and end apart: 25 -> 25, of which waited for: 17 -> 18; matrix products, arithmetic and copies ran while one was open for 15% -> 12% of each run, Pallas kernels for 50% -> 20%
where the time goes in v4:
time: 341 us; the launch traced here: 335 us
  waiting for transfers between devices  131 us (38%)
  starting transfers between devices  82.6 us (24%)
  Pallas kernels  68.4 us (20%)
  local copies, waits for them, and re-layouts  21.6 us (6%)
  other arithmetic  18.5 us (5%)
  matrix products  7.95 us (2%)
  between operations  4.28 us (1%)
    ppermute x15, waiting for transfers between devices, advance(): sent = lax.ppermute(held, 'seq', pairs)  92.8 us
    pallas_call x17, Pallas kernels, attend_step(): pl.pallas_call(_step_kernel, grid_spec=grid_spec, out_shape=jax.ShapeDtyp...  68.4 us
    ppermute x6, waiting for transfers between devices, tp_gather(): lax.ppermute(x, 'tp', [(i, (i + s) % count) for i in range(count)])  37.9 us
    ppermute x15, starting transfers between devices, advance(): sent = lax.ppermute(held, 'seq', pairs)  37.6 us
    all_to_all x1, starting transfers between devices, body(): out_cols = lax.all_to_all(out_late, 'tp', 1, 0, tiled=True)  15.3 us
    all_to_all x1, starting transfers between devices, body(): cross_steps = jnp.sum(lax.all_to_all(told, 'seq', 0, 0, tiled=True))  13.5 us
    ppermute x6, starting transfers between devices, tp_gather(): lax.ppermute(x, 'tp', [(i, (i + s) % count) for i in range(count)])  12.2 us
  transfers between devices with their start and end apart: 25, of which 18 were waited for; matrix products, arithmetic and copies ran while one was open for 12% of the time, Pallas kernels for 20%

profile of v4, /device:TPU:24, one launch (start us, length us, event | category | flops | bytes accessed | tf_op | source)
XLA Modules:
  0.0 334.7 jit_solution(4013559220490684642)
XLA Ops:
  0.6 2.0 collective-permute-start.2
  2.6 3.3 collective-permute-start.3
  6.9 1.9 collective-permute-start.9
  13.5 13.5 %all-to-all-start = ((s32[64,1,1]{2,1,0:T(1,128)}), s32[64,1,1]{2,1,0:T(1,128)S(1)}, u32[]{:S(2)}, u32[]{:S(2)}) async-start(s32[64,1,1]{2,1,0:T(1,128)} %broadcast_in_dim.104), calls=%async_computation | async-start | bytes 65536 | tf_op jit(solution)/shard_map/all_to_all | solution.py:155
  29.1 2.4 copy.98
  33.6 1.8 multiply_cosine_fusion
  35.4 5.4 %collective-permute-done.3 = bf16[512,512]{1,0:T(8,128)(2,1)} collective-permute-done((bf16[512,512]{1,0:T(8,128)(2,1)}, bf16[512,512]{1,0:T(8,128)(2,1)}, u32[]{:S(2)}, u32[]{:S(2)}) %collective-permute-start.3) | collective-permute-done | bytes 524320 | tf_op jit(solution)/shard_map/ppermute | solution.py:106
  40.8 3.0 pad_maximum_fusion
  43.7 2.3 gather_fusion
  46.7 2.0 fusion.3
  48.7 2.8 copy.97
  51.5 2.5 fusion.22
  60.3 2.1 collective-permute-start.5
  66.1 9.2 %shard_map.104 = f32[4,512,128]{2,1,0:T(8,128)S(1)} custom-call(s32[1]{0:T(128)} %constant.116.clone.1.step_ref, s32[3]{0:T(128)S(1)} %pad_add_fusion.meta_ref, s32[1,512]{1,0:T(1,128)S(1)} %bitcast.86, s32[512,1]{1,0:T(8,128)S(1)} %copy.115.seg_ref, bf16[4,512,64]{2,1,0:T(8,128)(2,1)S(1)} %maximum_bitcast_fusion.q_ref, ...), custom_call_target="tpu_custom_call", output_to_operand_aliasing={{}: (6, {})} | custom-call | flops 402653184 | bytes 2883584 | tf_op jit(solution)/shard_map/pallas_call | solution.py:90
  75.4 76.0 %while.24 = (s32[]{:T(128)}, bf16[4,512,128]{2,1,0:T(8,128)(2,1)S(1)}, f32[4,512,128]{2,1,0:T(8,128)S(1)}, s32[]{:T(128)}, s32[3]{0:T(128)S(1)}, /*index=5*/s32[...) while((s32[]{:T(128)}, bf16[4,512,128]{2,1,0:T(8,128)(2,1)S(1)}, ...), condition=%wide.region_3.4_spmd, body=%wide.region_2.3_spmd.sunk | while | flops 402653184 | bytes 8126633 | solution.py:215
  75.4 3.5 %collective-permute-start = (bf16[4,512,128]{2,1,0:T(8,128)(2,1)S(1)}, bf16[4,512,128]{2,1,0:T(8,128)(2,1)S(1)}, u32[]{:S(2)}, u32[]{:S(2)}) collective-permute-start(bf16[4,512,128]{2,1,0:T(8,128)(2,1)S(1)} %copy.143.kv_ref), channel_id=1, source_target_pairs={{0,4},{4,8},{8,12},{12,16},{16,20},{20,24},{24,28},{28,32},{32,36}... | collective-permute-start | bytes 1572872 | tf_op jit(solution)/shard_map/while/body/ppermute | solution.py:209
  79.0 8.8 %body.4 = f32[4,512,128]{2,1,0:T(8,128)S(1)} custom-call(s32[1]{0:T(128)} %bitcast.70.step_ref, s32[3]{0:T(128)S(1)} %get-tuple-element.309.meta_ref, s32[1,512]{1,0:T(1,128)S(1)} %get-tuple-element.310.valid_ref, s32[512,1]{1,0:T(8,128)S(1)} %get-tuple-element.311.seg_ref, ...), custom_call_target="tpu_custom_call", output_to_operand_aliasing={{}: (6, {})} | custom-call | flops 402653184 | bytes 2883584 | tf_op jit(solution)/shard_map/while/body/pallas_call | solution.py:90
  88.1 1.9 collective-permute-start
  90.0 8.8 %body.4 = f32[4,512,128]{2,1,0:T(8,128)S(1)} custom-call(s32[1]{0:T(128)} %bitcast.70.step_ref, s32[3]{0:T(128)S(1)} %get-tuple-element.309.meta_ref, s32[1,512]{1,0:T(1,128)S(1)} %get-tuple-element.310.valid_ref, s32[512,1]{1,0:T(8,128)S(1)} %get-tuple-element.311.seg_ref, ...), custom_call_target="tpu_custom_call", output_to_operand_aliasing={{}: (6, {})} | custom-call | flops 402653184 | bytes 2883584 | tf_op jit(solution)/shard_map/while/body/pallas_call | solution.py:90
  98.8 1.9 collective-permute-done
  100.8 1.9 collective-permute-start
  102.7 9.2 %body.4 = f32[4,512,128]{2,1,0:T(8,128)S(1)} custom-call(s32[1]{0:T(128)} %bitcast.70.step_ref, s32[3]{0:T(128)S(1)} %get-tuple-element.309.meta_ref, s32[1,512]{1,0:T(1,128)S(1)} %get-tuple-element.310.valid_ref, s32[512,1]{1,0:T(8,128)S(1)} %get-tuple-element.311.seg_ref, ...), custom_call_target="tpu_custom_call", output_to_operand_aliasing={{}: (6, {})} | custom-call | flops 402653184 | bytes 2883584 | tf_op jit(solution)/shard_map/while/body/pallas_call | solution.py:90
  113.4 1.9 collective-permute-start
  115.4 2.6 body.4
  118.0 8.0 %collective-permute-done = bf16[4,512,128]{2,1,0:T(8,128)(2,1)S(1)} collective-permute-done((bf16[4,512,128]{2,1,0:T(8,128)(2,1)S(1)}, bf16[4,512,128]{2,1,0:T(8,128)(2,1)S(1)}, u32[]{:S(2)}, u32[]{:S(2)}) %collective-permute-start) | collective-permute-done | bytes 524320 | tf_op jit(solution)/shard_map/while/body/ppermute | solution.py:209
  126.1 1.9 collective-permute-start
  128.0 2.6 body.4
  130.7 8.0 %collective-permute-done = bf16[4,512,128]{2,1,0:T(8,128)(2,1)S(1)} collective-permute-done((bf16[4,512,128]{2,1,0:T(8,128)(2,1)S(1)}, bf16[4,512,128]{2,1,0:T(8,128)(2,1)S(1)}, u32[]{:S(2)}, u32[]{:S(2)}) %collective-permute-start) | collective-permute-done | bytes 524320 | tf_op jit(solution)/shard_map/while/body/ppermute | solution.py:209
  138.8 1.9 collective-permute-start
  140.7 2.6 body.4
  143.3 8.0 %collective-permute-done = bf16[4,512,128]{2,1,0:T(8,128)(2,1)S(1)} collective-permute-done((bf16[4,512,128]{2,1,0:T(8,128)(2,1)S(1)}, bf16[4,512,128]{2,1,0:T(8,128)(2,1)S(1)}, u32[]{:S(2)}, u32[]{:S(2)}) %collective-permute-start) | collective-permute-done | bytes 524320 | tf_op jit(solution)/shard_map/while/body/ppermute | solution.py:209
  151.4 113.9 %while.25 = (s32[]{:T(128)}, bf16[4,512,128]{2,1,0:T(8,128)(2,1)S(1)}, f32[4,512,128]{2,1,0:T(8,128)S(1)}, s32[3]{0:T(128)S(1)}, s32[1,512]{1,0:T(1,128)S(1)}, /...) while((s32[]{:T(128)}, bf16[4,512,128]{2,1,0:T(8,128)(2,1)S(1)}, ...), condition=%wide.region_5.6_spmd, body=%wide.region_4.5_spmd.sunk | while | flops 402653184 | bytes 8126625 | solution.py:216
  151.4 1.9 collective-permute-start.1
  153.4 2.6 body.5
  156.0 8.0 %collective-permute-done.1 = bf16[4,512,128]{2,1,0:T(8,128)(2,1)S(1)} collective-permute-done((bf16[4,512,128]{2,1,0:T(8,128)(2,1)S(1)}, bf16[4,512,128]{2,1,0:T(8,128)(2,1)S(1)}, u32[]{:S(2)}, u32[]{:S(2)}) %collective-permute-start.1) | collective-permute-done | bytes 524320 | tf_op jit(solution)/shard_map/while/body/ppermute | solution.py:209
  164.1 1.9 collective-permute-start.1
  166.0 2.6 body.5
  168.7 8.0 %collective-permute-done.1 = bf16[4,512,128]{2,1,0:T(8,128)(2,1)S(1)} collective-permute-done((bf16[4,512,128]{2,1,0:T(8,128)(2,1)S(1)}, bf16[4,512,128]{2,1,0:T(8,128)(2,1)S(1)}, u32[]{:S(2)}, u32[]{:S(2)}) %collective-permute-start.1) | collective-permute-done | bytes 524320 | tf_op jit(solution)/shard_map/while/body/ppermute | solution.py:209
  176.7 1.9 collective-permute-start.1
  178.7 2.6 body.5
  181.3 8.0 %collective-permute-done.1 = bf16[4,512,128]{2,1,0:T(8,128)(2,1)S(1)} collective-permute-done((bf16[4,512,128]{2,1,0:T(8,128)(2,1)S(1)}, bf16[4,512,128]{2,1,0:T(8,128)(2,1)S(1)}, u32[]{:S(2)}, u32[]{:S(2)}) %collective-permute-start.1) | collective-permute-done | bytes 524320 | tf_op jit(solution)/shard_map/while/body/ppermute | solution.py:209
  189.4 1.9 collective-permute-start.1
  191.3 2.6 body.5
  194.0 8.0 %collective-permute-done.1 = bf16[4,512,128]{2,1,0:T(8,128)(2,1)S(1)} collective-permute-done((bf16[4,512,128]{2,1,0:T(8,128)(2,1)S(1)}, bf16[4,512,128]{2,1,0:T(8,128)(2,1)S(1)}, u32[]{:S(2)}, u32[]{:S(2)}) %collective-permute-start.1) | collective-permute-done | bytes 524320 | tf_op jit(solution)/shard_map/while/body/ppermute | solution.py:209
  202.1 1.9 collective-permute-start.1
  204.0 2.6 body.5
  206.6 8.0 %collective-permute-done.1 = bf16[4,512,128]{2,1,0:T(8,128)(2,1)S(1)} collective-permute-done((bf16[4,512,128]{2,1,0:T(8,128)(2,1)S(1)}, bf16[4,512,128]{2,1,0:T(8,128)(2,1)S(1)}, u32[]{:S(2)}, u32[]{:S(2)}) %collective-permute-start.1) | collective-permute-done | bytes 524320 | tf_op jit(solution)/shard_map/while/body/ppermute | solution.py:209
  214.7 1.9 collective-permute-start.1
  216.7 2.6 body.5
  219.3 8.0 %collective-permute-done.1 = bf16[4,512,128]{2,1,0:T(8,128)(2,1)S(1)} collective-permute-done((bf16[4,512,128]{2,1,0:T(8,128)(2,1)S(1)}, bf16[4,512,128]{2,1,0:T(8,128)(2,1)S(1)}, u32[]{:S(2)}, u32[]{:S(2)}) %collective-permute-start.1) | collective-permute-done | bytes 524320 | tf_op jit(solution)/shard_map/while/body/ppermute | solution.py:209
  227.4 6.4 %collective-permute-start.1 = (bf16[4,512,128]{2,1,0:T(8,128)(2,1)S(1)}, bf16[4,512,128]{2,1,0:T(8,128)(2,1)S(1)}, u32[]{:S(2)}, u32[]{:S(2)}) collective-permute-start(bf16[4,512,128]{2,1,0:T(8,128)(2,1)S(1)} %copy.152.kv_ref), channel_id=1, source_target_pairs={{0,4},{4,8},{8,12},{12,16},{16,20},{20,24},{24,28},{28,32},{32,36}... | collective-permute-start | bytes 1572872 | tf_op jit(solution)/shard_map/while/body/ppermute | solution.py:209
  233.8 2.6 body.5
  236.5 3.5 %collective-permute-done.1 = bf16[4,512,128]{2,1,0:T(8,128)(2,1)S(1)} collective-permute-done((bf16[4,512,128]{2,1,0:T(8,128)(2,1)S(1)}, bf16[4,512,128]{2,1,0:T(8,128)(2,1)S(1)}, u32[]{:S(2)}, u32[]{:S(2)}) %collective-permute-start.1) | collective-permute-done | bytes 524320 | tf_op jit(solution)/shard_map/while/body/ppermute | solution.py:209
  240.0 4.3 %collective-permute-start.1 = (bf16[4,512,128]{2,1,0:T(8,128)(2,1)S(1)}, bf16[4,512,128]{2,1,0:T(8,128)(2,1)S(1)}, u32[]{:S(2)}, u32[]{:S(2)}) collective-permute-start(bf16[4,512,128]{2,1,0:T(8,128)(2,1)S(1)} %copy.152.kv_ref), channel_id=1, source_target_pairs={{0,4},{4,8},{8,12},{12,16},{16,20},{20,24},{24,28},{28,32},{32,36}... | collective-permute-start | bytes 1572872 | tf_op jit(solution)/shard_map/while/body/ppermute | solution.py:209
  244.4 2.6 body.5
  247.0 5.6 %collective-permute-done.1 = bf16[4,512,128]{2,1,0:T(8,128)(2,1)S(1)} collective-permute-done((bf16[4,512,128]{2,1,0:T(8,128)(2,1)S(1)}, bf16[4,512,128]{2,1,0:T(8,128)(2,1)S(1)}, u32[]{:S(2)}, u32[]{:S(2)}) %collective-permute-start.1) | collective-permute-done | bytes 524320 | tf_op jit(solution)/shard_map/while/body/ppermute | solution.py:209
  252.7 2.2 collective-permute-start.1
  254.9 2.6 body.5
  257.6 7.7 %collective-permute-done.1 = bf16[4,512,128]{2,1,0:T(8,128)(2,1)S(1)} collective-permute-done((bf16[4,512,128]{2,1,0:T(8,128)(2,1)S(1)}, bf16[4,512,128]{2,1,0:T(8,128)(2,1)S(1)}, u32[]{:S(2)}, u32[]{:S(2)}) %collective-permute-start.1) | collective-permute-done | bytes 524320 | tf_op jit(solution)/shard_map/while/body/ppermute | solution.py:209
  270.5 15.3 %all-to-all-start.1 = ((bf16[256,4,512]{2,0,1:T(8,128)(2,1)}), bf16[256,4,512]{2,0,1:T(8,128)(2,1)}, u32[]{:S(2)}, u32[]{:S(2)}) async-start(bf16[256,4,512]{2,0,1:T(8,128)(2,1)} %copy.118), calls=%async_computation.1 | async-start | bytes 2097152 | tf_op jit(solution)/shard_map/all_to_all | solution.py:239
  288.5 3.1 collective-permute-start.6
  296.9 16.7 %collective-permute-done.6 = bf16[512,256]{0,1:T(8,128)(2,1)S(1)} collective-permute-done((bf16[512,256]{0,1:T(8,128)(2,1)S(1)}, bf16[512,256]{0,1:T(8,128)(2,1)S(1)}, u32[]{:S(2)}, u32[]{:S(2)}) %collective-permute-start.6) | collective-permute-done | bytes 262176 | tf_op jit(solution)/shard_map/ppermute | solution.py:106
  313.6 15.8 %collective-permute-done.7 = bf16[512,256]{0,1:T(8,128)(2,1)S(1)} collective-permute-done((bf16[512,256]{0,1:T(8,128)(2,1)S(1)}, bf16[512,256]{0,1:T(8,128)(2,1)S(1)}, u32[]{:S(2)}, u32[]{:S(2)}) %collective-permute-start.7) | collective-permute-done | bytes 262176 | tf_op jit(solution)/shard_map/ppermute | solution.py:106
  331.9 2.8 fusion.5
  (131 shorter events, 35.2 us)
Async XLA Ops:
  0.6 30.9 %copy-start.4 = (bf16[2048,256]{1,0:T(8,128)(2,1)S(1)}, bf16[2048,256]{1,0:T(8,128)(2,1)}, u32[]{:S(2)}) copy-start(bf16[2048,256]{1,0:T(8,128)(2,1)} %param.16) | copy-start | bytes 3145732
  0.6 34.8 %collective-permute-start.2 = (bf16[512,512]{1,0:T(8,128)(2,1)}, bf16[512,512]{1,0:T(8,128)(2,1)}, u32[]{:S(2)}, u32[]{:S(2)}) collective-permute-start(bf16[512,512]{1,0:T(8,128)(2,1)} %param.13), channel_id=1, source_target_pairs={{0,1},{1,2},{2,3},{3,0},{4,5},{5,6},{6,7},{7,4},{8,9},{9,10},{10,1... | collective-permute-start | bytes 1572872 | tf_op jit(solution)/shard_map/ppermute | solution.py:106
  2.6 38.1 %collective-permute-start.3 = (bf16[512,512]{1,0:T(8,128)(2,1)}, bf16[512,512]{1,0:T(8,128)(2,1)}, u32[]{:S(2)}, u32[]{:S(2)}) collective-permute-start(bf16[512,512]{1,0:T(8,128)(2,1)} %param.13), channel_id=1, source_target_pairs={{0,2},{1,3},{2,0},{3,1},{4,6},{5,7},{6,4},{7,5},{8,10},{9,11},{10,... | collective-permute-start | bytes 1572872 | tf_op jit(solution)/shard_map/ppermute | solution.py:106
  5.9 34.9 %collective-permute-start.4 = (bf16[512,512]{1,0:T(8,128)(2,1)}, bf16[512,512]{1,0:T(8,128)(2,1)}, u32[]{:S(2)}, u32[]{:S(2)}) collective-permute-start(bf16[512,512]{1,0:T(8,128)(2,1)} %param.13), channel_id=1, source_target_pairs={{0,3},{1,0},{2,1},{3,2},{4,7},{5,4},{6,5},{7,6},{8,11},{9,8},{10,9... | collective-permute-start | bytes 1572872 | tf_op jit(solution)/shard_map/ppermute | solution.py:106
  6.9 56.4 %collective-permute-start.9 = (s32[4]{0:T(128)}, s32[4]{0:T(128)S(1)}, u32[]{:S(2)}, u32[]{:S(2)}) collective-permute-start(s32[4]{0:T(128)} %param.21), channel_id=1, source_target_pairs={{0,4},{4,8},{8,12},{12,16},{16,20},{20,24},{24,28},{28,32},{32,36}... | collective-permute-start | bytes 56 | tf_op jit(solution)/shard_map/ppermute | solution.py:116
  13.5 49.8 %all-to-all-start = ((s32[64,1,1]{2,1,0:T(1,128)}), s32[64,1,1]{2,1,0:T(1,128)S(1)}, u32[]{:S(2)}, u32[]{:S(2)}) async-start(s32[64,1,1]{2,1,0:T(1,128)} %broadcast_in_dim.104), calls=%async_computation | async-start | bytes 65536 | tf_op jit(solution)/shard_map/all_to_all | solution.py:155
  29.1 3.0 copy-start.5
  31.5 2.1 copy-start.12
  32.1 8.6 %copy-start.8 = (bf16[512,512]{1,0:T(8,128)(2,1)S(1)}, bf16[512,512]{1,0:T(8,128)(2,1)}, u32[]{:S(2)}) copy-start(bf16[512,512]{1,0:T(8,128)(2,1)} %param.13) | copy-start | bytes 1572868
  54.0 1.3 copy-start.6
  55.4 1.3 copy-start.7
  58.7 7.3 %copy-start.2 = (bf16[512,4,2,64]{3,0,1,2:T(8,128)(2,1)}, bf16[512,4,2,64]{3,0,1,2:T(8,128)(2,1)S(1)}, u32[]{:S(2)}) copy-start(bf16[512,4,2,64]{3,0,1,2:T(8,128)(2,1)S(1)} %pad_maximum_fusion.1) | copy-start | bytes 1572868
  59.3 6.8 %copy-start.10 = (s32[512]{0:T(512)S(1)}, s32[512]{0:T(512)}, u32[]{:S(2)}) copy-start(s32[512]{0:T(512)} %param.20) | copy-start | bytes 6148
  60.3 15.1 %collective-permute-start.5 = (bf16[4,512,128]{2,1,0:T(8,128)(2,1)}, bf16[4,512,128]{2,1,0:T(8,128)(2,1)S(1)}, u32[]{:S(2)}, u32[]{:S(2)}) collective-permute-start(bf16[4,512,128]{2,1,0:T(8,128)(2,1)} %select_bitcast_fusion.kv_ref), channel_id=1, source_target_pairs={{0,4},{4,8},{8,12},{12,16},{16,20},{20,24},{24,28},{28,32},{32,36}... | collective-permute-start | bytes 1572872 | tf_op jit(solution)/shard_map/ppermute | solution.py:203
  75.4 3.5 %copy-start = (bf16[4,512,128]{2,1,0:T(8,128)(2,1)}, bf16[4,512,128]{2,1,0:T(8,128)(2,1)S(1)}, u32[]{:S(2)}) copy-start(bf16[4,512,128]{2,1,0:T(8,128)(2,1)S(1)} %copy.143.kv_ref) | copy-start | bytes 1572868 | tf_op jit(solution)/shard_map/while
  75.4 12.6 %collective-permute-start = (bf16[4,512,128]{2,1,0:T(8,128)(2,1)S(1)}, bf16[4,512,128]{2,1,0:T(8,128)(2,1)S(1)}, u32[]{:S(2)}, u32[]{:S(2)}) collective-permute-start(bf16[4,512,128]{2,1,0:T(8,128)(2,1)S(1)} %copy.143.kv_ref), channel_id=1, source_target_pairs={{0,4},{4,8},{8,12},{12,16},{16,20},{20,24},{24,28},{28,32},{32,36}... | collective-permute-start | bytes 1572872 | tf_op jit(solution)/shard_map/while/body/ppermute | solution.py:209
  88.1 1.9 copy-start
  88.1 12.6 %collective-permute-start = (bf16[4,512,128]{2,1,0:T(8,128)(2,1)S(1)}, bf16[4,512,128]{2,1,0:T(8,128)(2,1)S(1)}, u32[]{:S(2)}, u32[]{:S(2)}) collective-permute-start(bf16[4,512,128]{2,1,0:T(8,128)(2,1)S(1)} %copy.143.kv_ref), channel_id=1, source_target_pairs={{0,4},{4,8},{8,12},{12,16},{16,20},{20,24},{24,28},{28,32},{32,36}... | collective-permute-start | bytes 1572872 | tf_op jit(solution)/shard_map/while/body/ppermute | solution.py:209
  100.8 1.9 copy-start
  100.8 12.6 %collective-permute-start = (bf16[4,512,128]{2,1,0:T(8,128)(2,1)S(1)}, bf16[4,512,128]{2,1,0:T(8,128)(2,1)S(1)}, u32[]{:S(2)}, u32[]{:S(2)}) collective-permute-start(bf16[4,512,128]{2,1,0:T(8,128)(2,1)S(1)} %copy.143.kv_ref), channel_id=1, source_target_pairs={{0,4},{4,8},{8,12},{12,16},{16,20},{20,24},{24,28},{28,32},{32,36}... | collective-permute-start | bytes 1572872 | tf_op jit(solution)/shard_map/while/body/ppermute | solution.py:209
  113.4 1.9 copy-start
  113.4 12.6 %collective-permute-start = (bf16[4,512,128]{2,1,0:T(8,128)(2,1)S(1)}, bf16[4,512,128]{2,1,0:T(8,128)(2,1)S(1)}, u32[]{:S(2)}, u32[]{:S(2)}) collective-permute-start(bf16[4,512,128]{2,1,0:T(8,128)(2,1)S(1)} %copy.143.kv_ref), channel_id=1, source_target_pairs={{0,4},{4,8},{8,12},{12,16},{16,20},{20,24},{24,28},{28,32},{32,36}... | collective-permute-start | bytes 1572872 | tf_op jit(solution)/shard_map/while/body/ppermute | solution.py:209
  126.1 1.9 copy-start
  126.1 12.6 %collective-permute-start = (bf16[4,512,128]{2,1,0:T(8,128)(2,1)S(1)}, bf16[4,512,128]{2,1,0:T(8,128)(2,1)S(1)}, u32[]{:S(2)}, u32[]{:S(2)}) collective-permute-start(bf16[4,512,128]{2,1,0:T(8,128)(2,1)S(1)} %copy.143.kv_ref), channel_id=1, source_target_pairs={{0,4},{4,8},{8,12},{12,16},{16,20},{20,24},{24,28},{28,32},{32,36}... | collective-permute-start | bytes 1572872 | tf_op jit(solution)/shard_map/while/body/ppermute | solution.py:209
  138.7 1.9 copy-start
  138.8 12.6 %collective-permute-start = (bf16[4,512,128]{2,1,0:T(8,128)(2,1)S(1)}, bf16[4,512,128]{2,1,0:T(8,128)(2,1)S(1)}, u32[]{:S(2)}, u32[]{:S(2)}) collective-permute-start(bf16[4,512,128]{2,1,0:T(8,128)(2,1)S(1)} %copy.143.kv_ref), channel_id=1, source_target_pairs={{0,4},{4,8},{8,12},{12,16},{16,20},{20,24},{24,28},{28,32},{32,36}... | collective-permute-start | bytes 1572872 | tf_op jit(solution)/shard_map/while/body/ppermute | solution.py:209
  151.4 1.9 copy-start.1
  151.4 12.6 %collective-permute-start.1 = (bf16[4,512,128]{2,1,0:T(8,128)(2,1)S(1)}, bf16[4,512,128]{2,1,0:T(8,128)(2,1)S(1)}, u32[]{:S(2)}, u32[]{:S(2)}) collective-permute-start(bf16[4,512,128]{2,1,0:T(8,128)(2,1)S(1)} %copy.152.kv_ref), channel_id=1, source_target_pairs={{0,4},{4,8},{8,12},{12,16},{16,20},{20,24},{24,28},{28,32},{32,36}... | collective-permute-start | bytes 1572872 | tf_op jit(solution)/shard_map/while/body/ppermute | solution.py:209
  164.1 1.9 copy-start.1
  164.1 12.6 %collective-permute-start.1 = (bf16[4,512,128]{2,1,0:T(8,128)(2,1)S(1)}, bf16[4,512,128]{2,1,0:T(8,128)(2,1)S(1)}, u32[]{:S(2)}, u32[]{:S(2)}) collective-permute-start(bf16[4,512,128]{2,1,0:T(8,128)(2,1)S(1)} %copy.152.kv_ref), channel_id=1, source_target_pairs={{0,4},{4,8},{8,12},{12,16},{16,20},{20,24},{24,28},{28,32},{32,36}... | collective-permute-start | bytes 1572872 | tf_op jit(solution)/shard_map/while/body/ppermute | solution.py:209
  176.7 1.9 copy-start.1
  176.7 12.6 %collective-permute-start.1 = (bf16[4,512,128]{2,1,0:T(8,128)(2,1)S(1)}, bf16[4,512,128]{2,1,0:T(8,128)(2,1)S(1)}, u32[]{:S(2)}, u32[]{:S(2)}) collective-permute-start(bf16[4,512,128]{2,1,0:T(8,128)(2,1)S(1)} %copy.152.kv_ref), channel_id=1, source_target_pairs={{0,4},{4,8},{8,12},{12,16},{16,20},{20,24},{24,28},{28,32},{32,36}... | collective-permute-start | bytes 1572872 | tf_op jit(solution)/shard_map/while/body/ppermute | solution.py:209
  189.4 1.9 copy-start.1
  189.4 12.6 %collective-permute-start.1 = (bf16[4,512,128]{2,1,0:T(8,128)(2,1)S(1)}, bf16[4,512,128]{2,1,0:T(8,128)(2,1)S(1)}, u32[]{:S(2)}, u32[]{:S(2)}) collective-permute-start(bf16[4,512,128]{2,1,0:T(8,128)(2,1)S(1)} %copy.152.kv_ref), channel_id=1, source_target_pairs={{0,4},{4,8},{8,12},{12,16},{16,20},{20,24},{24,28},{28,32},{32,36}... | collective-permute-start | bytes 1572872 | tf_op jit(solution)/shard_map/while/body/ppermute | solution.py:209
  202.0 1.9 copy-start.1
  202.1 12.6 %collective-permute-start.1 = (bf16[4,512,128]{2,1,0:T(8,128)(2,1)S(1)}, bf16[4,512,128]{2,1,0:T(8,128)(2,1)S(1)}, u32[]{:S(2)}, u32[]{:S(2)}) collective-permute-start(bf16[4,512,128]{2,1,0:T(8,128)(2,1)S(1)} %copy.152.kv_ref), channel_id=1, source_target_pairs={{0,4},{4,8},{8,12},{12,16},{16,20},{20,24},{24,28},{28,32},{32,36}... | collective-permute-start | bytes 1572872 | tf_op jit(solution)/shard_map/while/body/ppermute | solution.py:209
  214.7 1.9 copy-start.1
  214.7 12.6 %collective-permute-start.1 = (bf16[4,512,128]{2,1,0:T(8,128)(2,1)S(1)}, bf16[4,512,128]{2,1,0:T(8,128)(2,1)S(1)}, u32[]{:S(2)}, u32[]{:S(2)}) collective-permute-start(bf16[4,512,128]{2,1,0:T(8,128)(2,1)S(1)} %copy.152.kv_ref), channel_id=1, source_target_pairs={{0,4},{4,8},{8,12},{12,16},{16,20},{20,24},{24,28},{28,32},{32,36}... | collective-permute-start | bytes 1572872 | tf_op jit(solution)/shard_map/while/body/ppermute | solution.py:209
  227.4 6.4 %copy-start.1 = (bf16[4,512,128]{2,1,0:T(8,128)(2,1)}, bf16[4,512,128]{2,1,0:T(8,128)(2,1)S(1)}, u32[]{:S(2)}) copy-start(bf16[4,512,128]{2,1,0:T(8,128)(2,1)S(1)} %copy.152.kv_ref) | copy-start | bytes 1572868 | tf_op jit(solution)/shard_map/while
  227.4 12.6 %collective-permute-start.1 = (bf16[4,512,128]{2,1,0:T(8,128)(2,1)S(1)}, bf16[4,512,128]{2,1,0:T(8,128)(2,1)S(1)}, u32[]{:S(2)}, u32[]{:S(2)}) collective-permute-start(bf16[4,512,128]{2,1,0:T(8,128)(2,1)S(1)} %copy.152.kv_ref), channel_id=1, source_target_pairs={{0,4},{4,8},{8,12},{12,16},{16,20},{20,24},{24,28},{28,32},{32,36}... | collective-permute-start | bytes 1572872 | tf_op jit(solution)/shard_map/while/body/ppermute | solution.py:209
  240.0 4.3 %copy-start.1 = (bf16[4,512,128]{2,1,0:T(8,128)(2,1)}, bf16[4,512,128]{2,1,0:T(8,128)(2,1)S(1)}, u32[]{:S(2)}) copy-start(bf16[4,512,128]{2,1,0:T(8,128)(2,1)S(1)} %copy.152.kv_ref) | copy-start | bytes 1572868 | tf_op jit(solution)/shard_map/while
  240.0 12.6 %collective-permute-start.1 = (bf16[4,512,128]{2,1,0:T(8,128)(2,1)S(1)}, bf16[4,512,128]{2,1,0:T(8,128)(2,1)S(1)}, u32[]{:S(2)}, u32[]{:S(2)}) collective-permute-start(bf16[4,512,128]{2,1,0:T(8,128)(2,1)S(1)} %copy.152.kv_ref), channel_id=1, source_target_pairs={{0,4},{4,8},{8,12},{12,16},{16,20},{20,24},{24,28},{28,32},{32,36}... | collective-permute-start | bytes 1572872 | tf_op jit(solution)/shard_map/while/body/ppermute | solution.py:209
  252.7 2.2 copy-start.1
  252.7 12.6 %collective-permute-start.1 = (bf16[4,512,128]{2,1,0:T(8,128)(2,1)S(1)}, bf16[4,512,128]{2,1,0:T(8,128)(2,1)S(1)}, u32[]{:S(2)}, u32[]{:S(2)}) collective-permute-start(bf16[4,512,128]{2,1,0:T(8,128)(2,1)S(1)} %copy.152.kv_ref), channel_id=1, source_target_pairs={{0,4},{4,8},{8,12},{12,16},{16,20},{20,24},{24,28},{28,32},{32,36}... | collective-permute-start | bytes 1572872 | tf_op jit(solution)/shard_map/while/body/ppermute | solution.py:209
  269.1 16.7 %copy-start.13 = (s32[4]{0:T(128)S(1)}, s32[4]{0:T(128)}, u32[]{:S(2)}) copy-start(s32[4]{0:T(128)} %param.21) | copy-start | bytes 52
  269.2 17.5 %copy-start.3 = (bf16[512,4,2,64]{3,0,1,2:T(8,128)(2,1)S(1)}, bf16[512,4,2,64]{3,0,1,2:T(8,128)(2,1)}, u32[]{:S(2)}) copy-start(bf16[512,4,2,64]{3,0,1,2:T(8,128)(2,1)} %copy-done.2) | copy-start | bytes 1572868
  270.5 61.4 %all-to-all-start.1 = ((bf16[256,4,512]{2,0,1:T(8,128)(2,1)}), bf16[256,4,512]{2,0,1:T(8,128)(2,1)}, u32[]{:S(2)}, u32[]{:S(2)}) async-start(bf16[256,4,512]{2,0,1:T(8,128)(2,1)} %copy.118), calls=%async_computation.1 | async-start | bytes 2097152 | tf_op jit(solution)/shard_map/all_to_all | solution.py:239
  288.5 25.1 %collective-permute-start.6 = (bf16[512,256]{0,1:T(8,128)(2,1)S(1)}, bf16[512,256]{0,1:T(8,128)(2,1)S(1)}, u32[]{:S(2)}, u32[]{:S(2)}) collective-permute-start(bf16[512,256]{0,1:T(8,128)(2,1)S(1)} %bitcast.81), channel_id=1, source_target_pairs={{0,1},{1,2},{2,3},{3,0},{4,5},{5,6},{6,7},{7,4},{8,9},{9,10},{10,1... | collective-permute-start | bytes 786440 | tf_op jit(solution)/shard_map/ppermute | solution.py:106
  291.6 37.8 %collective-permute-start.7 = (bf16[512,256]{0,1:T(8,128)(2,1)S(1)}, bf16[512,256]{0,1:T(8,128)(2,1)S(1)}, u32[]{:S(2)}, u32[]{:S(2)}) collective-permute-start(bf16[512,256]{0,1:T(8,128)(2,1)S(1)} %bitcast.82), channel_id=1, source_target_pairs={{0,2},{1,3},{2,0},{3,1},{4,6},{5,7},{6,4},{7,5},{8,10},{9,11},{10,... | collective-permute-start | bytes 786440 | tf_op jit(solution)/shard_map/ppermute | solution.py:106
  293.0 36.4 %collective-permute-start.8 = (bf16[512,256]{0,1:T(8,128)(2,1)S(1)}, bf16[512,256]{0,1:T(8,128)(2,1)S(1)}, u32[]{:S(2)}, u32[]{:S(2)}) collective-permute-start(bf16[512,256]{0,1:T(8,128)(2,1)S(1)} %bitcast.83), channel_id=1, source_target_pairs={{0,3},{1,0},{2,1},{3,2},{4,7},{5,4},{6,5},{7,6},{8,11},{9,8},{10,9... | collective-permute-start | bytes 786440 | tf_op jit(solution)/shard_map/ppermute | solution.py:106
  329.4 0.7 copy-start.11
  330.1 1.8 copy-start.9
